TPU v7x, 128 devices: a whole 4x4x4 slice. The times are simulated.
128 devices in a mesh: dom: 8 (over y, core), seq: 16 (over x, z).
Axes of the slice: x: 4, y: 4, z: 4, core: 2. Of those that a mesh axis runs over, the one named last changes fastest.
Arguments:
- tokens_x: bfloat16 [32768, 4096], P(('dom', 'seq')), may hold values from -6 to 6
- gate_z: bfloat16 [32768, 4096], P(('dom', 'seq')), may hold values from -6 to 6
- in_b: bfloat16 [32768, 128], P(('dom', 'seq')), may hold values from -6 to 6
- in_c: bfloat16 [32768, 128], P(('dom', 'seq')), may hold values from -0.19921875 to 0.19921875
- log_decay: bfloat16 [32768, 64], P(('dom', 'seq')), may hold values from -1 to 0
- domain_ids: int32 [8, 16, 8], P('dom', 'seq'), may hold values from 0 to 7, each once within a row
- out_weight: bfloat16 [8, 4096, 4096], P('dom', None, 'seq'), may hold values from -0.09375 to 0.09375
- norm_gain: float32 [8, 4096], P('dom'), may hold values from 0.1 to 1.9
- skip_gain: float32 [8, 64], P('dom'), may hold values from 0.5 to 8
Outputs:
- mixed: bfloat16 [8, 4096, 4096], P('dom', 'seq')
Inputs may be any that keep to these rules, and one draw needn't show every extreme that they name: Each row of domain_ids names every domain once.
All inputs are finite; a program needn't handle non-finite values.
Results may differ from a plain program's by a relative error of at most 0.0056.
Values may be sent and summed in bfloat16 or wider, within the bound.
No kernel may reach another device: no remote copies, remote signals or barrier semaphores. Data moves between devices by JAX's collectives and lax.ppermute only.
A program may use at most 192 MiB of HBM per device.

v0:
```python
import jax
import jax.numpy as jnp
from jax import lax
from jax.sharding import PartitionSpec as P

SPAN = 256


def shifted(block, axis, distance):
    devices = range(lax.axis_size(axis))
    route = [(i - distance, i) for i in devices if i - distance in devices]
    return lax.ppermute(block, axis, route)


def per_device(
    tokens_x, gate_z, in_b, in_c, log_decay, domain_ids, out_weight, norm_gain, skip_gain
):
    groups = lax.axis_size("dom")
    rows = tokens_x.shape[0]
    seg_rows = rows // groups
    order = jnp.argsort(domain_ids.reshape(groups))

    def arrange(value_rows):
        return jnp.take(value_rows.reshape(groups, seg_rows, value_rows.shape[-1]), order, axis=0)

    received = (
        lax.all_to_all(arrange(tokens_x), "dom", split_axis=0, concat_axis=0, tiled=True),
        lax.all_to_all(arrange(gate_z), "dom", split_axis=0, concat_axis=0, tiled=True),
        lax.all_to_all(arrange(in_b), "dom", split_axis=0, concat_axis=0, tiled=True),
        lax.all_to_all(arrange(in_c), "dom", split_axis=0, concat_axis=0, tiled=True),
        lax.all_to_all(arrange(log_decay), "dom", split_axis=0, concat_axis=0, tiled=True),
    )
    xs, zs, bs, cs, ls = [piece.reshape(rows, piece.shape[-1]) for piece in received]
    heads = skip_gain.shape[-1]
    width = xs.shape[1]
    hsize = width // heads
    nstate = bs.shape[1]
    blocks = rows // SPAN
    xc = xs.reshape(blocks, SPAN, heads, hsize)
    bc = bs.reshape(blocks, SPAN, nstate)
    cc = cs.reshape(blocks, SPAN, nstate)
    cum = jnp.cumsum(ls.astype(jnp.float32).reshape(blocks, SPAN, heads), axis=1)
    scores = jnp.einsum("cin,cjn->cij", cc, bc, preferred_element_type=jnp.float32)
    cum_heads = jnp.transpose(cum, (0, 2, 1))
    diff = cum_heads[:, :, :, None] - cum_heads[:, :, None, :]
    positions = jnp.arange(SPAN)
    lower = positions[:, None] >= positions[None, :]
    decay = jnp.where(lower[None, None], jnp.exp(jnp.minimum(diff, 0.0)), 0.0)
    weights = (scores[:, None] * decay).astype(jnp.bfloat16)
    inner = jnp.einsum("chij,cjhp->cihp", weights, xc, preferred_element_type=jnp.float32)
    totals = cum[:, -1, :]
    decayed = (xc.astype(jnp.float32) * jnp.exp(totals[:, None, :] - cum)[..., None]).astype(
        jnp.bfloat16
    )
    block_state = jnp.einsum("cjhp,cjn->chpn", decayed, bc, preferred_element_type=jnp.float32)
    running = jnp.zeros((heads, hsize, nstate), jnp.float32)
    before = [running]
    running = jnp.exp(totals[0])[:, None, None] * running + block_state[0]
    local_end = running
    local_before = jnp.stack(before, axis=0)
    shard_decay = jnp.exp(jnp.sum(totals, axis=0))
    empty_state = jnp.zeros((heads, hsize, nstate), jnp.float32)

    def hop(step, incoming):
        return shifted(shard_decay[:, None, None] * incoming + local_end, "seq", 1)

    incoming = lax.fori_loop(0, lax.axis_size("seq") - 1, hop, empty_state)
    prefix = jnp.cumsum(totals, axis=0) - totals
    full_before = local_before + jnp.exp(prefix)[:, :, None, None] * incoming[None]
    carried = jnp.einsum(
        "cin,chpn->cihp", cc.astype(jnp.float32), full_before, precision=lax.Precision.HIGHEST
    )
    ys = (
        inner
        + jnp.exp(cum)[..., None] * carried
        + skip_gain[0][None, None, :, None] * xc.astype(jnp.float32)
    )
    gated = ys.reshape(rows, width) * jax.nn.silu(zs.astype(jnp.float32))
    normed = (
        gated
        * lax.rsqrt(jnp.mean(gated * gated, axis=-1, keepdims=True) + 1e-05)
        * norm_gain[0][None, :]
    ).astype(jnp.bfloat16)
    mixed = jnp.dot(
        normed,
        lax.all_gather(out_weight[0], "seq", axis=1, tiled=True),
        preferred_element_type=jnp.float32,
    ).astype(jnp.bfloat16)
    return mixed.reshape(1, rows, mixed.shape[-1])


def solution(mesh):
    in_specs = (
        P(("dom", "seq"), None),
        P(("dom", "seq"), None),
        P(("dom", "seq"), None),
        P(("dom", "seq"), None),
        P(("dom", "seq"), None),
        P("dom", "seq", None),
        P("dom", None, "seq"),
        P("dom", None),
        P("dom", None),
    )
    out_specs = P("dom", "seq", None)
    return jax.shard_map(
        per_device, mesh=mesh, in_specs=in_specs, out_specs=out_specs, check_vma=False
    )
```

profile of v0, /device:TPU:0, one launch (start us, length us, event | category | flops | bytes accessed | tf_op | source)
XLA Modules:
  0.0 981.8 jit_solution(3108809300649920440)
XLA Ops:
  11.2 4.6 all-to-all-start.3
  21.2 3.4 all-to-all-start.2
  26.6 3.8 gather_fusion.4
  30.4 4.7 all-to-all-start.1
  35.1 4.0 broadcast_select_fusion
  40.7 3.6 all-to-all-start
  46.8 24.7 %all-to-all-done = bf16[8,32,4096]{2,1,0:T(8,128)(2,1)S(1)} async-done(((bf16[8,32,4096]{2,1,0:T(8,128)(2,1)}), bf16[8,32,4096]{2,1,0:T(8,128)(2,1)S(1)}, u32[]{:S(2)}, u32[]{:S(2)}) %all-to-all-start) | async-done | bytes 2097184 | tf_op jit(solution)/shard_map/all_to_all | solution.py:27
  71.5 4.4 all-to-all-start.4
  76.1 4.6 mul.133
  80.7 8.1 mul.134
  89.0 4.3 multiply_convert_fusion.2
  93.3 6.9 convert_element_type.75
  100.2 5.5 reshape.286
  105.7 7.7 copy.34
  113.5 7.0 reshape.288
  120.5 7.8 copy.37
  128.3 5.5 reshape.269
  133.9 7.3 fusion.26
  141.1 14.2 %fusion.2 = f32[64,64,256]{2,1,0:T(8,128)} fusion(f32[64,256]{1,0:T(8,128)S(1)} %bitcast_add_fusion.1, f32[256,256]{1,0:T(8,128)S(1)} %fusion.32, pred[256,256]{1,0:T(8,128)(4,1)S(1)} %iota_compare_fusion, bf16[256,64,64]{2,1,0:T(8,128)(2,1)S(1)} %copy-done.3), kind=kOutput, calls=%fused_computation.9 | convolution fusion | flops 557842432 | bytes 6684672 | tf_op jit(solution)/shard_map/chij,cjhp->cihp/dot_general | solution.py:50
  156.9 780.1 %while.10 = (s32[]{:T(128)}, f32[64,64,128]{2,1,0:T(8,128)}, f32[64]{0:T(128)S(1)}, f32[64,64,128]{2,1,0:T(8,128)S(1)}, s32[]{:T(128)}) while((s32[]{:T(128)}, f32[64,64,128]{2,1,0:T(8,128)}, f32[64]{0:T(128)S(1)}, f32[64,64,128]{2,1,0:T(8,128)S(1)}, s32[]{:T(128)}) %tuple.26), condition=%wide.region_4.7_spmd, body=%wide.region_3.6_spmd.sunk | while | flops 1048578 | bytes 14680421 | solution.py:67
  156.9 3.2 multiply_add_fusion.2
  160.1 5.2 collective-permute-start
  165.3 89.8 %collective-permute-done = f32[64,64,128]{2,1,0:T(8,128)} collective-permute-done((f32[64,64,128]{2,1,0:T(8,128)}, f32[64,64,128]{2,1,0:T(8,128)}, u32[]{:S(2)}, u32[]{:S(2)}) %collective-permute-start) | collective-permute-done | bytes 2097184 | tf_op jit(solution)/shard_map/while/body/eval_jaxpr/ppermute | solution.py:12
  255.1 3.2 multiply_add_fusion.2
  258.2 5.7 collective-permute-start
  263.9 43.7 %collective-permute-done = f32[64,64,128]{2,1,0:T(8,128)} collective-permute-done((f32[64,64,128]{2,1,0:T(8,128)}, f32[64,64,128]{2,1,0:T(8,128)}, u32[]{:S(2)}, u32[]{:S(2)}) %collective-permute-start) | collective-permute-done | bytes 2097184 | tf_op jit(solution)/shard_map/while/body/eval_jaxpr/ppermute | solution.py:12
  307.6 3.2 multiply_add_fusion.2
  310.8 5.7 collective-permute-start
  316.5 42.8 %collective-permute-done = f32[64,64,128]{2,1,0:T(8,128)} collective-permute-done((f32[64,64,128]{2,1,0:T(8,128)}, f32[64,64,128]{2,1,0:T(8,128)}, u32[]{:S(2)}, u32[]{:S(2)}) %collective-permute-start) | collective-permute-done | bytes 2097184 | tf_op jit(solution)/shard_map/while/body/eval_jaxpr/ppermute | solution.py:12
  359.3 3.2 multiply_add_fusion.2
  362.5 5.7 collective-permute-start
  368.2 42.0 %collective-permute-done = f32[64,64,128]{2,1,0:T(8,128)} collective-permute-done((f32[64,64,128]{2,1,0:T(8,128)}, f32[64,64,128]{2,1,0:T(8,128)}, u32[]{:S(2)}, u32[]{:S(2)}) %collective-permute-start) | collective-permute-done | bytes 2097184 | tf_op jit(solution)/shard_map/while/body/eval_jaxpr/ppermute | solution.py:12
  410.2 3.2 multiply_add_fusion.2
  413.4 5.7 collective-permute-start
  419.1 41.1 %collective-permute-done = f32[64,64,128]{2,1,0:T(8,128)} collective-permute-done((f32[64,64,128]{2,1,0:T(8,128)}, f32[64,64,128]{2,1,0:T(8,128)}, u32[]{:S(2)}, u32[]{:S(2)}) %collective-permute-start) | collective-permute-done | bytes 2097184 | tf_op jit(solution)/shard_map/while/body/eval_jaxpr/ppermute | solution.py:12
  460.2 3.2 multiply_add_fusion.2
  463.4 7.0 collective-permute-start
  470.4 40.5 %collective-permute-done = f32[64,64,128]{2,1,0:T(8,128)} collective-permute-done((f32[64,64,128]{2,1,0:T(8,128)}, f32[64,64,128]{2,1,0:T(8,128)}, u32[]{:S(2)}, u32[]{:S(2)}) %collective-permute-start) | collective-permute-done | bytes 2097184 | tf_op jit(solution)/shard_map/while/body/eval_jaxpr/ppermute | solution.py:12
  510.9 3.2 multiply_add_fusion.2
  514.0 7.8 collective-permute-start
  521.8 39.6 %collective-permute-done = f32[64,64,128]{2,1,0:T(8,128)} collective-permute-done((f32[64,64,128]{2,1,0:T(8,128)}, f32[64,64,128]{2,1,0:T(8,128)}, u32[]{:S(2)}, u32[]{:S(2)}) %collective-permute-start) | collective-permute-done | bytes 2097184 | tf_op jit(solution)/shard_map/while/body/eval_jaxpr/ppermute | solution.py:12
  561.5 3.2 multiply_add_fusion.2
  564.6 7.8 collective-permute-start
  572.5 38.8 %collective-permute-done = f32[64,64,128]{2,1,0:T(8,128)} collective-permute-done((f32[64,64,128]{2,1,0:T(8,128)}, f32[64,64,128]{2,1,0:T(8,128)}, u32[]{:S(2)}, u32[]{:S(2)}) %collective-permute-start) | collective-permute-done | bytes 2097184 | tf_op jit(solution)/shard_map/while/body/eval_jaxpr/ppermute | solution.py:12
  614.4 7.8 collective-permute-start
  622.2 37.9 %collective-permute-done = f32[64,64,128]{2,1,0:T(8,128)} collective-permute-done((f32[64,64,128]{2,1,0:T(8,128)}, f32[64,64,128]{2,1,0:T(8,128)}, u32[]{:S(2)}, u32[]{:S(2)}) %collective-permute-start) | collective-permute-done | bytes 2097184 | tf_op jit(solution)/shard_map/while/body/eval_jaxpr/ppermute | solution.py:12
  663.3 7.8 collective-permute-start
  671.1 37.1 %collective-permute-done = f32[64,64,128]{2,1,0:T(8,128)} collective-permute-done((f32[64,64,128]{2,1,0:T(8,128)}, f32[64,64,128]{2,1,0:T(8,128)}, u32[]{:S(2)}, u32[]{:S(2)}) %collective-permute-start) | collective-permute-done | bytes 2097184 | tf_op jit(solution)/shard_map/while/body/eval_jaxpr/ppermute | solution.py:12
  711.3 7.8 collective-permute-start
  719.1 36.2 %collective-permute-done = f32[64,64,128]{2,1,0:T(8,128)} collective-permute-done((f32[64,64,128]{2,1,0:T(8,128)}, f32[64,64,128]{2,1,0:T(8,128)}, u32[]{:S(2)}, u32[]{:S(2)}) %collective-permute-start) | collective-permute-done | bytes 2097184 | tf_op jit(solution)/shard_map/while/body/eval_jaxpr/ppermute | solution.py:12
  755.3 3.2 multiply_add_fusion.2
  758.5 7.8 collective-permute-start
  766.3 35.3 %collective-permute-done = f32[64,64,128]{2,1,0:T(8,128)} collective-permute-done((f32[64,64,128]{2,1,0:T(8,128)}, f32[64,64,128]{2,1,0:T(8,128)}, u32[]{:S(2)}, u32[]{:S(2)}) %collective-permute-start) | collective-permute-done | bytes 2097184 | tf_op jit(solution)/shard_map/while/body/eval_jaxpr/ppermute | solution.py:12
  804.8 7.8 collective-permute-start
  812.6 34.8 %collective-permute-done = f32[64,64,128]{2,1,0:T(8,128)} collective-permute-done((f32[64,64,128]{2,1,0:T(8,128)}, f32[64,64,128]{2,1,0:T(8,128)}, u32[]{:S(2)}, u32[]{:S(2)}) %collective-permute-start) | collective-permute-done | bytes 2097184 | tf_op jit(solution)/shard_map/while/body/eval_jaxpr/ppermute | solution.py:12
  847.4 3.2 multiply_add_fusion.2
  850.6 7.8 collective-permute-start
  858.4 34.8 %collective-permute-done = f32[64,64,128]{2,1,0:T(8,128)} collective-permute-done((f32[64,64,128]{2,1,0:T(8,128)}, f32[64,64,128]{2,1,0:T(8,128)}, u32[]{:S(2)}, u32[]{:S(2)}) %collective-permute-start) | collective-permute-done | bytes 2097184 | tf_op jit(solution)/shard_map/while/body/eval_jaxpr/ppermute | solution.py:12
  896.4 7.8 collective-permute-start
  904.2 32.8 %collective-permute-done = f32[64,64,128]{2,1,0:T(8,128)} collective-permute-done((f32[64,64,128]{2,1,0:T(8,128)}, f32[64,64,128]{2,1,0:T(8,128)}, u32[]{:S(2)}, u32[]{:S(2)}) %collective-permute-start) | collective-permute-done | bytes 2097184 | tf_op jit(solution)/shard_map/while/body/eval_jaxpr/ppermute | solution.py:12
  937.0 9.6 multiply_reduce_fusion
  946.6 5.7 copy.35
  952.3 5.8 fusion.24
  958.2 16.8 %fusion.11 = bf16[1,256,4096]{2,1,0:T(8,128)(2,1)} fusion(bf16[256,4096]{1,0:T(8,128)(2,1)} %fusion.24, bf16[1,4096,4096]{2,1,0:T(8,128)(2,1)} %all-gather.3.cloned.1.call-done), kind=kOutput, calls=%fused_computation.16 | convolution fusion | flops 8590983168 | bytes 37748736 | tf_op jit(solution)/shard_map/dot_general | solution.py:84
  (59 shorter events, 34.0 us)
Async XLA Ops:
  6.5 18.0 %copy-start = (bf16[256,4096]{1,0:T(8,128)(2,1)S(1)}, bf16[256,4096]{1,0:T(8,128)(2,1)}, u32[]{:S(2)}) copy-start(bf16[256,4096]{1,0:T(8,128)(2,1)} %param.15) | copy-start | bytes 6291460
  6.5 951.7 %all-gather.3.cloned.1.call-start = ((), (), s32[]{:S(2)}) async-start(), calls=%async_computation.5 | async-start | bytes 35651584 | tf_op jit(solution)/shard_map/all_gather | solution.py:86
  11.2 10.0 %all-to-all-start.3 = ((bf16[8,2,1024]{2,1,0:T(2,128)(2,1)}), bf16[8,2,1024]{2,1,0:T(2,128)(2,1)S(1)}, u32[]{:S(2)}, u32[]{:S(2)}) async-start(bf16[8,2,1024]{2,1,0:T(2,128)(2,1)} %reshape.348), calls=%async_computation.3 | async-start | bytes 65536 | tf_op jit(solution)/shard_map/all_to_all | solution.py:31
  21.2 9.2 all-to-all-start.2
  26.6 8.5 copy-start.2
  30.4 10.3 %all-to-all-start.1 = ((bf16[8,32,128]{2,1,0:T(8,128)(2,1)}), bf16[8,32,128]{2,1,0:T(8,128)(2,1)S(1)}, u32[]{:S(2)}, u32[]{:S(2)}) async-start(bf16[8,32,128]{2,1,0:T(8,128)(2,1)} %get-tuple-element.48), calls=%async_computation.1 | async-start | bytes 131072 | tf_op jit(solution)/shard_map/all_to_all | solution.py:30
  40.7 30.7 %all-to-all-start = ((bf16[8,32,4096]{2,1,0:T(8,128)(2,1)}), bf16[8,32,4096]{2,1,0:T(8,128)(2,1)S(1)}, u32[]{:S(2)}, u32[]{:S(2)}) async-start(bf16[8,32,4096]{2,1,0:T(8,128)(2,1)} %get-tuple-element.43), calls=%async_computation | async-start | bytes 4194304 | tf_op jit(solution)/shard_map/all_to_all | solution.py:27
  71.5 42.0 %all-to-all-start.4 = ((bf16[8,32,4096]{2,1,0:T(8,128)(2,1)}), bf16[8,32,4096]{2,1,0:T(8,128)(2,1)}, u32[]{:S(2)}, u32[]{:S(2)}) async-start(bf16[8,32,4096]{2,1,0:T(8,128)(2,1)} %get-tuple-element.42), calls=%async_computation.4 | async-start | bytes 4194304 | tf_op jit(solution)/shard_map/all_to_all | solution.py:28
  133.9 7.3 copy-start.3
  156.9 780.1 %copy-start.5 = (f32[1,64]{1,0:T(1,128)S(1)}, f32[1,64]{1,0:T(1,128)}, u32[]{:S(2)}) copy-start(f32[1,64]{1,0:T(1,128)} %param.23) | copy-start | bytes 772
  160.1 95.0 %collective-permute-start = (f32[64,64,128]{2,1,0:T(8,128)}, f32[64,64,128]{2,1,0:T(8,128)}, u32[]{:S(2)}, u32[]{:S(2)}) collective-permute-start(f32[64,64,128]{2,1,0:T(8,128)} %multiply_add_fusion.2), channel_id=1, source_target_pairs={{0,1},{1,2},{2,3},{3,4},{4,5},{5,6},{6,7},{7,8},{8,9},{9,10},{10,1... | collective-permute-start | bytes 6291464 | tf_op jit(solution)/shard_map/while/body/eval_jaxpr/ppermute | solution.py:12
  258.2 49.4 %collective-permute-start = (f32[64,64,128]{2,1,0:T(8,128)}, f32[64,64,128]{2,1,0:T(8,128)}, u32[]{:S(2)}, u32[]{:S(2)}) collective-permute-start(f32[64,64,128]{2,1,0:T(8,128)} %multiply_add_fusion.2), channel_id=1, source_target_pairs={{0,1},{1,2},{2,3},{3,4},{4,5},{5,6},{6,7},{7,8},{8,9},{9,10},{10,1... | collective-permute-start | bytes 6291464 | tf_op jit(solution)/shard_map/while/body/eval_jaxpr/ppermute | solution.py:12
  310.8 48.5 %collective-permute-start = (f32[64,64,128]{2,1,0:T(8,128)}, f32[64,64,128]{2,1,0:T(8,128)}, u32[]{:S(2)}, u32[]{:S(2)}) collective-permute-start(f32[64,64,128]{2,1,0:T(8,128)} %multiply_add_fusion.2), channel_id=1, source_target_pairs={{0,1},{1,2},{2,3},{3,4},{4,5},{5,6},{6,7},{7,8},{8,9},{9,10},{10,1... | collective-permute-start | bytes 6291464 | tf_op jit(solution)/shard_map/while/body/eval_jaxpr/ppermute | solution.py:12
  362.5 47.7 %collective-permute-start = (f32[64,64,128]{2,1,0:T(8,128)}, f32[64,64,128]{2,1,0:T(8,128)}, u32[]{:S(2)}, u32[]{:S(2)}) collective-permute-start(f32[64,64,128]{2,1,0:T(8,128)} %multiply_add_fusion.2), channel_id=1, source_target_pairs={{0,1},{1,2},{2,3},{3,4},{4,5},{5,6},{6,7},{7,8},{8,9},{9,10},{10,1... | collective-permute-start | bytes 6291464 | tf_op jit(solution)/shard_map/while/body/eval_jaxpr/ppermute | solution.py:12
  413.4 46.8 %collective-permute-start = (f32[64,64,128]{2,1,0:T(8,128)}, f32[64,64,128]{2,1,0:T(8,128)}, u32[]{:S(2)}, u32[]{:S(2)}) collective-permute-start(f32[64,64,128]{2,1,0:T(8,128)} %multiply_add_fusion.2), channel_id=1, source_target_pairs={{0,1},{1,2},{2,3},{3,4},{4,5},{5,6},{6,7},{7,8},{8,9},{9,10},{10,1... | collective-permute-start | bytes 6291464 | tf_op jit(solution)/shard_map/while/body/eval_jaxpr/ppermute | solution.py:12
  463.4 47.5 %collective-permute-start = (f32[64,64,128]{2,1,0:T(8,128)}, f32[64,64,128]{2,1,0:T(8,128)}, u32[]{:S(2)}, u32[]{:S(2)}) collective-permute-start(f32[64,64,128]{2,1,0:T(8,128)} %multiply_add_fusion.2), channel_id=1, source_target_pairs={{0,1},{1,2},{2,3},{3,4},{4,5},{5,6},{6,7},{7,8},{8,9},{9,10},{10,1... | collective-permute-start | bytes 6291464 | tf_op jit(solution)/shard_map/while/body/eval_jaxpr/ppermute | solution.py:12
  514.0 47.4 %collective-permute-start = (f32[64,64,128]{2,1,0:T(8,128)}, f32[64,64,128]{2,1,0:T(8,128)}, u32[]{:S(2)}, u32[]{:S(2)}) collective-permute-start(f32[64,64,128]{2,1,0:T(8,128)} %multiply_add_fusion.2), channel_id=1, source_target_pairs={{0,1},{1,2},{2,3},{3,4},{4,5},{5,6},{6,7},{7,8},{8,9},{9,10},{10,1... | collective-permute-start | bytes 6291464 | tf_op jit(solution)/shard_map/while/body/eval_jaxpr/ppermute | solution.py:12
  564.6 46.6 %collective-permute-start = (f32[64,64,128]{2,1,0:T(8,128)}, f32[64,64,128]{2,1,0:T(8,128)}, u32[]{:S(2)}, u32[]{:S(2)}) collective-permute-start(f32[64,64,128]{2,1,0:T(8,128)} %multiply_add_fusion.2), channel_id=1, source_target_pairs={{0,1},{1,2},{2,3},{3,4},{4,5},{5,6},{6,7},{7,8},{8,9},{9,10},{10,1... | collective-permute-start | bytes 6291464 | tf_op jit(solution)/shard_map/while/body/eval_jaxpr/ppermute | solution.py:12
  614.4 45.7 %collective-permute-start = (f32[64,64,128]{2,1,0:T(8,128)}, f32[64,64,128]{2,1,0:T(8,128)}, u32[]{:S(2)}, u32[]{:S(2)}) collective-permute-start(f32[64,64,128]{2,1,0:T(8,128)} %multiply_add_fusion.2), channel_id=1, source_target_pairs={{0,1},{1,2},{2,3},{3,4},{4,5},{5,6},{6,7},{7,8},{8,9},{9,10},{10,1... | collective-permute-start | bytes 6291464 | tf_op jit(solution)/shard_map/while/body/eval_jaxpr/ppermute | solution.py:12
  663.3 44.9 %collective-permute-start = (f32[64,64,128]{2,1,0:T(8,128)}, f32[64,64,128]{2,1,0:T(8,128)}, u32[]{:S(2)}, u32[]{:S(2)}) collective-permute-start(f32[64,64,128]{2,1,0:T(8,128)} %multiply_add_fusion.2), channel_id=1, source_target_pairs={{0,1},{1,2},{2,3},{3,4},{4,5},{5,6},{6,7},{7,8},{8,9},{9,10},{10,1... | collective-permute-start | bytes 6291464 | tf_op jit(solution)/shard_map/while/body/eval_jaxpr/ppermute | solution.py:12
  711.3 44.0 %collective-permute-start = (f32[64,64,128]{2,1,0:T(8,128)}, f32[64,64,128]{2,1,0:T(8,128)}, u32[]{:S(2)}, u32[]{:S(2)}) collective-permute-start(f32[64,64,128]{2,1,0:T(8,128)} %multiply_add_fusion.2), channel_id=1, source_target_pairs={{0,1},{1,2},{2,3},{3,4},{4,5},{5,6},{6,7},{7,8},{8,9},{9,10},{10,1... | collective-permute-start | bytes 6291464 | tf_op jit(solution)/shard_map/while/body/eval_jaxpr/ppermute | solution.py:12
  758.5 43.1 %collective-permute-start = (f32[64,64,128]{2,1,0:T(8,128)}, f32[64,64,128]{2,1,0:T(8,128)}, u32[]{:S(2)}, u32[]{:S(2)}) collective-permute-start(f32[64,64,128]{2,1,0:T(8,128)} %multiply_add_fusion.2), channel_id=1, source_target_pairs={{0,1},{1,2},{2,3},{3,4},{4,5},{5,6},{6,7},{7,8},{8,9},{9,10},{10,1... | collective-permute-start | bytes 6291464 | tf_op jit(solution)/shard_map/while/body/eval_jaxpr/ppermute | solution.py:12
  804.8 42.6 %collective-permute-start = (f32[64,64,128]{2,1,0:T(8,128)}, f32[64,64,128]{2,1,0:T(8,128)}, u32[]{:S(2)}, u32[]{:S(2)}) collective-permute-start(f32[64,64,128]{2,1,0:T(8,128)} %multiply_add_fusion.2), channel_id=1, source_target_pairs={{0,1},{1,2},{2,3},{3,4},{4,5},{5,6},{6,7},{7,8},{8,9},{9,10},{10,1... | collective-permute-start | bytes 6291464 | tf_op jit(solution)/shard_map/while/body/eval_jaxpr/ppermute | solution.py:12
  850.6 42.6 %collective-permute-start = (f32[64,64,128]{2,1,0:T(8,128)}, f32[64,64,128]{2,1,0:T(8,128)}, u32[]{:S(2)}, u32[]{:S(2)}) collective-permute-start(f32[64,64,128]{2,1,0:T(8,128)} %multiply_add_fusion.2), channel_id=1, source_target_pairs={{0,1},{1,2},{2,3},{3,4},{4,5},{5,6},{6,7},{7,8},{8,9},{9,10},{10,1... | collective-permute-start | bytes 6291464 | tf_op jit(solution)/shard_map/while/body/eval_jaxpr/ppermute | solution.py:12
  896.4 40.6 %collective-permute-start = (f32[64,64,128]{2,1,0:T(8,128)}, f32[64,64,128]{2,1,0:T(8,128)}, u32[]{:S(2)}, u32[]{:S(2)}) collective-permute-start(f32[64,64,128]{2,1,0:T(8,128)} %multiply_add_fusion.2), channel_id=1, source_target_pairs={{0,1},{1,2},{2,3},{3,4},{4,5},{5,6},{6,7},{7,8},{8,9},{9,10},{10,1... | collective-permute-start | bytes 6291464 | tf_op jit(solution)/shard_map/while/body/eval_jaxpr/ppermute | solution.py:12
  946.6 5.7 copy-start.4
  958.2 16.8 %copy-start.1 = (bf16[256,4096]{1,0:T(8,128)(2,1)S(1)}, bf16[256,4096]{1,0:T(8,128)(2,1)}, u32[]{:S(2)}) copy-start(bf16[256,4096]{1,0:T(8,128)(2,1)} %param.15) | copy-start | bytes 6291460
Sparse Core Ops, SparseCore 0:
  9.4 248.4 all-gather.2
where the time goes:
time: 996 us; the launch traced here: 982 us
  waiting for transfers between devices  656 us (66%)
  starting transfers between devices  126 us (13%)
  local copies, waits for them, and re-layouts  73.1 us (7%)
  other arithmetic  65.2 us (7%)
  matrix products  48 us (5%)
  between operations  13.6 us (1%)
    ppermute x15, waiting for transfers between devices, shifted(): return lax.ppermute(block, axis, route)  627 us
    ppermute x15, starting transfers between devices, shifted(): return lax.ppermute(block, axis, route)  105 us
    add x15, other arithmetic, hop(): return shifted(shard_decay[:, None, None] * incoming + local_end, 'seq', 1)  47.6 us
    all_to_all x1, waiting for transfers between devices, per_device(): lax.all_to_all(arrange(tokens_x), 'dom', split_axis=0, concat_axis=0, til...  24.7 us
  transfers between devices with their start and end apart: 21, of which 18 were waited for; matrix products, arithmetic and copies ran while one was open for 17% of the time, Pallas kernels for 0%

commit v1 on v0

--- a/solution.py
+++ b/solution.py
@@ -59,12 +59,20 @@
     local_end = running
     local_before = jnp.stack(before, axis=0)
     shard_decay = jnp.exp(jnp.sum(totals, axis=0))
-    empty_state = jnp.zeros((heads, hsize, nstate), jnp.float32)
-
-    def hop(step, incoming):
-        return shifted(shard_decay[:, None, None] * incoming + local_end, "seq", 1)
-
-    incoming = lax.fori_loop(0, lax.axis_size("seq") - 1, hop, empty_state)
+    packed = jnp.concatenate(
+        [local_end, jnp.broadcast_to(shard_decay[None, :, None], (1, heads, nstate))], axis=0
+    )
+    packed = shifted(packed, "seq", 1)
+    distance = 1
+    while distance < lax.axis_size("seq"):
+        got = shifted(packed, "seq", distance)
+        scale = packed[heads:]
+        packed = jnp.concatenate(
+            [jnp.transpose(scale, (1, 0, 2))[:, :, :1] * got[:heads] + packed[:heads], scale * got[heads:]],
+            axis=0,
+        )
+        distance *= 2
+    incoming = packed[:heads]
     prefix = jnp.cumsum(totals, axis=0) - totals
     full_before = local_before + jnp.exp(prefix)[:, :, None, None] * incoming[None]
     carried = jnp.einsum(

time: 996 us -> 499 us (0.50)
  waiting for transfers between devices: 656 us -> 295 us
  starting transfers between devices: 126 us -> 42.6 us
  other arithmetic: 65.2 us -> 24.5 us
    ppermute x15 -> x5, waiting for transfers between devices: 627 us -> 284 us  [shifted(): return lax.ppermute(block, axis, route)]
    ppermute x15 -> x5, starting transfers between devices: 105 us -> 25.4 us  [shifted(): return lax.ppermute(block, axis, route)]
    add x15 -> x3, other arithmetic: 47.6 us -> 3.02 us  [per_device(): jnp.transpose(scale, (1, 0, 2))[:, :, :1] * got[:heads] + packed[:heads]]
    all_to_all x1, waiting for transfers between devices: 24.7 us -> 10 us  [per_device(): lax.all_to_all(arrange(tokens_x), 'dom', split_axis=0, concat_axis=0, til...]
  transfers between devices with their start and end apart: 21 -> 10, of which waited for: 18 -> 6; matrix products, arithmetic and copies ran while one was open for 17% -> 24% of each run, Pallas kernels for 0% -> 0%
where the time goes in v1:
time: 499 us; the launch traced here: 494 us
  waiting for transfers between devices  295 us (59%)
  local copies, waits for them, and re-layouts  70 us (14%)
  starting transfers between devices  42.6 us (9%)
  matrix products  39.2 us (8%)
  other arithmetic  24.5 us (5%)
  between operations  13.7 us (3%)
  blocking collectives  9.7 us (2%)
    ppermute x5, waiting for transfers between devices, shifted(): return lax.ppermute(block, axis, route)  284 us
    ppermute x5, starting transfers between devices, shifted(): return lax.ppermute(block, axis, route)  25.4 us
    dot_general x1, matrix products, per_device(): jnp.dot(normed, lax.all_gather(out_weight[0], 'seq', axis=1, tiled=True),...  16.9 us
    convert_element_type x2, local copies, waits for them, and re-layouts, per_device(): gated = ys.reshape(rows, width) * jax.nn.silu(zs.astype(jnp.float32))  14.7 us
    convert_element_type x2, local copies, waits for them, and re-layouts, per_device(): xc.astype(jnp.float32) * jnp.exp(totals[:, None, :] - cum)[..., None]  13.2 us
    mul x3, local copies, waits for them, and re-layouts, per_device(): xc.astype(jnp.float32) * jnp.exp(totals[:, None, :] - cum)[..., None]  12.7 us
    all_to_all x1, waiting for transfers between devices, per_device(): lax.all_to_all(arrange(tokens_x), 'dom', split_axis=0, concat_axis=0, til...  10 us
  transfers between devices with their start and end apart: 10, of which 6 were waited for; matrix products, arithmetic and copies ran while one was open for 24% of the time, Pallas kernels for 0%

profile of v1, /device:TPU:0, one launch (start us, length us, event | category | flops | bytes accessed | tf_op | source)
XLA Modules:
  0.0 494.3 jit_solution(289571919164735768)
XLA Ops:
  6.5 0.7 all-gather.3.cloned.1.call-update
  7.3 0.9 copy.26
  8.2 1.0 sort.17
  9.1 0.6 gather_fusion
  9.8 0.7 reshape.358
  10.5 4.6 all-to-all-start.3
  15.1 2.0 gather_fusion.1
  17.1 3.7 gather_fusion.4
  20.8 4.4 broadcast_select_fusion
  25.3 5.0 %all-to-all-start = ((bf16[8,32,4096]{2,1,0:T(8,128)(2,1)}), bf16[8,32,4096]{2,1,0:T(8,128)(2,1)S(1)}, u32[]{:S(2)}, u32[]{:S(2)}) async-start(bf16[8,32,4096]{2,1,0:T(8,128)(2,1)} %get-tuple-element.14), calls=%async_computation | async-start | bytes 4194304 | tf_op jit(solution)/shard_map/all_to_all | solution.py:27
  30.3 0.6 gather_fusion.2
  30.8 0.6 gather_fusion.3
  31.4 0.7 broadcast_select_fusion.2
  32.1 0.1 reshape.359
  32.3 0.6 reduce-window.6
  33.0 0.2 slice_reduce_fusion
  33.2 0.1 copy.30
  33.3 0.1 broadcast.128
  33.4 0.1 fusion.36
  33.6 0.9 slice_reduce_fusion.5
  34.5 0.2 subtract_exponential_fusion
  34.7 0.1 copy.41
  34.8 4.6 mul.174
  39.4 8.0 %mul.175 = f32[8,32,4096]{2,1,0:T(8,128)} reshape(f32[256,64,64]{2,1,0:T(8,128)} %mul.174) | data formatting | bytes 8388608 | tf_op jit(solution)/shard_map/mul | solution.py:52
  47.4 10.0 %all-to-all-done = bf16[8,32,4096]{2,1,0:T(8,128)(2,1)S(1)} async-done(((bf16[8,32,4096]{2,1,0:T(8,128)(2,1)}), bf16[8,32,4096]{2,1,0:T(8,128)(2,1)S(1)}, u32[]{:S(2)}, u32[]{:S(2)}) %all-to-all-start) | async-done | bytes 2097184 | tf_op jit(solution)/shard_map/all_to_all | solution.py:27
  57.4 3.4 all-to-all-start.2
  60.8 4.0 multiply_convert_fusion.2
  64.8 6.9 %convert_element_type.75 = bf16[256,64,64]{2,1,0:T(8,128)(2,1)} reshape(bf16[8,32,4096]{2,1,0:T(8,128)(2,1)} %multiply_convert_fusion.2) | data formatting | bytes 4194304 | tf_op jit(solution)/shard_map/convert_element_type | solution.py:52
  71.7 6.9 %fusion.30 = f32[64,64,128]{2,1,0:T(8,128)S(1)} fusion(bf16[256,128,1]{1,0,2:T(8,128)(2,1)S(1)} %bitcast.90, bf16[256,64,64]{2,1,0:T(8,128)(2,1)} %convert_element_type.75, f32[64]{0:T(128)S(1)} %get-tuple-element.16), kind=kOutput, calls=%fused_computation.47 | convolution fusion | flops 268959744 | bytes 4260096 | tf_op jit(solution)/shard_map/cjhp,cjn->chpn/dot_general | solution.py:55
  78.7 0.2 pad_maximum_fusion
  79.0 4.0 collective-permute-start
  83.0 92.1 %collective-permute-done = f32[65,64,128]{2,1,0:T(8,128)S(1)} collective-permute-done((f32[65,64,128]{2,1,0:T(8,128)S(1)}, f32[65,64,128]{2,1,0:T(8,128)S(1)}, u32[]{:S(2)}, u32[]{:S(2)}) %collective-permute-start) | collective-permute-done | bytes 2129952 | tf_op jit(solution)/shard_map/ppermute | solution.py:12
  175.1 4.5 collective-permute-start.1
  179.6 91.9 %collective-permute-done.1 = f32[65,64,128]{2,1,0:T(8,128)S(1)} collective-permute-done((f32[65,64,128]{2,1,0:T(8,128)S(1)}, f32[65,64,128]{2,1,0:T(8,128)S(1)}, u32[]{:S(2)}, u32[]{:S(2)}) %collective-permute-start.1) | collective-permute-done | bytes 2129952 | tf_op jit(solution)/shard_map/ppermute | solution.py:12
  271.4 0.1 slice_reduce_fusion.4
  271.5 0.3 slice_add_fusion
  271.8 0.1 pad_maximum_fusion.1
  272.0 4.8 collective-permute-start.2
  276.7 0.1 slice_reduce_fusion.3
  276.9 68.8 %collective-permute-done.2 = f32[65,64,128]{2,1,0:T(8,128)S(1)} collective-permute-done((f32[65,64,128]{2,1,0:T(8,128)S(1)}, f32[65,64,128]{2,1,0:T(8,128)S(1)}, u32[]{:S(2)}, u32[]{:S(2)}) %collective-permute-start.2) | collective-permute-done | bytes 2129952 | tf_op jit(solution)/shard_map/ppermute | solution.py:12
  345.6 0.3 fusion.29
  345.9 1.6 pad_maximum_fusion.2
  347.5 4.9 collective-permute-start.3
  352.4 9.7 %all_to_all.25 = bf16[8,32,128]{2,1,0:T(8,128)(2,1)S(1)} all-to-all(bf16[8,32,128]{2,1,0:T(8,128)(2,1)S(1)} %get-tuple-element.19), channel_id=1, replica_groups=mesh['dom'=8,'seq'=16] {'dom'}, dimensions={0} | all-to-all | bytes 131072 | tf_op jit(solution)/shard_map/all_to_all | solution.py:30
  362.1 4.4 all-to-all-start.4
  366.5 0.1 slice_reduce_fusion.1
  366.6 30.1 %collective-permute-done.3 = f32[65,64,128]{2,1,0:T(8,128)} collective-permute-done((f32[65,64,128]{2,1,0:T(8,128)}, f32[65,64,128]{2,1,0:T(8,128)}, u32[]{:S(2)}, u32[]{:S(2)}) %collective-permute-start.3) | collective-permute-done | bytes 2129952 | tf_op jit(solution)/shard_map/ppermute | solution.py:12
  396.7 0.8 slice_multiply_fusion.4
  397.5 2.5 fusion.28
  400.0 1.6 pad_maximum_fusion.3
  401.6 7.2 %collective-permute-start.4 = (f32[65,64,128]{2,1,0:T(8,128)}, f32[65,64,128]{2,1,0:T(8,128)}, u32[]{:S(2)}, u32[]{:S(2)}) collective-permute-start(f32[65,64,128]{2,1,0:T(8,128)} %pad_maximum_fusion.3), channel_id=1, source_target_pairs={{0,8},{1,9},{2,10},{3,11},{4,12},{5,13},{6,14},{7,15},{16,24},{17,... | collective-permute-start | bytes 6389768 | tf_op jit(solution)/shard_map/ppermute | solution.py:12
  409.0 0.2 fusion.37
  409.2 5.5 %reshape.292 = f32[1,256,64,64]{3,2,1,0:T(8,128)} reshape(bf16[8,32,4096]{2,1,0:T(8,128)(2,1)S(1)} %all-to-all-done) | data formatting | bytes 6291456 | tf_op jit(solution)/shard_map/convert_element_type | solution.py:52
  414.7 7.7 %copy.35 = f32[1,256,64,64]{1,3,2,0:T(8,128)} copy(f32[1,256,64,64]{3,2,1,0:T(8,128)} %reshape.292) | data formatting | bytes 8388608 | tf_op jit(solution)/shard_map/convert_element_type | solution.py:52
  422.4 7.0 %reshape.294 = f32[1,256,64,64]{3,2,1,0:T(8,128)} reshape(bf16[8,32,4096]{2,1,0:T(8,128)(2,1)} %all-to-all-done.4) | data formatting | bytes 6291456 | tf_op jit(solution)/shard_map/convert_element_type | solution.py:86
  429.4 7.8 %copy.38 = f32[1,256,64,64]{1,3,2,0:T(8,128)} copy(f32[1,256,64,64]{3,2,1,0:T(8,128)} %reshape.294) | data formatting | bytes 8388608 | tf_op jit(solution)/shard_map/convert_element_type | solution.py:86
  437.1 5.5 %reshape.275 = bf16[256,64,64]{2,1,0:T(8,128)(2,1)} reshape(bf16[8,32,4096]{2,1,0:T(8,128)(2,1)S(1)} %all-to-all-done) | data formatting | bytes 4194304 | tf_op jit(solution)/shard_map/reshape.27
  442.7 8.5 %fusion.2 = f32[64,64,256]{2,1,0:T(8,128)S(1)} fusion(f32[64,256]{1,0:T(8,128)S(1)} %bitcast_add_fusion.1, f32[256,256]{1,0:T(8,128)S(1)} %fusion.37, pred[256,256]{1,0:T(8,128)(4,1)S(1)} %iota_compare_fusion, bf16[256,64,64]{2,1,0:T(8,128)(2,1)} %reshape.275), kind=kOutput, calls=%fused_computation.8 | convolution fusion | flops 557842432 | bytes 6684672 | tf_op jit(solution)/shard_map/chij,cjhp->cihp/dot_general | solution.py:50
  451.2 0.1 slice_reduce_fusion.2
  451.3 1.0 collective-permute-done.4
  452.3 6.7 %multiply_reduce_fusion = (f32[256]{0:T(256)S(1)}, f32[1,256,64,64]{1,3,2,0:T(8,128)}) fusion(f32[1,256,64,64]{1,3,2,0:T(8,128)S(1)} %copy-done.7, f32[1,256,64,64]{1,3,2,0:T(8,128)S(1)} %copy-done.6, f32[64]{0:T(128)S(1)} %bitcast.111, bf16[256,128,1]{1,0,2:T(8,128)(2,1)S(1)} %bitcast.103, f32[64,64,128]{2,1,0:T(8,128)S(1)} %copy-done.4, ...), kind=kOutput, calls=%fused_computation.29 | convolution fusion | flops 1623719680 | bytes 21104384 | tf_op jit(solution)/shard_map/cin,chpn->cihp/dot_general | solution.py:78
  459.0 5.7 %copy.36 = f32[256,4096]{1,0:T(8,128)} copy(f32[256,4096]{0,1:T(8,128)} %bitcast.88) | data formatting | bytes 8388608 | tf_op jit(solution)/shard_map/reshape | solution.py:86
  464.7 5.8 %fusion.24 = bf16[256,4096]{1,0:T(8,128)(2,1)} fusion(f32[256,4096]{1,0:T(8,128)} %copy.36, f32[4096]{0:T(1024)S(1)} %bitcast.108, f32[256]{0:T(256)S(1)} %add_rsqrt_fusion, bf16[8,32,4096]{2,1,0:T(8,128)(2,1)} %all-to-all-done.4), kind=kLoop, calls=%fused_computation.31 | loop fusion | flops 9437184 | bytes 8406016 | tf_op jit(solution)/shard_map/convert_element_type | solution.py:91
  470.5 16.9 %fusion.11 = bf16[1,256,4096]{2,1,0:T(8,128)(2,1)} fusion(bf16[256,4096]{1,0:T(8,128)(2,1)} %fusion.24, bf16[1,4096,4096]{2,1,0:T(8,128)(2,1)} %all-gather.3.cloned.1.call-done), kind=kOutput, calls=%fused_computation.15 | convolution fusion | flops 8590983168 | bytes 37748736 | tf_op jit(solution)/shard_map/dot_general | solution.py:92
  (50 shorter events, 0.5 us)
Async XLA Ops:
  6.5 8.6 %copy-start = (bf16[256,4096]{1,0:T(8,128)(2,1)S(1)}, bf16[256,4096]{1,0:T(8,128)(2,1)}, u32[]{:S(2)}) copy-start(bf16[256,4096]{1,0:T(8,128)(2,1)} %param.13) | copy-start | bytes 6291460
  6.5 1.6 copy-start.11
  6.5 464.0 %all-gather.3.cloned.1.call-start = ((), (), s32[]{:S(2)}) async-start(), calls=%async_computation.5 | async-start | bytes 35651584 | tf_op jit(solution)/shard_map/all_gather | solution.py:94
  10.5 14.8 %all-to-all-start.3 = ((bf16[8,2,1024]{2,1,0:T(2,128)(2,1)}), bf16[8,2,1024]{2,1,0:T(2,128)(2,1)S(1)}, u32[]{:S(2)}, u32[]{:S(2)}) async-start(bf16[8,2,1024]{2,1,0:T(2,128)(2,1)} %reshape.358), calls=%async_computation.3 | async-start | bytes 65536 | tf_op jit(solution)/shard_map/all_to_all | solution.py:31
  17.1 3.7 copy-start.5
  25.3 5.0 %copy-start.8 = (bf16[256,128]{1,0:T(8,128)(2,1)S(1)}, bf16[256,128]{1,0:T(8,128)(2,1)}, u32[]{:S(2)}) copy-start(bf16[256,128]{1,0:T(8,128)(2,1)} %param.16) | copy-start | bytes 196612
  25.3 5.5 %copy-start.9 = (bf16[256,128]{1,0:T(8,128)(2,1)S(1)}, bf16[256,128]{1,0:T(8,128)(2,1)}, u32[]{:S(2)}) copy-start(bf16[256,128]{1,0:T(8,128)(2,1)} %param.15) | copy-start | bytes 196612
  25.3 32.1 %all-to-all-start = ((bf16[8,32,4096]{2,1,0:T(8,128)(2,1)}), bf16[8,32,4096]{2,1,0:T(8,128)(2,1)S(1)}, u32[]{:S(2)}, u32[]{:S(2)}) async-start(bf16[8,32,4096]{2,1,0:T(8,128)(2,1)} %get-tuple-element.14), calls=%async_computation | async-start | bytes 4194304 | tf_op jit(solution)/shard_map/all_to_all | solution.py:27
  57.4 14.3 %all-to-all-start.2 = ((bf16[8,32,128]{2,1,0:T(8,128)(2,1)}), bf16[8,32,128]{2,1,0:T(8,128)(2,1)S(1)}, u32[]{:S(2)}, u32[]{:S(2)}) async-start(bf16[8,32,128]{2,1,0:T(8,128)(2,1)} %get-tuple-element.18), calls=%async_computation.2 | async-start | bytes 131072 | tf_op jit(solution)/shard_map/all_to_all | solution.py:29
  79.0 96.1 %collective-permute-start = (f32[65,64,128]{2,1,0:T(8,128)S(1)}, f32[65,64,128]{2,1,0:T(8,128)S(1)}, u32[]{:S(2)}, u32[]{:S(2)}) collective-permute-start(f32[65,64,128]{2,1,0:T(8,128)S(1)} %pad_maximum_fusion), channel_id=1, source_target_pairs={{0,1},{1,2},{2,3},{3,4},{4,5},{5,6},{6,7},{7,8},{8,9},{9,10},{10,1... | collective-permute-start | bytes 6389768 | tf_op jit(solution)/shard_map/ppermute | solution.py:12
  175.1 96.4 %collective-permute-start.1 = (f32[65,64,128]{2,1,0:T(8,128)S(1)}, f32[65,64,128]{2,1,0:T(8,128)S(1)}, u32[]{:S(2)}, u32[]{:S(2)}) collective-permute-start(f32[65,64,128]{2,1,0:T(8,128)S(1)} %collective-permute-done), channel_id=1, source_target_pairs={{0,1},{1,2},{2,3},{3,4},{4,5},{5,6},{6,7},{7,8},{8,9},{9,10},{10,1... | collective-permute-start | bytes 6389768 | tf_op jit(solution)/shard_map/ppermute | solution.py:12
  272.0 73.6 %collective-permute-start.2 = (f32[65,64,128]{2,1,0:T(8,128)S(1)}, f32[65,64,128]{2,1,0:T(8,128)S(1)}, u32[]{:S(2)}, u32[]{:S(2)}) collective-permute-start(f32[65,64,128]{2,1,0:T(8,128)S(1)} %pad_maximum_fusion.1), channel_id=1, source_target_pairs={{0,2},{1,3},{2,4},{3,5},{4,6},{5,7},{6,8},{7,9},{8,10},{9,11},{10,... | collective-permute-start | bytes 6389768 | tf_op jit(solution)/shard_map/ppermute | solution.py:12
  345.9 6.5 %copy-start.2 = (f32[64,64,128]{2,1,0:T(8,128)}, f32[64,64,128]{2,1,0:T(8,128)S(1)}, u32[]{:S(2)}) copy-start(f32[64,64,128]{2,1,0:T(8,128)S(1)} %fusion.29) | copy-start | bytes 6291460
  347.5 49.2 %collective-permute-start.3 = (f32[65,64,128]{2,1,0:T(8,128)}, f32[65,64,128]{2,1,0:T(8,128)}, u32[]{:S(2)}, u32[]{:S(2)}) collective-permute-start(f32[65,64,128]{2,1,0:T(8,128)} %pad_maximum_fusion.2), channel_id=1, source_target_pairs={{0,4},{1,5},{2,6},{3,7},{4,8},{5,9},{6,10},{7,11},{8,12},{9,13},{1... | collective-permute-start | bytes 6389768 | tf_op jit(solution)/shard_map/ppermute | solution.py:12
  362.1 60.3 %all-to-all-start.4 = ((bf16[8,32,4096]{2,1,0:T(8,128)(2,1)}), bf16[8,32,4096]{2,1,0:T(8,128)(2,1)}, u32[]{:S(2)}, u32[]{:S(2)}) async-start(bf16[8,32,4096]{2,1,0:T(8,128)(2,1)} %get-tuple-element.13), calls=%async_computation.4 | async-start | bytes 4194304 | tf_op jit(solution)/shard_map/all_to_all | solution.py:28
  400.0 8.9 %copy-start.3 = (f32[64,64,128]{2,1,0:T(8,128)}, f32[64,64,128]{2,1,0:T(8,128)S(1)}, u32[]{:S(2)}) copy-start(f32[64,64,128]{2,1,0:T(8,128)S(1)} %fusion.28) | copy-start | bytes 6291460
  401.6 50.7 %collective-permute-start.4 = (f32[65,64,128]{2,1,0:T(8,128)}, f32[65,64,128]{2,1,0:T(8,128)}, u32[]{:S(2)}, u32[]{:S(2)}) collective-permute-start(f32[65,64,128]{2,1,0:T(8,128)} %pad_maximum_fusion.3), channel_id=1, source_target_pairs={{0,8},{1,9},{2,10},{3,11},{4,12},{5,13},{6,14},{7,15},{16,24},{17,... | collective-permute-start | bytes 6389768 | tf_op jit(solution)/shard_map/ppermute | solution.py:12
  442.7 9.6 %copy-start.4 = (f32[64,64,128]{2,1,0:T(8,128)S(1)}, f32[64,64,128]{2,1,0:T(8,128)}, u32[]{:S(2)}) copy-start(f32[64,64,128]{2,1,0:T(8,128)} %copy-done.3) | copy-start | bytes 6291460
  442.7 9.6 %copy-start.6 = (f32[1,256,64,64]{1,3,2,0:T(8,128)S(1)}, f32[1,256,64,64]{1,3,2,0:T(8,128)}, u32[]{:S(2)}) copy-start(f32[1,256,64,64]{1,3,2,0:T(8,128)} %copy.35) | copy-start | bytes 12582916
  442.7 9.6 %copy-start.7 = (f32[1,256,64,64]{1,3,2,0:T(8,128)S(1)}, f32[1,256,64,64]{1,3,2,0:T(8,128)}, u32[]{:S(2)}) copy-start(f32[1,256,64,64]{1,3,2,0:T(8,128)} %copy.38) | copy-start | bytes 12582916
  442.7 9.6 %copy-start.12 = (f32[1,64]{1,0:T(1,128)S(1)}, f32[1,64]{1,0:T(1,128)}, u32[]{:S(2)}) copy-start(f32[1,64]{1,0:T(1,128)} %param.21) | copy-start | bytes 772
  459.0 5.7 %copy-start.10 = (f32[1,4096]{1,0:T(1,128)S(1)}, f32[1,4096]{1,0:T(1,128)}, u32[]{:S(2)}) copy-start(f32[1,4096]{1,0:T(1,128)} %param.20) | copy-start | bytes 49156
  470.5 16.9 %copy-start.1 = (bf16[256,4096]{1,0:T(8,128)(2,1)S(1)}, bf16[256,4096]{1,0:T(8,128)(2,1)}, u32[]{:S(2)}) copy-start(bf16[256,4096]{1,0:T(8,128)(2,1)} %param.13) | copy-start | bytes 6291460
Sparse Core Ops, SparseCore 0:
  9.4 314.6 all-gather.2

commit v2 on v0

v2 whole, which is shorter than its diff:
```python
import jax
import jax.numpy as jnp
from jax import lax
from jax.sharding import PartitionSpec as P

SPAN = 256


def per_device(
    tokens_x, gate_z, in_b, in_c, log_decay, domain_ids, out_weight, norm_gain, skip_gain
):
    groups = lax.axis_size("dom")
    shards = lax.axis_size("seq")
    rows = tokens_x.shape[0]
    seg_rows = rows // groups
    width = tokens_x.shape[1]
    nstate = in_b.shape[1]
    heads = skip_gain.shape[-1]
    hsize = width // heads
    order = jnp.argsort(domain_ids.reshape(groups))

    pad = (-log_decay.shape[1]) % 128
    packed = jnp.concatenate(
        [tokens_x, gate_z, in_b, in_c, log_decay, jnp.zeros((rows, pad), log_decay.dtype)], axis=1
    )
    packed = jnp.take(packed.reshape(groups, seg_rows, packed.shape[-1]), order, axis=0)
    packed = lax.all_to_all(packed, "dom", split_axis=0, concat_axis=0, tiled=True)
    packed = packed.reshape(rows, packed.shape[-1])
    xs = packed[:, :width]
    zs = packed[:, width : 2 * width]
    bs = packed[:, 2 * width : 2 * width + nstate]
    cs = packed[:, 2 * width + nstate : 2 * width + 2 * nstate]
    ls = packed[:, 2 * width + 2 * nstate : 2 * width + 2 * nstate + heads]

    local = width // shards
    lheads = heads // shards
    xbc = jnp.concatenate(
        [
            jnp.transpose(xs.reshape(rows, shards, local), (1, 0, 2)),
            jnp.broadcast_to(bs[None], (shards, rows, nstate)),
            jnp.broadcast_to(cs[None], (shards, rows, nstate)),
        ],
        axis=2,
    )
    xbc = lax.all_to_all(xbc, "seq", split_axis=0, concat_axis=0, tiled=True)
    lsh = jnp.transpose(ls.reshape(rows, shards, lheads), (1, 0, 2))
    lsh = lax.all_to_all(lsh, "seq", split_axis=0, concat_axis=0, tiled=True)

    blocks = shards * rows // SPAN
    xc = xbc[:, :, :local].reshape(blocks, SPAN, lheads, hsize)
    bc = xbc[:, :, local : local + nstate].reshape(blocks, SPAN, nstate)
    cc = xbc[:, :, local + nstate :].reshape(blocks, SPAN, nstate)
    cum = jnp.cumsum(lsh.astype(jnp.float32).reshape(blocks, SPAN, lheads), axis=1)
    scores = jnp.einsum("cin,cjn->cij", cc, bc, preferred_element_type=jnp.float32)
    cum_heads = jnp.transpose(cum, (0, 2, 1))
    diff = cum_heads[:, :, :, None] - cum_heads[:, :, None, :]
    positions = jnp.arange(SPAN)
    lower = positions[:, None] >= positions[None, :]
    decay = jnp.where(lower[None, None], jnp.exp(jnp.minimum(diff, 0.0)), 0.0)
    weights = (scores[:, None] * decay).astype(jnp.bfloat16)
    inner = jnp.einsum("chij,cjhp->cihp", weights, xc, preferred_element_type=jnp.float32)
    totals = cum[:, -1, :]
    decayed = (xc.astype(jnp.float32) * jnp.exp(totals[:, None, :] - cum)[..., None]).astype(
        jnp.bfloat16
    )
    block_state = jnp.einsum("cjhp,cjn->chpn", decayed, bc, preferred_element_type=jnp.float32)

    idx = jnp.arange(blocks)
    between = (idx[None, :, None] < idx[None, None, :]) & (idx[None, None, :] < idx[:, None, None])
    gaps = jnp.einsum(
        "kji,ih->hkj", between.astype(jnp.float32), totals, precision=lax.Precision.HIGHEST
    )
    earlier = idx[None, :] < idx[:, None]
    carry = jnp.where(earlier[None], jnp.exp(jnp.minimum(gaps, 0.0)), 0.0)
    before = jnp.einsum("hkj,jhpn->khpn", carry, block_state, precision=lax.Precision.HIGHEST)
    carried = jnp.einsum(
        "cin,chpn->cihp", cc.astype(jnp.float32), before, precision=lax.Precision.HIGHEST
    )
    skip = lax.dynamic_slice_in_dim(skip_gain[0], lax.axis_index("seq") * lheads, lheads)
    ys = (
        inner
        + jnp.exp(cum)[..., None] * carried
        + skip[None, None, :, None] * xc.astype(jnp.float32)
    )

    ys = lax.all_to_all(
        ys.reshape(shards, rows, local), "seq", split_axis=0, concat_axis=0, tiled=True
    )
    ys = jnp.transpose(ys, (1, 0, 2)).reshape(rows, width)
    gated = ys * jax.nn.silu(zs.astype(jnp.float32))
    normed = (
        gated
        * lax.rsqrt(jnp.mean(gated * gated, axis=-1, keepdims=True) + 1e-05)
        * norm_gain[0][None, :]
    ).astype(jnp.bfloat16)
    mixed = jnp.dot(
        normed,
        lax.all_gather(out_weight[0], "seq", axis=1, tiled=True),
        preferred_element_type=jnp.float32,
    ).astype(jnp.bfloat16)
    return mixed.reshape(1, rows, mixed.shape[-1])


def solution(mesh):
    in_specs = (
        P(("dom", "seq"), None),
        P(("dom", "seq"), None),
        P(("dom", "seq"), None),
        P(("dom", "seq"), None),
        P(("dom", "seq"), None),
        P("dom", "seq", None),
        P("dom", None, "seq"),
        P("dom", None),
        P("dom", None),
    )
    out_specs = P("dom", "seq", None)
    return jax.shard_map(
        per_device, mesh=mesh, in_specs=in_specs, out_specs=out_specs, check_vma=False
    )
```

time: 996 us -> 352 us (0.35); the launches traced: 982 us -> 351 us
  waiting for transfers between devices: 656 us -> 79.5 us
  blocking collectives: 0 us -> 158 us
  starting transfers between devices: 126 us -> 15.2 us
  other arithmetic: 65.2 us -> 13.8 us
  local copies, waits for them, and re-layouts: 73.1 us -> 34.8 us
  matrix products: 48 us -> 36 us
    ppermute x15 -> x0, waiting for transfers between devices: 627 us -> none  [shifted(): return lax.ppermute(block, axis, route)]
    all_to_all x0 -> x2, blocking collectives: none -> 158 us  [the longest x1 102 us: per_device(): lax.all_to_all(ys.reshape(shards, rows, local), 'seq', split_axis=0, conc...]
    ppermute x15 -> x0, starting transfers between devices: 105 us -> none  [shifted(): return lax.ppermute(block, axis, route)]
    all_to_all x5 -> x2, waiting for transfers between devices: 28.1 us -> 78.7 us  [the longest x1 78.7 us: per_device(): xbc = lax.all_to_all(xbc, 'seq', split_axis=0, concat_axis=0, tiled=True)]
    add x15 -> x0, other arithmetic: 47.6 us -> none  [hop(): return shifted(shard_decay[:, None, None] * incoming + local_end, 'seq', 1)]
    convert_element_type x5 -> x0, local copies, waits for them, and re-layouts: 35 us -> none  [the longest x2 14.8 us: per_device(): gated = ys.reshape(rows, width) * jax.nn.silu(zs.astype(jnp.float32))]
    mul x3 -> x1, local copies, waits for them, and re-layouts: 12.8 us -> 0.07 us  [per_device(): skip[None, None, :, None] * xc.astype(jnp.float32)]
    convert_element_type x2 -> x0, other arithmetic: 10.1 us -> none  [the longest x1 5.84 us: per_device(): normed = (gated * lax.rsqrt(jnp.mean(gated * gated, axis=-1, keepdims=Tru...]
  transfers between devices with their start and end apart: 21 -> 3, of which waited for: 18 -> 1; matrix products, arithmetic and copies ran while one was open for 17% -> 18% of each run, Pallas kernels for 0% -> 0%
where the time goes in v2:
time: 352 us; the launch traced here: 351 us
  blocking collectives  158 us (45%)
  waiting for transfers between devices  79.5 us (23%)
  matrix products  36 us (10%)
  local copies, waits for them, and re-layouts  34.8 us (10%)
  starting transfers between devices  15.2 us (4%)
  other arithmetic  13.8 us (4%)
  between operations  13.7 us (4%)
    all_to_all x1, blocking collectives, per_device(): lax.all_to_all(ys.reshape(shards, rows, local), 'seq', split_axis=0, conc...  102 us
    all_to_all x1, waiting for transfers between devices, per_device(): xbc = lax.all_to_all(xbc, 'seq', split_axis=0, concat_axis=0, tiled=True)  78.7 us
    all_to_all x1, blocking collectives, per_device(): lax.all_to_all(packed, 'dom', split_axis=0, concat_axis=0, tiled=True)  56.1 us
    dot_general x1, matrix products, per_device(): jnp.dot(normed, lax.all_gather(out_weight[0], 'seq', axis=1, tiled=True),...  18.7 us
    concatenate x1, local copies, waits for them, and re-layouts, per_device(): jnp.concatenate([tokens_x, gate_z, in_b, in_c, log_decay, jnp.zeros((rows...  8.35 us
    all_to_all x1, starting transfers between devices, per_device(): lsh = lax.all_to_all(lsh, 'seq', split_axis=0, concat_axis=0, tiled=True)  7.92 us
    all_to_all x1, starting transfers between devices, per_device(): xbc = lax.all_to_all(xbc, 'seq', split_axis=0, concat_axis=0, tiled=True)  7.27 us
  transfers between devices with their start and end apart: 3, of which 1 were waited for; matrix products, arithmetic and copies ran while one was open for 18% of the time, Pallas kernels for 0%

profile of v2, /device:TPU:0, one launch (start us, length us, event | category | flops | bytes accessed | tf_op | source)
XLA Modules:
  0.0 351.0 jit_solution(319460345717523173)
XLA Ops:
  6.5 0.0 copy-start
  6.5 0.0 all-gather.3.cloned.1.call-start
  6.5 0.7 all-gather.3.cloned.1.call-update
  7.3 0.9 copy.46
  8.1 1.6 sort.17
  9.8 8.3 %concatenate.6 = bf16[256,8576]{1,0:T(8,128)(2,1)} concatenate(bf16[256,4096]{1,0:T(8,128)(2,1)} %param.9, bf16[256,4096]{1,0:T(8,128)(2,1)} %param.10, bf16[256,128]{1,0:T(8,128)(2,1)} %param.11, bf16[256,128]{1,0:T(8,128)(2,1)} %param.12, bf16[256,64]{1,0:T(8,128)(2,1)S(1)} %copy.46, bf16[256,64]{1,0:T(8,128)(2,1)S(1)} %broadcast_in_dim.35), dimensions={1} | concatenate | bytes 8781824 | tf_op jit(solution)/shard_map/concatenate | solution.py:23
  18.1 5.5 %gather_fusion = bf16[8,32,8576]{2,1,0:T(8,128)(2,1)} fusion(bf16[8,32,8576]{2,1,0:T(8,128)(2,1)} %bitcast.71, s32[1024]{0:T(1024)S(1)} %pad_clamp_fusion), kind=kCustom, calls=%fused_computation | custom fusion | bytes 8781856 | tf_op jit(solution)/shard_map/jit(_take)/gather | solution.py:26
  23.7 3.1 broadcast_select_fusion
  26.7 56.1 %all_to_all.20 = bf16[8,32,8576]{2,1,0:T(8,128)(2,1)S(1)} all-to-all(bf16[8,32,8576]{2,1,0:T(8,128)(2,1)S(1)} %broadcast_select_fusion), channel_id=1, replica_groups=mesh['dom'=8,'seq'=16] {'dom'}, dimensions={0} | all-to-all | bytes 8781824 | tf_op jit(solution)/shard_map/all_to_all | solution.py:27
  82.9 0.0 copy-start.2
  82.9 2.1 copy-done.2
  85.0 0.2 slice.46
  85.2 0.1 copy.50
  85.3 0.6 reshape.138
  85.9 7.9 %all-to-all-start.2 = ((bf16[16,256,4]{1,2,0:T(4,128)(2,1)}), bf16[16,256,4]{1,2,0:T(4,128)(2,1)S(1)}, u32[]{:S(2)}, u32[]{:S(2)}) async-start(bf16[16,256,4]{1,2,0:T(4,128)(2,1)} %bitcast.6), calls=%async_computation.2 | async-start | bytes 65536 | tf_op jit(solution)/shard_map/all_to_all | solution.py:47
  93.9 2.5 copy.47
  96.3 2.8 copy.48
  99.2 0.9 fusion.50
  100.1 0.2 broadcast_in_dim.38
  100.3 0.2 broadcast_in_dim.39
  100.5 2.2 pad_maximum_fusion
  102.7 0.0 all-to-all-done.2
  102.7 7.3 %all-to-all-start.1 = ((bf16[16,256,512]{2,1,0:T(8,128)(2,1)}), bf16[16,256,512]{2,1,0:T(8,128)(2,1)}, u32[]{:S(2)}, u32[]{:S(2)}) async-start(bf16[16,256,512]{2,1,0:T(8,128)(2,1)} %pad_maximum_fusion), calls=%async_computation.1 | async-start | bytes 8388608 | tf_op jit(solution)/shard_map/all_to_all | solution.py:45
  110.0 0.0 copy-done
  110.0 0.1 dynamic-slice_bitcast_fusion
  110.1 0.1 reshape.159
  110.2 2.3 reduce-window.6
  112.5 0.2 slice_reduce_fusion
  112.7 0.1 copy_bitcast_fusion
  112.8 0.2 slice_reduce_fusion.1
  112.9 0.1 bitcast_exponential_fusion
  113.2 0.6 fusion.34
  113.8 78.7 %all-to-all-done.1 = bf16[16,256,512]{2,1,0:T(8,128)(2,1)} async-done(((bf16[16,256,512]{2,1,0:T(8,128)(2,1)}), bf16[16,256,512]{2,1,0:T(8,128)(2,1)}, u32[]{:S(2)}, u32[]{:S(2)}) %all-to-all-start.1) | async-done | bytes 4194336 | tf_op jit(solution)/shard_map/all_to_all | solution.py:45
  192.5 1.7 slice.49
  194.2 2.4 copy.49
  196.6 2.6 fusion.20
  199.2 3.1 fusion.29
  202.3 2.3 fusion.38
  204.6 0.0 copy-start.3
  204.6 3.7 %fusion.22 = f32[16,256,4,64]{1,3,2,0:T(8,128)S(1)} fusion(f32[16,4,64,128]{3,0,2,1:T(8,128)S(1)} %fusion.29, bf16[16,256,512]{2,1,0:T(8,128)(2,1)} %all-to-all-done.1), kind=kOutput, calls=%fused_computation.28 | convolution fusion | flops 1610612736 | bytes 7340032 | tf_op jit(solution)/shard_map/cin,chpn->cihp/dot_general | solution.py:76
  208.3 0.0 copy-done.3
  208.3 5.1 %fusion.15 = f32[16,256,4,64]{1,3,2,0:T(8,128)S(1)} fusion(bf16[16,256,4,64]{1,3,2,0:T(8,128)(2,1)S(1)} %bitcast.75, f32[16,256,4,64]{1,3,2,0:T(8,128)S(1)} %fusion.22, f32[16,4,256]{2,1,0:T(4,128)S(1)} %copy.54, f32[16,256,256]{2,1,0:T(8,128)S(1)} %fusion.38, pred[256,256]{1,0:T(8,128)(4,1)S(1)} %iota_compare_fusion, f32[4]{0:T(128)S(1)} %dynamic-slice_bitcast_fusion, ...), kind=kOutput, calls=%fused_computation.18 | convolution fusion | flops 563085312 | bytes 14876688 | tf_op jit(solution)/shard_map/chij,cjhp->cihp/dot_general | solution.py:61
  213.4 101.9 %all_to_all.21 = f32[16,256,256]{1,2,0:T(8,128)} all-to-all(f32[16,256,256]{1,2,0:T(8,128)S(1)} %bitcast.77), channel_id=1, replica_groups=mesh['dom'=8,'seq'=16] {'seq'}, dimensions={0} | all-to-all | bytes 8388608 | tf_op jit(solution)/shard_map/all_to_all | solution.py:86
  315.3 5.7 %copy.69 = f32[256,4096]{1,0:T(8,128)} copy(f32[256,4096]{0,1:T(8,128)} %bitcast.72) | data formatting | bytes 8388608 | tf_op jit(solution)/shard_map/reshape | solution.py:89
  321.0 0.0 copy-start.4
  321.0 4.4 %multiply_reduce_fusion = f32[256]{0:T(256)S(1)} fusion(f32[256,4096]{1,0:T(8,128)} %copy.69, bf16[256,8576]{1,0:T(8,128)(2,1)} %bitcast.69), kind=kLoop, calls=%fused_computation.26 | loop fusion | flops 8388352 | bytes 6292480 | tf_op jit(solution)/shard_map/reduce_sum | solution.py:93
  325.4 0.0 all-gather.3.cloned.1.call-done
  325.4 0.0 copy-done.4
  325.4 0.0 copy-start.1
  325.5 18.7 %fusion.11 = bf16[1,256,4096]{2,1,0:T(8,128)(2,1)} fusion(bf16[1,4096,4096]{2,1,0:T(8,128)(2,1)} %all-gather.3.cloned.1.call-done, f32[4096]{0:T(1024)S(1)} %bitcast.78, f32[256]{0:T(256)S(1)} %add_rsqrt_fusion, f32[256,4096]{1,0:T(8,128)} %copy.69, bf16[256,8576]{1,0:T(8,128)(2,1)} %bitcast.70), kind=kOutput, calls=%fused_computation.15 | convolution fusion | flops 8600420352 | bytes 41960448 | tf_op jit(solution)/shard_map/dot_general | solution.py:96
  344.2 0.0 copy-done.1
  (16 shorter events, 0.2 us)
Async XLA Ops:
  6.5 103.4 %copy-start = (f32[1,64]{1,0:T(1,128)S(1)}, f32[1,64]{1,0:T(1,128)}, u32[]{:S(2)}) copy-start(f32[1,64]{1,0:T(1,128)} %param.17) | copy-start | bytes 772
  6.5 318.9 %all-gather.3.cloned.1.call-start = ((), (), s32[]{:S(2)}) async-start(), calls=%async_computation.4 | async-start | bytes 35651584 | tf_op jit(solution)/shard_map/all_gather | solution.py:98
  82.9 2.1 copy-start.2
  85.9 16.7 %all-to-all-start.2 = ((bf16[16,256,4]{1,2,0:T(4,128)(2,1)}), bf16[16,256,4]{1,2,0:T(4,128)(2,1)S(1)}, u32[]{:S(2)}, u32[]{:S(2)}) async-start(bf16[16,256,4]{1,2,0:T(4,128)(2,1)} %bitcast.6), calls=%async_computation.2 | async-start | bytes 65536 | tf_op jit(solution)/shard_map/all_to_all | solution.py:47
  102.7 89.8 %all-to-all-start.1 = ((bf16[16,256,512]{2,1,0:T(8,128)(2,1)}), bf16[16,256,512]{2,1,0:T(8,128)(2,1)}, u32[]{:S(2)}, u32[]{:S(2)}) async-start(bf16[16,256,512]{2,1,0:T(8,128)(2,1)} %pad_maximum_fusion), calls=%async_computation.1 | async-start | bytes 8388608 | tf_op jit(solution)/shard_map/all_to_all | solution.py:45
  204.6 3.8 %copy-start.3 = (bf16[16,256,256]{1,2,0:T(8,128)(2,1)S(1)}, bf16[16,256,256]{1,2,0:T(8,128)(2,1)}, u32[]{:S(2)}) copy-start(bf16[16,256,256]{1,2,0:T(8,128)(2,1)} %copy.49) | copy-start | bytes 6291460
  321.0 4.4 %copy-start.4 = (f32[1,4096]{1,0:T(1,128)S(1)}, f32[1,4096]{1,0:T(1,128)}, u32[]{:S(2)}) copy-start(f32[1,4096]{1,0:T(1,128)} %param.16) | copy-start | bytes 49156
  325.4 18.7 %copy-start.1 = (f32[1,64]{1,0:T(1,128)S(1)}, f32[1,64]{1,0:T(1,128)}, u32[]{:S(2)}) copy-start(f32[1,64]{1,0:T(1,128)} %param.17) | copy-start | bytes 772
Sparse Core Ops, SparseCore 0:
  9.4 305.2 all-gather.2

commit v3 on v2

--- a/solution.py
+++ b/solution.py
@@ -19,18 +19,21 @@
     hsize = width // heads
     order = jnp.argsort(domain_ids.reshape(groups))
 
+    def arrange(value_rows):
+        return jnp.take(value_rows.reshape(groups, seg_rows, value_rows.shape[-1]), order, axis=0)
+
     pad = (-log_decay.shape[1]) % 128
     packed = jnp.concatenate(
-        [tokens_x, gate_z, in_b, in_c, log_decay, jnp.zeros((rows, pad), log_decay.dtype)], axis=1
+        [tokens_x, in_b, in_c, log_decay, jnp.zeros((rows, pad), log_decay.dtype)], axis=1
     )
-    packed = jnp.take(packed.reshape(groups, seg_rows, packed.shape[-1]), order, axis=0)
-    packed = lax.all_to_all(packed, "dom", split_axis=0, concat_axis=0, tiled=True)
+    packed = lax.all_to_all(arrange(packed), "dom", split_axis=0, concat_axis=0, tiled=True)
     packed = packed.reshape(rows, packed.shape[-1])
+    zs = lax.all_to_all(arrange(gate_z), "dom", split_axis=0, concat_axis=0, tiled=True)
+    zs = zs.reshape(rows, width)
     xs = packed[:, :width]
-    zs = packed[:, width : 2 * width]
-    bs = packed[:, 2 * width : 2 * width + nstate]
-    cs = packed[:, 2 * width + nstate : 2 * width + 2 * nstate]
-    ls = packed[:, 2 * width + 2 * nstate : 2 * width + 2 * nstate + heads]
+    bs = packed[:, width : width + nstate]
+    cs = packed[:, width + nstate : width + 2 * nstate]
+    ls = packed[:, width + 2 * nstate : width + 2 * nstate + heads]
 
     local = width // shards
     lheads = heads // shards
@@ -93,11 +96,14 @@
         * lax.rsqrt(jnp.mean(gated * gated, axis=-1, keepdims=True) + 1e-05)
         * norm_gain[0][None, :]
     ).astype(jnp.bfloat16)
-    mixed = jnp.dot(
-        normed,
-        lax.all_gather(out_weight[0], "seq", axis=1, tiled=True),
-        preferred_element_type=jnp.float32,
-    ).astype(jnp.bfloat16)
+    pieces = 4
+    span = width // pieces
+    mixed = None
+    for k in range(pieces):
+        part = lax.all_gather(out_weight[0, k * span : (k + 1) * span], "seq", axis=1, tiled=True)
+        term = jnp.dot(normed[:, k * span : (k + 1) * span], part, preferred_element_type=jnp.float32)
+        mixed = term if mixed is None else mixed + term
+    mixed = mixed.astype(jnp.bfloat16)
     return mixed.reshape(1, rows, mixed.shape[-1])
 
 

time: 352 us -> 426 us (1.21)
  waiting for transfers between devices: 79.5 us -> 259 us
  blocking collectives: 158 us -> 0 us
  matrix products: 36 us -> 53.4 us
  starting transfers between devices: 15.2 us -> 30.5 us
  local copies, waits for them, and re-layouts: 34.8 us -> 46.6 us
  other arithmetic: 13.8 us -> 22.4 us
    all_to_all x2 -> x0, blocking collectives: 158 us -> none  [the longest x1 102 us: per_device(): lax.all_to_all(ys.reshape(shards, rows, local), 'seq', split_axis=0, conc...]
    all_to_all x0 -> x3, waiting for transfers between devices: none -> 107 us  [the longest x1 78.4 us: per_device(): lax.all_to_all(ys.reshape(shards, rows, local), 'seq', split_axis=0, conc...]
    all_gather x1 -> x4, waiting for transfers between devices: 0.02 us -> 97.9 us  [per_device(): lax.all_gather(out_weight[0, k * span:(k + 1) * span], 'seq', axis=1, til...]
    all_to_all x1, waiting for transfers between devices: 78.7 us -> 51.5 us  [per_device(): xbc = lax.all_to_all(xbc, 'seq', split_axis=0, concat_axis=0, tiled=True)]
    dot_general x1 -> x4, matrix products: 18.7 us -> 34.7 us  [per_device(): jnp.dot(normed[:, k * span:(k + 1) * span], part, preferred_element_type=...]
    all_to_all x0 -> x3, starting transfers between devices: none -> 15.3 us  [the longest x1 6.96 us: per_device(): lax.all_to_all(ys.reshape(shards, rows, local), 'seq', split_axis=0, conc...]
    slice x2, local copies, waits for them, and re-layouts: 2.7 us -> 7.21 us  [per_device(): xs = packed[:, :width]]
  transfers between devices with their start and end apart: 3 -> 9, of which waited for: 1 -> 5; matrix products, arithmetic and copies ran while one was open for 18% -> 26% of each run, Pallas kernels for 0% -> 0%
where the time goes in v3:
time: 426 us; the launch traced here: 425 us
  waiting for transfers between devices  259 us (61%)
  matrix products  53.4 us (13%)
  local copies, waits for them, and re-layouts  46.6 us (11%)
  starting transfers between devices  30.5 us (7%)
  other arithmetic  22.4 us (5%)
  between operations  13.4 us (3%)
    all_gather x4, waiting for transfers between devices, per_device(): lax.all_gather(out_weight[0, k * span:(k + 1) * span], 'seq', axis=1, til...  97.9 us
    all_to_all x1, waiting for transfers between devices, per_device(): lax.all_to_all(ys.reshape(shards, rows, local), 'seq', split_axis=0, conc...  78.4 us
    all_to_all x1, waiting for transfers between devices, per_device(): xbc = lax.all_to_all(xbc, 'seq', split_axis=0, concat_axis=0, tiled=True)  51.5 us
    dot_general x4, matrix products, per_device(): jnp.dot(normed[:, k * span:(k + 1) * span], part, preferred_element_type=...  34.7 us
    all_to_all x1, waiting for transfers between devices, per_device(): lax.all_to_all(arrange(packed), 'dom', split_axis=0, concat_axis=0, tiled...  28.8 us
  transfers between devices with their start and end apart: 9, of which 5 were waited for; matrix products, arithmetic and copies ran while one was open for 26% of the time, Pallas kernels for 0%

profile of v3, /device:TPU:0, one launch (start us, length us, event | category | flops | bytes accessed | tf_op | source)
XLA Modules:
  0.0 424.9 jit_solution(5697056754750081593)
XLA Ops:
  6.5 0.0 all-gather.11.cloned.1.call-start
  6.6 3.0 fusion.76
  9.6 0.0 all-gather.11.cloned.1.call-update
  9.6 0.0 all-gather.9.cloned.1.call-start
  9.7 0.7 all-gather.9.cloned.1.call-update
  10.4 0.0 all-gather.13.cloned.1.call-start
  10.4 0.7 all-gather.13.cloned.1.call-update
  11.1 0.1 copy.65
  11.3 1.0 sort.17
  12.3 4.5 %concatenate.6 = bf16[256,4480]{1,0:T(8,128)(2,1)} concatenate(bf16[256,4096]{1,0:T(8,128)(2,1)} %param.9, bf16[256,128]{1,0:T(8,128)(2,1)S(1)} %copy-done.5, bf16[256,128]{1,0:T(8,128)(2,1)S(1)} %copy-done.6, bf16[256,64]{1,0:T(8,128)(2,1)S(1)} %copy.65, bf16[256,64]{1,0:T(8,128)(2,1)S(1)} %broadcast_in_dim.45), dimensions={1} | concatenate | bytes 4587520 | tf_op jit(solution)/shard_map/concatenate | solution.py:26
  16.8 3.8 gather_fusion
  20.6 3.5 broadcast_select_fusion
  24.1 4.6 %all-to-all-start = ((bf16[8,32,4480]{2,1,0:T(8,128)(2,1)}), bf16[8,32,4480]{2,1,0:T(8,128)(2,1)}, u32[]{:S(2)}, u32[]{:S(2)}) async-start(bf16[8,32,4480]{2,1,0:T(8,128)(2,1)} %broadcast_select_fusion), calls=%async_computation | async-start | bytes 4587520 | tf_op jit(solution)/shard_map/all_to_all | solution.py:29
  28.7 0.0 all-gather.15.cloned.1.call-start
  28.8 0.5 all-gather.15.cloned.1.call-update
  29.3 28.8 %all-to-all-done = bf16[8,32,4480]{2,1,0:T(8,128)(2,1)} async-done(((bf16[8,32,4480]{2,1,0:T(8,128)(2,1)}), bf16[8,32,4480]{2,1,0:T(8,128)(2,1)}, u32[]{:S(2)}, u32[]{:S(2)}) %all-to-all-start) | async-done | bytes 2293792 | tf_op jit(solution)/shard_map/all_to_all | solution.py:29
  58.1 0.8 slice.82
  59.0 3.1 slice.76
  62.1 0.1 copy.69
  62.2 0.6 reshape.147
  62.8 7.9 %all-to-all-start.2 = ((bf16[16,256,4]{1,2,0:T(4,128)(2,1)}), bf16[16,256,4]{1,2,0:T(4,128)(2,1)S(1)}, u32[]{:S(2)}, u32[]{:S(2)}) async-start(bf16[16,256,4]{1,2,0:T(4,128)(2,1)} %bitcast.6), calls=%async_computation.2 | async-start | bytes 65536 | tf_op jit(solution)/shard_map/all_to_all | solution.py:50
  70.7 4.1 copy.66
  74.8 3.9 copy.67
  78.7 0.9 fusion.75
  79.6 0.2 broadcast_in_dim.52
  79.8 0.2 broadcast_in_dim.53
  80.0 3.5 pad_maximum_fusion
  83.5 0.0 all-to-all-done.2
  83.5 7.2 %all-to-all-start.1 = ((bf16[16,256,512]{2,1,0:T(8,128)(2,1)}), bf16[16,256,512]{2,1,0:T(8,128)(2,1)}, u32[]{:S(2)}, u32[]{:S(2)}) async-start(bf16[16,256,512]{2,1,0:T(8,128)(2,1)} %pad_maximum_fusion), calls=%async_computation.1 | async-start | bytes 8388608 | tf_op jit(solution)/shard_map/all_to_all | solution.py:48
  90.7 0.0 copy-start.10
  90.7 2.0 gather_fusion.1
  92.7 0.1 dynamic-slice_bitcast_fusion
  92.9 3.2 broadcast_select_fusion.1
  96.1 0.1 reshape.183
  96.2 2.3 reduce-window.6
  98.5 0.2 slice_reduce_fusion
  98.7 0.1 copy_bitcast_fusion
  98.8 0.2 slice_reduce_fusion.1
  98.9 0.1 bitcast_exponential_fusion
  99.2 0.6 fusion.56
  99.8 51.5 %all-to-all-done.1 = bf16[16,256,512]{2,1,0:T(8,128)(2,1)} async-done(((bf16[16,256,512]{2,1,0:T(8,128)(2,1)}), bf16[16,256,512]{2,1,0:T(8,128)(2,1)}, u32[]{:S(2)}, u32[]{:S(2)}) %all-to-all-start.1) | async-done | bytes 4194336 | tf_op jit(solution)/shard_map/all_to_all | solution.py:48
  151.3 3.8 all-to-all-start.4
  155.1 3.1 slice.79
  158.2 3.9 copy.68
  162.1 2.7 fusion.44
  164.8 2.4 fusion.60
  167.1 3.1 fusion.51
  170.2 3.6 fusion.46
  173.8 6.4 %fusion.30 = f32[16,256,4,64]{1,3,2,0:T(8,128)} fusion(bf16[16,256,4,64]{1,3,2,0:T(8,128)(2,1)S(1)} %bitcast.131, f32[16,256,4,64]{1,3,2,0:T(8,128)S(1)} %fusion.46, f32[16,4,256]{2,1,0:T(4,128)S(1)} %copy.73, f32[16,256,256]{2,1,0:T(8,128)S(1)} %fusion.60, pred[256,256]{1,0:T(8,128)(4,1)S(1)} %iota_compare_fusion, f32[4]{0:T(128)S(1)} %dynamic-slice_bitcast_fusion, ...), kind=kOutput, calls=%fused_computation.25 | convolution fusion | flops 563085312 | bytes 14876688 | tf_op jit(solution)/shard_map/chij,cjhp->cihp/dot_general | solution.py:64
  180.3 5.5 %copy.80 = f32[16,256,256]{2,1,0:T(8,128)} copy(f32[16,256,256]{1,2,0:T(8,128)} %bitcast.133) | data formatting | bytes 8388608 | tf_op jit(solution)/shard_map/reshape | solution.py:90
  185.7 0.0 all-to-all-done.4
  185.7 7.0 %all-to-all-start.3 = ((f32[16,256,256]{2,1,0:T(8,128)}), f32[16,256,256]{2,1,0:T(8,128)}, u32[]{:S(2)}, u32[]{:S(2)}) async-start(f32[16,256,256]{2,1,0:T(8,128)} %copy.80), calls=%async_computation.3 | async-start | bytes 8388608 | tf_op jit(solution)/shard_map/all_to_all | solution.py:89
  192.7 2.6 copy.91
  195.3 78.4 %all-to-all-done.3 = f32[16,256,256]{2,1,0:T(8,128)} async-done(((f32[16,256,256]{2,1,0:T(8,128)}), f32[16,256,256]{2,1,0:T(8,128)}, u32[]{:S(2)}, u32[]{:S(2)}) %all-to-all-start.3) | async-done | bytes 4194336 | tf_op jit(solution)/shard_map/all_to_all | solution.py:89
  273.7 2.8 copy.90
  276.5 0.6 copy-done.2
  277.1 5.5 %fusion.43 = f32[256]{0:T(256)S(1)} fusion(f32[32,8,16,256]{3,2,1,0:T(8,128)S(1)} %copy-done.2, f32[16,256,256]{2,1,0:T(8,128)} %all-to-all-done.3), kind=kLoop, calls=%fused_computation.44 | loop fusion | flops 7339776 | bytes 8389632 | tf_op jit(solution)/shard_map/reduce_sum | solution.py:96
  282.7 3.1 fusion.42
  285.8 8.1 %fusion.5 = f32[256,4096]{1,0:T(8,128)} fusion(bf16[1,1024,4096]{2,1,0:T(8,128)(2,1)} %all-gather.11.cloned.1.call-done, bf16[256,4096]{1,0:T(8,128)(2,1)} %fusion.42), kind=kOutput, calls=%fused_computation.8 | convolution fusion | flops 2147483648 | bytes 13107200 | tf_op jit(solution)/shard_map/dot_general | solution.py:104
  293.9 9.0 %fusion.14 = f32[256,4096]{1,0:T(8,128)} fusion(f32[256,4096]{1,0:T(8,128)} %fusion.5, bf16[1,1024,4096]{2,1,0:T(8,128)(2,1)} %all-gather.9.cloned.1.call-done, bf16[256,4096]{1,0:T(8,128)(2,1)S(1)} %copy-done.4), kind=kOutput, calls=%fused_computation.19 | convolution fusion | flops 2148532224 | bytes 17301504 | tf_op jit(solution)/shard_map/dot_general | solution.py:104
  302.9 28.3 %all-gather.13.cloned.1.call-done = bf16[1,1024,4096]{2,1,0:T(8,128)(2,1)} async-done(((bf16[1,1024,256]{2,1,0:T(8,128)(2,1)}), bf16[1,1024,4096]{2,1,0:T(8,128)(2,1)}) %all-gather.13.cloned.1.call-update) | async-done | bytes 8388624 | tf_op jit(solution)/shard_map/all_gather | solution.py:103
  331.2 9.0 %fusion.17 = f32[256,4096]{1,0:T(8,128)} fusion(f32[256,4096]{1,0:T(8,128)} %fusion.14, bf16[1,1024,4096]{2,1,0:T(8,128)(2,1)} %all-gather.13.cloned.1.call-done, bf16[256,4096]{1,0:T(8,128)(2,1)S(1)} %copy-done.4), kind=kOutput, calls=%fused_computation.20 | convolution fusion | flops 2148532224 | bytes 17301504 | tf_op jit(solution)/shard_map/dot_general | solution.py:104
  340.2 69.6 %all-gather.15.cloned.1.call-done = bf16[1,1024,4096]{2,1,0:T(8,128)(2,1)} async-done(((bf16[1,1024,256]{2,1,0:T(8,128)(2,1)}), bf16[1,1024,4096]{2,1,0:T(8,128)(2,1)}) %all-gather.15.cloned.1.call-update) | async-done | bytes 8388624 | tf_op jit(solution)/shard_map/all_gather | solution.py:103
  409.8 8.5 %fusion.26 = bf16[1,256,4096]{2,1,0:T(8,128)(2,1)} fusion(f32[256,4096]{1,0:T(8,128)} %fusion.17, bf16[1,1024,4096]{2,1,0:T(8,128)(2,1)} %all-gather.15.cloned.1.call-done, bf16[256,4096]{1,0:T(8,128)(2,1)} %fusion.42), kind=kOutput, calls=%fused_computation.23 | convolution fusion | flops 2149580800 | bytes 15204352 | tf_op jit(solution)/shard_map/dot_general | solution.py:104
  (37 shorter events, 0.3 us)
Async XLA Ops:
  6.5 84.2 %copy-start = (bf16[256,4096]{1,0:T(8,128)(2,1)S(1)}, bf16[256,4096]{1,0:T(8,128)(2,1)}, u32[]{:S(2)}) copy-start(bf16[256,4096]{1,0:T(8,128)(2,1)} %param.10) | copy-start | bytes 6291460
  6.5 4.6 %copy-start.7 = (bf16[256,64]{0,1:T(8,128)(2,1)S(1)}, bf16[256,64]{0,1:T(8,128)(2,1)}, u32[]{:S(2)}) copy-start(bf16[256,64]{0,1:T(8,128)(2,1)} %param.13) | copy-start | bytes 98308
  6.5 4.7 %copy-start.9 = (s32[1,1,8]{2,1,0:T(1,128)S(1)}, s32[1,1,8]{2,1,0:T(1,128)}, u32[]{:S(2)}) copy-start(s32[1,1,8]{2,1,0:T(1,128)} %param.14) | copy-start | bytes 100
  6.5 5.7 %copy-start.5 = (bf16[256,128]{1,0:T(8,128)(2,1)S(1)}, bf16[256,128]{1,0:T(8,128)(2,1)}, u32[]{:S(2)}) copy-start(bf16[256,128]{1,0:T(8,128)(2,1)} %param.11) | copy-start | bytes 196612
  6.5 5.7 %copy-start.6 = (bf16[256,128]{1,0:T(8,128)(2,1)S(1)}, bf16[256,128]{1,0:T(8,128)(2,1)}, u32[]{:S(2)}) copy-start(bf16[256,128]{1,0:T(8,128)(2,1)} %param.12) | copy-start | bytes 196612
  6.5 279.2 %all-gather.11.cloned.1.call-start = ((), (), s32[]{:S(2)}) async-start(), calls=%async_computation.6 | async-start | bytes 8912896 | tf_op jit(solution)/shard_map/all_gather | solution.py:103
  9.6 284.2 %all-gather.9.cloned.1.call-start = ((), (), s32[]{:S(2)}) async-start(), calls=%async_computation.5 | async-start | bytes 8912896 | tf_op jit(solution)/shard_map/all_gather | solution.py:103
  10.4 320.8 %all-gather.13.cloned.1.call-start = ((), (), s32[]{:S(2)}) async-start(), calls=%async_computation.7 | async-start | bytes 8912896 | tf_op jit(solution)/shard_map/all_gather | solution.py:103
  24.1 34.0 %all-to-all-start = ((bf16[8,32,4480]{2,1,0:T(8,128)(2,1)}), bf16[8,32,4480]{2,1,0:T(8,128)(2,1)}, u32[]{:S(2)}, u32[]{:S(2)}) async-start(bf16[8,32,4480]{2,1,0:T(8,128)(2,1)} %broadcast_select_fusion), calls=%async_computation | async-start | bytes 4587520 | tf_op jit(solution)/shard_map/all_to_all | solution.py:29
  28.7 381.1 %all-gather.15.cloned.1.call-start = ((), (), s32[]{:S(2)}) async-start(), calls=%async_computation.8 | async-start | bytes 8912896 | tf_op jit(solution)/shard_map/all_gather | solution.py:103
  62.8 20.7 %all-to-all-start.2 = ((bf16[16,256,4]{1,2,0:T(4,128)(2,1)}), bf16[16,256,4]{1,2,0:T(4,128)(2,1)S(1)}, u32[]{:S(2)}, u32[]{:S(2)}) async-start(bf16[16,256,4]{1,2,0:T(4,128)(2,1)} %bitcast.6), calls=%async_computation.2 | async-start | bytes 65536 | tf_op jit(solution)/shard_map/all_to_all | solution.py:50
  83.5 67.8 %all-to-all-start.1 = ((bf16[16,256,512]{2,1,0:T(8,128)(2,1)}), bf16[16,256,512]{2,1,0:T(8,128)(2,1)}, u32[]{:S(2)}, u32[]{:S(2)}) async-start(bf16[16,256,512]{2,1,0:T(8,128)(2,1)} %pad_maximum_fusion), calls=%async_computation.1 | async-start | bytes 8388608 | tf_op jit(solution)/shard_map/all_to_all | solution.py:48
  90.7 2.0 copy-start.10
  151.3 34.5 %all-to-all-start.4 = ((bf16[8,32,4096]{2,1,0:T(8,128)(2,1)}), bf16[8,32,4096]{2,1,0:T(8,128)(2,1)S(1)}, u32[]{:S(2)}, u32[]{:S(2)}) async-start(bf16[8,32,4096]{2,1,0:T(8,128)(2,1)} %broadcast_select_fusion.1), calls=%async_computation.4 | async-start | bytes 4194304 | tf_op jit(solution)/shard_map/all_to_all | solution.py:31
  170.2 3.6 copy-start.3
  185.7 87.9 %all-to-all-start.3 = ((f32[16,256,256]{2,1,0:T(8,128)}), f32[16,256,256]{2,1,0:T(8,128)}, u32[]{:S(2)}, u32[]{:S(2)}) async-start(f32[16,256,256]{2,1,0:T(8,128)} %copy.80), calls=%async_computation.3 | async-start | bytes 8388608 | tf_op jit(solution)/shard_map/all_to_all | solution.py:89
  273.7 3.4 copy-start.2
  277.1 5.5 %copy-start.8 = (f32[1,4096]{1,0:T(1,128)S(1)}, f32[1,4096]{1,0:T(1,128)}, u32[]{:S(2)}) copy-start(f32[1,4096]{1,0:T(1,128)} %param.16) | copy-start | bytes 49156
  285.8 8.1 %copy-start.4 = (bf16[256,4096]{1,0:T(8,128)(2,1)S(1)}, bf16[256,4096]{1,0:T(8,128)(2,1)}, u32[]{:S(2)}) copy-start(bf16[256,4096]{1,0:T(8,128)(2,1)} %fusion.42) | copy-start | bytes 6291460
  409.8 8.6 %copy-start.1 = (bf16[256,4096]{1,0:T(8,128)(2,1)S(1)}, bf16[256,4096]{1,0:T(8,128)(2,1)}, u32[]{:S(2)}) copy-start(bf16[256,4096]{1,0:T(8,128)(2,1)} %param.10) | copy-start | bytes 6291460
Sparse Core Ops, SparseCore 0:
  9.8 80.1 all-gather.10
  92.1 135.9 all-gather.8
  230.2 100.9 all-gather.12
  333.2 76.6 all-gather.14

commit v4 on v3

--- a/solution.py
+++ b/solution.py
@@ -96,14 +96,11 @@
         * lax.rsqrt(jnp.mean(gated * gated, axis=-1, keepdims=True) + 1e-05)
         * norm_gain[0][None, :]
     ).astype(jnp.bfloat16)
-    pieces = 4
-    span = width // pieces
-    mixed = None
-    for k in range(pieces):
-        part = lax.all_gather(out_weight[0, k * span : (k + 1) * span], "seq", axis=1, tiled=True)
-        term = jnp.dot(normed[:, k * span : (k + 1) * span], part, preferred_element_type=jnp.float32)
-        mixed = term if mixed is None else mixed + term
-    mixed = mixed.astype(jnp.bfloat16)
+    mixed = jnp.dot(
+        normed,
+        lax.all_gather(out_weight[0], "seq", axis=1, tiled=True),
+        preferred_element_type=jnp.float32,
+    ).astype(jnp.bfloat16)
     return mixed.reshape(1, rows, mixed.shape[-1])
 
 

time: 426 us -> 348 us (0.82); the launches traced: 425 us -> 342 us
  waiting for transfers between devices: 259 us -> 160 us
  blocking collectives: 0 us -> 33.7 us
  matrix products: 53.4 us -> 35.5 us
    all_gather x4 -> x1, waiting for transfers between devices: 97.9 us -> 0.01 us  [per_device(): lax.all_gather(out_weight[0], 'seq', axis=1, tiled=True)]
    all_to_all x0 -> x1, blocking collectives: none -> 33.7 us  [per_device(): lax.all_to_all(arrange(packed), 'dom', split_axis=0, concat_axis=0, tiled...]
    all_to_all x1 -> x0, waiting for transfers between devices: 28.8 us -> none  [per_device(): lax.all_to_all(arrange(packed), 'dom', split_axis=0, concat_axis=0, tiled...]
    all_to_all x1, waiting for transfers between devices: 51.5 us -> 72.6 us  [per_device(): xbc = lax.all_to_all(xbc, 'seq', split_axis=0, concat_axis=0, tiled=True)]
    dot_general x4 -> x1, matrix products: 34.7 us -> 16.7 us  [per_device(): jnp.dot(normed, lax.all_gather(out_weight[0], 'seq', axis=1, tiled=True),...]
    all_to_all x1, starting transfers between devices: 6.96 us -> 15.4 us  [per_device(): lax.all_to_all(ys.reshape(shards, rows, local), 'seq', split_axis=0, conc...]
    all_to_all x1, waiting for transfers between devices: 78.4 us -> 86.5 us  [per_device(): lax.all_to_all(ys.reshape(shards, rows, local), 'seq', split_axis=0, conc...]
    all_to_all x1 -> x0, starting transfers between devices: 4.58 us -> none  [per_device(): lax.all_to_all(arrange(packed), 'dom', split_axis=0, concat_axis=0, tiled...]
  transfers between devices with their start and end apart: 9 -> 5, of which waited for: 5 -> 2; matrix products, arithmetic and copies ran while one was open for 26% -> 24% of each run, Pallas kernels for 0% -> 0%
where the time goes in v4:
time: 348 us; the launch traced here: 342 us
  waiting for transfers between devices  160 us (46%)
  local copies, waits for them, and re-layouts  43.4 us (12%)
  matrix products  35.5 us (10%)
  starting transfers between devices  34.4 us (10%)
  blocking collectives  33.7 us (10%)
  other arithmetic  21.3 us (6%)
  between operations  13.6 us (4%)
    all_to_all x1, waiting for transfers between devices, per_device(): lax.all_to_all(ys.reshape(shards, rows, local), 'seq', split_axis=0, conc...  86.5 us
    all_to_all x1, waiting for transfers between devices, per_device(): xbc = lax.all_to_all(xbc, 'seq', split_axis=0, concat_axis=0, tiled=True)  72.6 us
    all_to_all x1, blocking collectives, per_device(): lax.all_to_all(arrange(packed), 'dom', split_axis=0, concat_axis=0, tiled...  33.7 us
    dot_general x1, matrix products, per_device(): jnp.dot(normed, lax.all_gather(out_weight[0], 'seq', axis=1, tiled=True),...  16.7 us
    all_to_all x1, starting transfers between devices, per_device(): lax.all_to_all(ys.reshape(shards, rows, local), 'seq', split_axis=0, conc...  15.4 us
    unnamed x17, local copies, waits for them, and re-layouts  8.26 us
    all_to_all x1, starting transfers between devices, per_device(): lsh = lax.all_to_all(lsh, 'seq', split_axis=0, concat_axis=0, tiled=True)  7.91 us
    all_to_all x1, starting transfers between devices, per_device(): xbc = lax.all_to_all(xbc, 'seq', split_axis=0, concat_axis=0, tiled=True)  7.27 us
  transfers between devices with their start and end apart: 5, of which 2 were waited for; matrix products, arithmetic and copies ran while one was open for 24% of the time, Pallas kernels for 0%

profile of v4, /device:TPU:0, one launch (start us, length us, event | category | flops | bytes accessed | tf_op | source)
XLA Modules:
  0.0 341.7 jit_solution(10297323648021078176)
XLA Ops:
  6.5 0.0 copy-start
  6.5 0.0 all-gather.3.cloned.1.call-start
  6.5 0.7 all-gather.3.cloned.1.call-update
  7.3 0.9 copy.65
  8.1 1.6 sort.17
  9.8 4.5 %concatenate.6 = bf16[256,4480]{1,0:T(8,128)(2,1)} concatenate(bf16[256,4096]{1,0:T(8,128)(2,1)} %param.9, bf16[256,128]{1,0:T(8,128)(2,1)} %param.11, bf16[256,128]{1,0:T(8,128)(2,1)} %param.12, bf16[256,64]{1,0:T(8,128)(2,1)S(1)} %copy.65, bf16[256,64]{1,0:T(8,128)(2,1)S(1)} %broadcast_in_dim.45), dimensions={1} | concatenate | bytes 4587520 | tf_op jit(solution)/shard_map/concatenate | solution.py:26
  14.3 3.9 %gather_fusion = bf16[8,32,4480]{2,1,0:T(8,128)(2,1)} fusion(bf16[8,32,4480]{2,1,0:T(8,128)(2,1)} %bitcast.117, s32[1024]{0:T(1024)S(1)} %pad_clamp_fusion), kind=kCustom, calls=%fused_computation | custom fusion | bytes 4587552 | tf_op jit(solution)/shard_map/jit(_take)/gather | solution.py:23
  18.2 1.9 broadcast_select_fusion
  20.1 33.7 %all_to_all.25 = bf16[8,32,4480]{2,1,0:T(8,128)(2,1)S(1)} all-to-all(bf16[8,32,4480]{2,1,0:T(8,128)(2,1)S(1)} %broadcast_select_fusion), channel_id=1, replica_groups=mesh['dom'=8,'seq'=16] {'dom'}, dimensions={0} | all-to-all | bytes 4587520 | tf_op jit(solution)/shard_map/all_to_all | solution.py:29
  53.8 0.0 copy-start.3
  53.8 1.4 copy-done.3
  55.2 1.6 slice.44
  56.8 0.1 copy.69
  56.9 0.6 reshape.147
  57.5 7.9 %all-to-all-start.2 = ((bf16[16,256,4]{1,2,0:T(4,128)(2,1)}), bf16[16,256,4]{1,2,0:T(4,128)(2,1)S(1)}, u32[]{:S(2)}, u32[]{:S(2)}) async-start(bf16[16,256,4]{1,2,0:T(4,128)(2,1)} %bitcast.6), calls=%async_computation.2 | async-start | bytes 65536 | tf_op jit(solution)/shard_map/all_to_all | solution.py:50
  65.4 4.1 %copy.66 = bf16[256,4096]{0,1:T(8,128)(2,1)} copy(bf16[256,4096]{1,0:T(8,128)(2,1)} %slice.44) | data formatting | bytes 4194304 | tf_op jit(solution)/shard_map/slice | solution.py:33
  69.5 3.9 %copy.67 = bf16[256,16,256]{2,0,1:T(8,128)(2,1)} copy(bf16[256,16,256]{0,2,1:T(8,128)(2,1)} %bitcast.118) | data formatting | bytes 4194304 | tf_op jit(solution)/shard_map/reshape | solution.py:42
  73.4 0.9 fusion.56
  74.3 0.2 broadcast_in_dim.52
  74.5 0.2 broadcast_in_dim.53
  74.7 3.5 %pad_maximum_fusion = bf16[16,256,512]{2,1,0:T(8,128)(2,1)} fusion(bf16[16,256,128]{2,1,0:T(8,128)(2,1)S(1)} %broadcast_in_dim.53, bf16[16,256,128]{2,1,0:T(8,128)(2,1)S(1)} %broadcast_in_dim.52, bf16[16,256,256]{2,1,0:T(8,128)(2,1)} %bitcast.121), kind=kLoop, calls=%fused_computation.24 | loop fusion | flops 12582912 | bytes 8388608 | tf_op jit(solution)/shard_map/concatenate | solution.py:40
  78.2 0.0 all-to-all-done.2
  78.2 7.3 %all-to-all-start.1 = ((bf16[16,256,512]{2,1,0:T(8,128)(2,1)}), bf16[16,256,512]{2,1,0:T(8,128)(2,1)}, u32[]{:S(2)}, u32[]{:S(2)}) async-start(bf16[16,256,512]{2,1,0:T(8,128)(2,1)} %pad_maximum_fusion), calls=%async_computation.1 | async-start | bytes 8388608 | tf_op jit(solution)/shard_map/all_to_all | solution.py:48
  85.5 0.0 copy-start.6
  85.5 0.0 copy-done
  85.5 2.0 gather_fusion.1
  87.5 0.0 copy-done.6
  87.5 0.1 dynamic-slice_bitcast_fusion
  87.7 3.3 broadcast_select_fusion.1
  91.0 0.1 reshape.180
  91.0 2.3 reduce-window.6
  93.3 0.2 slice_reduce_fusion
  93.5 0.1 copy_bitcast_fusion
  93.6 0.2 slice_reduce_fusion.1
  93.8 0.1 bitcast_exponential_fusion
  94.0 0.6 fusion.41
  94.6 72.6 %all-to-all-done.1 = bf16[16,256,512]{2,1,0:T(8,128)(2,1)} async-done(((bf16[16,256,512]{2,1,0:T(8,128)(2,1)}), bf16[16,256,512]{2,1,0:T(8,128)(2,1)}, u32[]{:S(2)}, u32[]{:S(2)}) %all-to-all-start.1) | async-done | bytes 4194336 | tf_op jit(solution)/shard_map/all_to_all | solution.py:48
  167.2 3.8 %all-to-all-start.4 = ((bf16[8,32,4096]{2,1,0:T(8,128)(2,1)}), bf16[8,32,4096]{2,1,0:T(8,128)(2,1)S(1)}, u32[]{:S(2)}, u32[]{:S(2)}) async-start(bf16[8,32,4096]{2,1,0:T(8,128)(2,1)} %broadcast_select_fusion.1), calls=%async_computation.4 | async-start | bytes 4194304 | tf_op jit(solution)/shard_map/all_to_all | solution.py:31
  171.0 3.2 slice.47
  174.2 4.0 %copy.68 = bf16[16,256,256]{1,2,0:T(8,128)(2,1)} copy(bf16[16,256,256]{2,1,0:T(8,128)(2,1)} %slice.47) | data formatting | bytes 4194304 | tf_op jit(solution)/shard_map/slice | solution.py:53
  178.1 2.7 fusion.29
  180.8 2.4 fusion.45
  183.2 3.1 fusion.36
  186.3 0.0 copy-start.4
  186.3 3.6 %fusion.31 = f32[16,256,4,64]{1,3,2,0:T(8,128)S(1)} fusion(f32[16,4,64,128]{3,0,2,1:T(8,128)S(1)} %fusion.36, bf16[16,256,512]{2,1,0:T(8,128)(2,1)} %all-to-all-done.1), kind=kOutput, calls=%fused_computation.38 | convolution fusion | flops 1610612736 | bytes 7340032 | tf_op jit(solution)/shard_map/cin,chpn->cihp/dot_general | solution.py:79
  189.9 0.0 copy-done.4
  190.0 6.4 %fusion.15 = f32[16,256,4,64]{1,3,2,0:T(8,128)} fusion(bf16[16,256,4,64]{1,3,2,0:T(8,128)(2,1)S(1)} %bitcast.120, f32[16,256,4,64]{1,3,2,0:T(8,128)S(1)} %fusion.31, f32[16,4,256]{2,1,0:T(4,128)S(1)} %copy.73, f32[16,256,256]{2,1,0:T(8,128)S(1)} %fusion.45, pred[256,256]{1,0:T(8,128)(4,1)S(1)} %iota_compare_fusion, f32[4]{0:T(128)S(1)} %dynamic-slice_bitcast_fusion, ...), kind=kOutput, calls=%fused_computation.16 | convolution fusion | flops 563085312 | bytes 14876688 | tf_op jit(solution)/shard_map/chij,cjhp->cihp/dot_general | solution.py:64
  196.3 5.4 %copy.80 = f32[16,256,256]{2,1,0:T(8,128)} copy(f32[16,256,256]{1,2,0:T(8,128)} %bitcast.122) | data formatting | bytes 8388608 | tf_op jit(solution)/shard_map/reshape | solution.py:90
  201.7 0.0 all-to-all-done.4
  201.7 15.4 %all-to-all-start.3 = ((f32[16,256,256]{2,1,0:T(8,128)}), f32[16,256,256]{2,1,0:T(8,128)}, u32[]{:S(2)}, u32[]{:S(2)}) async-start(f32[16,256,256]{2,1,0:T(8,128)} %copy.80), calls=%async_computation.3 | async-start | bytes 8388608 | tf_op jit(solution)/shard_map/all_to_all | solution.py:89
  217.2 2.5 copy.91
  219.7 86.5 %all-to-all-done.3 = f32[16,256,256]{2,1,0:T(8,128)} async-done(((f32[16,256,256]{2,1,0:T(8,128)}), f32[16,256,256]{2,1,0:T(8,128)}, u32[]{:S(2)}, u32[]{:S(2)}) %all-to-all-start.3) | async-done | bytes 4194336 | tf_op jit(solution)/shard_map/all_to_all | solution.py:89
  306.2 0.0 copy-start.2
  306.2 2.8 copy.90
  309.0 0.6 copy-done.2
  309.7 0.0 copy-start.5
  309.7 5.3 %fusion.28 = f32[256]{0:T(256)S(1)} fusion(f32[32,8,16,256]{3,2,1,0:T(8,128)S(1)} %copy-done.2, f32[16,256,256]{2,1,0:T(8,128)} %all-to-all-done.3), kind=kLoop, calls=%fused_computation.35 | loop fusion | flops 7339776 | bytes 8389632 | tf_op jit(solution)/shard_map/reduce_sum | solution.py:96
  315.0 0.0 copy-done.5
  315.0 3.1 fusion.27
  318.1 0.0 all-gather.3.cloned.1.call-done
  318.1 0.0 copy-start.1
  318.1 16.7 %fusion.11 = bf16[1,256,4096]{2,1,0:T(8,128)(2,1)} fusion(bf16[256,4096]{1,0:T(8,128)(2,1)} %fusion.27, bf16[1,4096,4096]{2,1,0:T(8,128)(2,1)} %all-gather.3.cloned.1.call-done), kind=kOutput, calls=%fused_computation.14 | convolution fusion | flops 8590983168 | bytes 37748736 | tf_op jit(solution)/shard_map/dot_general | solution.py:99
  334.8 0.0 copy-done.1
  (16 shorter events, 0.2 us)
Async XLA Ops:
  6.5 79.0 %copy-start = (bf16[256,4096]{1,0:T(8,128)(2,1)S(1)}, bf16[256,4096]{1,0:T(8,128)(2,1)}, u32[]{:S(2)}) copy-start(bf16[256,4096]{1,0:T(8,128)(2,1)} %param.10) | copy-start | bytes 6291460
  6.5 311.5 %all-gather.3.cloned.1.call-start = ((), (), s32[]{:S(2)}) async-start(), calls=%async_computation.5 | async-start | bytes 35651584 | tf_op jit(solution)/shard_map/all_gather | solution.py:101
  53.8 1.4 copy-start.3
  57.5 20.7 %all-to-all-start.2 = ((bf16[16,256,4]{1,2,0:T(4,128)(2,1)}), bf16[16,256,4]{1,2,0:T(4,128)(2,1)S(1)}, u32[]{:S(2)}, u32[]{:S(2)}) async-start(bf16[16,256,4]{1,2,0:T(4,128)(2,1)} %bitcast.6), calls=%async_computation.2 | async-start | bytes 65536 | tf_op jit(solution)/shard_map/all_to_all | solution.py:50
  78.2 88.9 %all-to-all-start.1 = ((bf16[16,256,512]{2,1,0:T(8,128)(2,1)}), bf16[16,256,512]{2,1,0:T(8,128)(2,1)}, u32[]{:S(2)}, u32[]{:S(2)}) async-start(bf16[16,256,512]{2,1,0:T(8,128)(2,1)} %pad_maximum_fusion), calls=%async_computation.1 | async-start | bytes 8388608 | tf_op jit(solution)/shard_map/all_to_all | solution.py:48
  85.5 2.0 copy-start.6
  167.2 34.5 %all-to-all-start.4 = ((bf16[8,32,4096]{2,1,0:T(8,128)(2,1)}), bf16[8,32,4096]{2,1,0:T(8,128)(2,1)S(1)}, u32[]{:S(2)}, u32[]{:S(2)}) async-start(bf16[8,32,4096]{2,1,0:T(8,128)(2,1)} %broadcast_select_fusion.1), calls=%async_computation.4 | async-start | bytes 4194304 | tf_op jit(solution)/shard_map/all_to_all | solution.py:31
  186.3 3.6 %copy-start.4 = (bf16[16,256,256]{1,2,0:T(8,128)(2,1)S(1)}, bf16[16,256,256]{1,2,0:T(8,128)(2,1)}, u32[]{:S(2)}) copy-start(bf16[16,256,256]{1,2,0:T(8,128)(2,1)} %copy.68) | copy-start | bytes 6291460
  201.7 104.5 %all-to-all-start.3 = ((f32[16,256,256]{2,1,0:T(8,128)}), f32[16,256,256]{2,1,0:T(8,128)}, u32[]{:S(2)}, u32[]{:S(2)}) async-start(f32[16,256,256]{2,1,0:T(8,128)} %copy.80), calls=%async_computation.3 | async-start | bytes 8388608 | tf_op jit(solution)/shard_map/all_to_all | solution.py:89
  306.2 3.4 %copy-start.2 = (f32[32,8,16,256]{3,2,1,0:T(8,128)S(1)}, f32[32,8,16,256]{3,2,1,0:T(8,128)}, u32[]{:S(2)}) copy-start(f32[32,8,16,256]{3,2,1,0:T(8,128)} %copy.91) | copy-start | bytes 12582916
  309.7 5.3 %copy-start.5 = (f32[1,4096]{1,0:T(1,128)S(1)}, f32[1,4096]{1,0:T(1,128)}, u32[]{:S(2)}) copy-start(f32[1,4096]{1,0:T(1,128)} %param.16) | copy-start | bytes 49156
  318.1 16.8 %copy-start.1 = (bf16[256,4096]{1,0:T(8,128)(2,1)S(1)}, bf16[256,4096]{1,0:T(8,128)(2,1)}, u32[]{:S(2)}) copy-start(bf16[256,4096]{1,0:T(8,128)(2,1)} %param.10) | copy-start | bytes 6291460
Sparse Core Ops, SparseCore 0:
  9.4 298.6 all-gather.2

commit v5 on v4

--- a/solution.py
+++ b/solution.py
@@ -87,8 +87,12 @@
     )
 
     ys = lax.all_to_all(
-        ys.reshape(shards, rows, local), "seq", split_axis=0, concat_axis=0, tiled=True
-    )
+        ys.reshape(shards, rows, local).astype(jnp.bfloat16),
+        "seq",
+        split_axis=0,
+        concat_axis=0,
+        tiled=True,
+    ).astype(jnp.float32)
     ys = jnp.transpose(ys, (1, 0, 2)).reshape(rows, width)
     gated = ys * jax.nn.silu(zs.astype(jnp.float32))
     normed = (

time: 348 us -> 312 us (0.90); the launches traced: 342 us -> 310 us
  waiting for transfers between devices: 160 us -> 126 us
    all_to_all x1, waiting for transfers between devices: 86.5 us -> 43.1 us  [per_device(): lax.all_to_all(ys.reshape(shards, rows, local).astype(jnp.bfloat16), 'seq...]
    all_gather x1, waiting for transfers between devices: 0.01 us -> 9.95 us  [per_device(): lax.all_gather(out_weight[0], 'seq', axis=1, tiled=True)]
    reshape x1 -> x0, local copies, waits for them, and re-layouts: 5.39 us -> none  [per_device(): ys.reshape(shards, rows, local)]
    convert_element_type x0 -> x1, local copies, waits for them, and re-layouts: none -> 3.92 us  [per_device(): ys.reshape(shards, rows, local).astype(jnp.bfloat16)]
  transfers between devices with their start and end apart: 5 -> 5, of which waited for: 2 -> 3; matrix products, arithmetic and copies ran while one was open for 24% -> 27% of each run, Pallas kernels for 0% -> 0%
where the time goes in v5:
time: 312 us; the launch traced here: 310 us
  waiting for transfers between devices  126 us (40%)
  local copies, waits for them, and re-layouts  42.5 us (14%)
  matrix products  36.3 us (12%)
  starting transfers between devices  34.4 us (11%)
  blocking collectives  33.7 us (11%)
  other arithmetic  22.8 us (7%)
  between operations  13.7 us (4%)
    all_to_all x1, waiting for transfers between devices, per_device(): xbc = lax.all_to_all(xbc, 'seq', split_axis=0, concat_axis=0, tiled=True)  72.6 us
    all_to_all x1, waiting for transfers between devices, per_device(): lax.all_to_all(ys.reshape(shards, rows, local).astype(jnp.bfloat16), 'seq...  43.1 us
    all_to_all x1, blocking collectives, per_device(): lax.all_to_all(arrange(packed), 'dom', split_axis=0, concat_axis=0, tiled...  33.7 us
    dot_general x1, matrix products, per_device(): jnp.dot(normed, lax.all_gather(out_weight[0], 'seq', axis=1, tiled=True),...  16.7 us
    all_to_all x1, starting transfers between devices, per_device(): lax.all_to_all(ys.reshape(shards, rows, local).astype(jnp.bfloat16), 'seq...  15.4 us
    all_gather x1, waiting for transfers between devices, per_device(): lax.all_gather(out_weight[0], 'seq', axis=1, tiled=True)  9.95 us
    unnamed x17, local copies, waits for them, and re-layouts  8.81 us
    all_to_all x1, starting transfers between devices, per_device(): lsh = lax.all_to_all(lsh, 'seq', split_axis=0, concat_axis=0, tiled=True)  7.91 us
  transfers between devices with their start and end apart: 5, of which 3 were waited for; matrix products, arithmetic and copies ran while one was open for 27% of the time, Pallas kernels for 0%

profile of v5, /device:TPU:0, one launch (start us, length us, event | category | flops | bytes accessed | tf_op | source)
XLA Modules:
  0.0 309.7 jit_solution(18277665628529218645)
XLA Ops:
  6.5 0.0 copy-start
  6.5 0.0 all-gather.3.cloned.1.call-start
  6.5 0.7 all-gather.3.cloned.1.call-update
  7.3 0.9 copy.65
  8.1 1.6 sort.17
  9.8 4.5 %concatenate.6 = bf16[256,4480]{1,0:T(8,128)(2,1)} concatenate(bf16[256,4096]{1,0:T(8,128)(2,1)} %param.9, bf16[256,128]{1,0:T(8,128)(2,1)} %param.11, bf16[256,128]{1,0:T(8,128)(2,1)} %param.12, bf16[256,64]{1,0:T(8,128)(2,1)S(1)} %copy.65, bf16[256,64]{1,0:T(8,128)(2,1)S(1)} %broadcast_in_dim.45), dimensions={1} | concatenate | bytes 4587520 | tf_op jit(solution)/shard_map/concatenate | solution.py:26
  14.3 3.9 %gather_fusion = bf16[8,32,4480]{2,1,0:T(8,128)(2,1)} fusion(bf16[8,32,4480]{2,1,0:T(8,128)(2,1)} %bitcast.117, s32[1024]{0:T(1024)S(1)} %pad_clamp_fusion), kind=kCustom, calls=%fused_computation | custom fusion | bytes 4587552 | tf_op jit(solution)/shard_map/jit(_take)/gather | solution.py:23
  18.2 1.9 broadcast_select_fusion
  20.1 33.7 %all_to_all.25 = bf16[8,32,4480]{2,1,0:T(8,128)(2,1)S(1)} all-to-all(bf16[8,32,4480]{2,1,0:T(8,128)(2,1)S(1)} %broadcast_select_fusion), channel_id=1, replica_groups=mesh['dom'=8,'seq'=16] {'dom'}, dimensions={0} | all-to-all | bytes 4587520 | tf_op jit(solution)/shard_map/all_to_all | solution.py:29
  53.8 0.0 copy-start.3
  53.8 1.4 copy-done.3
  55.2 1.6 slice.44
  56.8 0.1 copy.69
  56.9 0.6 reshape.146
  57.5 7.9 %all-to-all-start.2 = ((bf16[16,256,4]{1,2,0:T(4,128)(2,1)}), bf16[16,256,4]{1,2,0:T(4,128)(2,1)S(1)}, u32[]{:S(2)}, u32[]{:S(2)}) async-start(bf16[16,256,4]{1,2,0:T(4,128)(2,1)} %bitcast.6), calls=%async_computation.2 | async-start | bytes 65536 | tf_op jit(solution)/shard_map/all_to_all | solution.py:50
  65.4 4.1 %copy.66 = bf16[256,4096]{0,1:T(8,128)(2,1)} copy(bf16[256,4096]{1,0:T(8,128)(2,1)} %slice.44) | data formatting | bytes 4194304 | tf_op jit(solution)/shard_map/slice | solution.py:33
  69.5 3.9 %copy.67 = bf16[256,16,256]{2,0,1:T(8,128)(2,1)} copy(bf16[256,16,256]{0,2,1:T(8,128)(2,1)} %bitcast.118) | data formatting | bytes 4194304 | tf_op jit(solution)/shard_map/reshape | solution.py:42
  73.4 0.9 fusion.57
  74.3 0.2 broadcast_in_dim.52
  74.5 0.2 broadcast_in_dim.53
  74.7 3.5 %pad_maximum_fusion = bf16[16,256,512]{2,1,0:T(8,128)(2,1)} fusion(bf16[16,256,128]{2,1,0:T(8,128)(2,1)S(1)} %broadcast_in_dim.53, bf16[16,256,128]{2,1,0:T(8,128)(2,1)S(1)} %broadcast_in_dim.52, bf16[16,256,256]{2,1,0:T(8,128)(2,1)} %bitcast.121), kind=kLoop, calls=%fused_computation.25 | loop fusion | flops 12582912 | bytes 8388608 | tf_op jit(solution)/shard_map/concatenate | solution.py:40
  78.2 0.0 all-to-all-done.2
  78.2 7.3 %all-to-all-start.1 = ((bf16[16,256,512]{2,1,0:T(8,128)(2,1)}), bf16[16,256,512]{2,1,0:T(8,128)(2,1)}, u32[]{:S(2)}, u32[]{:S(2)}) async-start(bf16[16,256,512]{2,1,0:T(8,128)(2,1)} %pad_maximum_fusion), calls=%async_computation.1 | async-start | bytes 8388608 | tf_op jit(solution)/shard_map/all_to_all | solution.py:48
  85.5 0.0 copy-start.6
  85.5 0.0 copy-done
  85.5 2.0 gather_fusion.1
  87.5 0.0 copy-done.6
  87.5 0.1 dynamic-slice_bitcast_fusion
  87.7 3.3 %broadcast_select_fusion.1 = bf16[8,32,4096]{2,1,0:T(8,128)(2,1)} fusion(bf16[8,32,4096]{2,1,0:T(8,128)(2,1)} %gather_fusion.1, pred[8]{0:T(512)(128)(4,1)S(1)} %compare_and_fusion), kind=kLoop, calls=%fused_computation.45 | loop fusion | flops 1048576 | bytes 4194312 | tf_op jit(solution)/shard_map/jit(_take)/select_n | solution.py:23
  91.0 0.1 reshape.178
  91.0 2.3 reduce-window.6
  93.3 0.2 slice_reduce_fusion
  93.5 0.1 copy_bitcast_fusion
  93.6 0.2 slice_reduce_fusion.1
  93.8 0.1 bitcast_exponential_fusion
  94.0 0.6 fusion.42
  94.6 72.6 %all-to-all-done.1 = bf16[16,256,512]{2,1,0:T(8,128)(2,1)} async-done(((bf16[16,256,512]{2,1,0:T(8,128)(2,1)}), bf16[16,256,512]{2,1,0:T(8,128)(2,1)}, u32[]{:S(2)}, u32[]{:S(2)}) %all-to-all-start.1) | async-done | bytes 4194336 | tf_op jit(solution)/shard_map/all_to_all | solution.py:48
  167.2 3.8 %all-to-all-start.4 = ((bf16[8,32,4096]{2,1,0:T(8,128)(2,1)}), bf16[8,32,4096]{2,1,0:T(8,128)(2,1)S(1)}, u32[]{:S(2)}, u32[]{:S(2)}) async-start(bf16[8,32,4096]{2,1,0:T(8,128)(2,1)} %broadcast_select_fusion.1), calls=%async_computation.4 | async-start | bytes 4194304 | tf_op jit(solution)/shard_map/all_to_all | solution.py:31
  171.0 3.2 %slice.47 = bf16[16,256,256]{2,1,0:T(8,128)(2,1)} slice(bf16[16,256,512]{2,1,0:T(8,128)(2,1)} %all-to-all-done.1), slice={[0:16], [0:256], [0:256]} | slice | bytes 4194304 | tf_op jit(solution)/shard_map/slice | solution.py:53
  174.2 4.0 %copy.68 = bf16[16,256,256]{1,2,0:T(8,128)(2,1)} copy(bf16[16,256,256]{2,1,0:T(8,128)(2,1)} %slice.47) | data formatting | bytes 4194304 | tf_op jit(solution)/shard_map/slice | solution.py:53
  178.1 2.7 fusion.30
  180.8 2.4 fusion.46
  183.2 3.1 %fusion.37 = f32[16,4,64,128]{3,0,2,1:T(8,128)S(1)} fusion(f32[16,4,64,128]{3,2,1,0:T(8,128)S(1)} %fusion.30, f32[4,16,16,1]{2,0,1,3:T(4,128)S(1)} %fusion.42), kind=kOutput, calls=%fused_computation.46 | convolution fusion | flops 100663296 | bytes 4198400 | tf_op jit(solution)/shard_map/hkj,jhpn->khpn/dot_general | solution.py:78
  186.3 0.0 copy-start.4
  186.3 3.6 %fusion.32 = f32[16,256,4,64]{1,3,2,0:T(8,128)S(1)} fusion(f32[16,4,64,128]{3,0,2,1:T(8,128)S(1)} %fusion.37, bf16[16,256,512]{2,1,0:T(8,128)(2,1)} %all-to-all-done.1), kind=kOutput, calls=%fused_computation.40 | convolution fusion | flops 1610612736 | bytes 7340032 | tf_op jit(solution)/shard_map/cin,chpn->cihp/dot_general | solution.py:79
  189.9 0.0 copy-done.4
  190.0 7.3 %fusion.16 = bf16[16,256,4,64]{1,3,2,0:T(8,128)(2,1)} fusion(bf16[16,256,4,64]{1,3,2,0:T(8,128)(2,1)S(1)} %bitcast.120, f32[16,256,4,64]{1,3,2,0:T(8,128)S(1)} %fusion.32, f32[16,4,256]{2,1,0:T(4,128)S(1)} %copy.73, f32[16,256,256]{2,1,0:T(8,128)S(1)} %fusion.46, pred[256,256]{1,0:T(8,128)(4,1)S(1)} %iota_compare_fusion, ...), kind=kOutput, calls=%fused_computation.17 | convolution fusion | flops 564133888 | bytes 12779536 | tf_op jit(solution)/shard_map/chij,cjhp->cihp/dot_general | solution.py:64
  197.2 3.9 %copy.80 = bf16[16,256,256]{2,1,0:T(8,128)(2,1)} copy(bf16[16,256,256]{1,2,0:T(8,128)(2,1)} %bitcast.122) | data formatting | bytes 4194304 | tf_op jit(solution)/shard_map/convert_element_type | solution.py:90
  201.1 0.0 all-to-all-done.4
  201.1 15.4 %all-to-all-start.3 = ((bf16[16,256,256]{2,1,0:T(8,128)(2,1)}), bf16[16,256,256]{2,1,0:T(8,128)(2,1)}, u32[]{:S(2)}, u32[]{:S(2)}) async-start(bf16[16,256,256]{2,1,0:T(8,128)(2,1)} %copy.80), calls=%async_computation.3 | async-start | bytes 4194304 | tf_op jit(solution)/shard_map/all_to_all | solution.py:89
  216.6 2.7 copy.91
  219.2 43.1 %all-to-all-done.3 = bf16[16,256,256]{2,1,0:T(8,128)(2,1)} async-done(((bf16[16,256,256]{2,1,0:T(8,128)(2,1)}), bf16[16,256,256]{2,1,0:T(8,128)(2,1)}, u32[]{:S(2)}, u32[]{:S(2)}) %all-to-all-start.3) | async-done | bytes 2097184 | tf_op jit(solution)/shard_map/all_to_all | solution.py:89
  262.4 2.8 copy_convert_fusion
  265.2 0.0 copy-start.2
  265.2 3.9 %copy.90 = f32[32,8,16,256]{3,1,2,0:T(8,128)S(1)} copy(f32[32,8,16,256]{3,2,1,0:T(8,128)S(1)} %bitcast.113) | data formatting | bytes 8388608
  269.0 0.0 copy-done.2
  269.1 0.0 copy-start.5
  269.1 4.0 %fusion.29 = f32[256]{0:T(256)S(1)} fusion(f32[32,8,16,256]{3,2,1,0:T(8,128)S(1)} %copy-done.2, bf16[16,256,256]{2,1,0:T(8,128)(2,1)} %all-to-all-done.3), kind=kLoop, calls=%fused_computation.36 | loop fusion | flops 8388352 | bytes 6292480 | tf_op jit(solution)/shard_map/reduce_sum | solution.py:100
  273.1 0.0 copy-done.5
  273.1 3.1 fusion.28
  276.2 10.0 %all-gather.3.cloned.1.call-done = bf16[1,4096,4096]{2,1,0:T(8,128)(2,1)} async-done(((bf16[1,4096,256]{2,1,0:T(8,128)(2,1)}), bf16[1,4096,4096]{2,1,0:T(8,128)(2,1)}) %all-gather.3.cloned.1.call-update) | async-done | bytes 33554448 | tf_op jit(solution)/shard_map/all_gather | solution.py:105
  286.1 0.0 copy-start.1
  286.1 16.7 %fusion.11 = bf16[1,256,4096]{2,1,0:T(8,128)(2,1)} fusion(bf16[256,4096]{1,0:T(8,128)(2,1)} %fusion.28, bf16[1,4096,4096]{2,1,0:T(8,128)(2,1)} %all-gather.3.cloned.1.call-done), kind=kOutput, calls=%fused_computation.14 | convolution fusion | flops 8590983168 | bytes 37748736 | tf_op jit(solution)/shard_map/dot_general | solution.py:103
  302.9 0.0 copy-done.1
  (16 shorter events, 0.2 us)
Async XLA Ops:
  6.5 79.0 %copy-start = (bf16[256,4096]{1,0:T(8,128)(2,1)S(1)}, bf16[256,4096]{1,0:T(8,128)(2,1)}, u32[]{:S(2)}) copy-start(bf16[256,4096]{1,0:T(8,128)(2,1)} %param.10) | copy-start | bytes 6291460
  6.5 279.6 %all-gather.3.cloned.1.call-start = ((), (), s32[]{:S(2)}) async-start(), calls=%async_computation.5 | async-start | bytes 35651584 | tf_op jit(solution)/shard_map/all_gather | solution.py:105
  53.8 1.4 copy-start.3
  57.5 20.7 %all-to-all-start.2 = ((bf16[16,256,4]{1,2,0:T(4,128)(2,1)}), bf16[16,256,4]{1,2,0:T(4,128)(2,1)S(1)}, u32[]{:S(2)}, u32[]{:S(2)}) async-start(bf16[16,256,4]{1,2,0:T(4,128)(2,1)} %bitcast.6), calls=%async_computation.2 | async-start | bytes 65536 | tf_op jit(solution)/shard_map/all_to_all | solution.py:50
  78.2 88.9 %all-to-all-start.1 = ((bf16[16,256,512]{2,1,0:T(8,128)(2,1)}), bf16[16,256,512]{2,1,0:T(8,128)(2,1)}, u32[]{:S(2)}, u32[]{:S(2)}) async-start(bf16[16,256,512]{2,1,0:T(8,128)(2,1)} %pad_maximum_fusion), calls=%async_computation.1 | async-start | bytes 8388608 | tf_op jit(solution)/shard_map/all_to_all | solution.py:48
  85.5 2.0 copy-start.6
  167.2 34.0 %all-to-all-start.4 = ((bf16[8,32,4096]{2,1,0:T(8,128)(2,1)}), bf16[8,32,4096]{2,1,0:T(8,128)(2,1)S(1)}, u32[]{:S(2)}, u32[]{:S(2)}) async-start(bf16[8,32,4096]{2,1,0:T(8,128)(2,1)} %broadcast_select_fusion.1), calls=%async_computation.4 | async-start | bytes 4194304 | tf_op jit(solution)/shard_map/all_to_all | solution.py:31
  186.3 3.6 %copy-start.4 = (bf16[16,256,256]{1,2,0:T(8,128)(2,1)S(1)}, bf16[16,256,256]{1,2,0:T(8,128)(2,1)}, u32[]{:S(2)}) copy-start(bf16[16,256,256]{1,2,0:T(8,128)(2,1)} %copy.68) | copy-start | bytes 6291460
  201.1 61.2 %all-to-all-start.3 = ((bf16[16,256,256]{2,1,0:T(8,128)(2,1)}), bf16[16,256,256]{2,1,0:T(8,128)(2,1)}, u32[]{:S(2)}, u32[]{:S(2)}) async-start(bf16[16,256,256]{2,1,0:T(8,128)(2,1)} %copy.80), calls=%async_computation.3 | async-start | bytes 4194304 | tf_op jit(solution)/shard_map/all_to_all | solution.py:89
  265.2 3.9 %copy-start.2 = (f32[32,8,16,256]{3,2,1,0:T(8,128)S(1)}, f32[32,8,16,256]{3,2,1,0:T(8,128)}, u32[]{:S(2)}) copy-start(f32[32,8,16,256]{3,2,1,0:T(8,128)} %copy.91) | copy-start | bytes 12582916
  269.1 4.0 %copy-start.5 = (f32[1,4096]{1,0:T(1,128)S(1)}, f32[1,4096]{1,0:T(1,128)}, u32[]{:S(2)}) copy-start(f32[1,4096]{1,0:T(1,128)} %param.16) | copy-start | bytes 49156
  286.1 16.8 %copy-start.1 = (bf16[256,4096]{1,0:T(8,128)(2,1)S(1)}, bf16[256,4096]{1,0:T(8,128)(2,1)}, u32[]{:S(2)}) copy-start(bf16[256,4096]{1,0:T(8,128)(2,1)} %param.10) | copy-start | bytes 6291460
Sparse Core Ops, SparseCore 0:
  9.4 276.6 all-gather.2

commit v6 on v5

--- a/solution.py
+++ b/solution.py
@@ -86,13 +86,21 @@
         + skip[None, None, :, None] * xc.astype(jnp.float32)
     )
 
-    ys = lax.all_to_all(
-        ys.reshape(shards, rows, local).astype(jnp.bfloat16),
+    amax = jnp.max(jnp.abs(ys), axis=-1, keepdims=True)
+    scale = amax / 32767.0
+    coded = jnp.clip(jnp.round(ys / jnp.where(scale > 0, scale, 1.0)), -32767.0, 32767.0)
+    coded = lax.all_to_all(
+        coded.astype(jnp.int16).reshape(shards, rows, local),
         "seq",
         split_axis=0,
         concat_axis=0,
         tiled=True,
-    ).astype(jnp.float32)
+    )
+    scale = lax.all_to_all(
+        scale.reshape(shards, rows, lheads), "seq", split_axis=0, concat_axis=0, tiled=True
+    )
+    ys = coded.reshape(shards, rows, lheads, hsize).astype(jnp.float32) * scale[..., None]
+    ys = ys.reshape(shards, rows, local)
     ys = jnp.transpose(ys, (1, 0, 2)).reshape(rows, width)
     gated = ys * jax.nn.silu(zs.astype(jnp.float32))
     normed = (

time: 312 us -> 314 us (level)
  waiting for transfers between devices: 126 us -> 115 us
  local copies, waits for them, and re-layouts: 42.5 us -> 48.6 us
  starting transfers between devices: 34.4 us -> 38.6 us
    all_to_all x1 -> x2, waiting for transfers between devices: 43.1 us -> 32.3 us  [the longest x1 28.6 us: per_device(): lax.all_to_all(coded.astype(jnp.int16).reshape(shards, rows, local), 'seq...]
    convert_element_type x1 -> x2, local copies, waits for them, and re-layouts: 3.92 us -> 11 us  [per_device(): gated = ys * jax.nn.silu(zs.astype(jnp.float32))]
    convert_element_type x0 -> x2, other arithmetic: none -> 6.44 us  [the longest x1 4.28 us: per_device(): coded.astype(jnp.int16).reshape(shards, rows, local)]
    all_to_all x1 -> x2, starting transfers between devices: 15.4 us -> 19.6 us  [the longest x1 15.7 us: per_device(): lax.all_to_all(scale.reshape(shards, rows, lheads), 'seq', split_axis=0,...]
    unnamed x17 -> x22, local copies, waits for them, and re-layouts: 8.81 us -> 7.86 us
  transfers between devices with their start and end apart: 5 -> 6, of which waited for: 3 -> 5; matrix products, arithmetic and copies ran while one was open for 27% -> 29% of each run, Pallas kernels for 0% -> 0%
where the time goes in v6:
time: 314 us; the launch traced here: 310 us
  waiting for transfers between devices  115 us (37%)
  local copies, waits for them, and re-layouts  48.6 us (15%)
  starting transfers between devices  38.6 us (12%)
  matrix products  35.6 us (11%)
  blocking collectives  33.7 us (11%)
  other arithmetic  25.1 us (8%)
  between operations  13.7 us (4%)
    all_to_all x1, waiting for transfers between devices, per_device(): xbc = lax.all_to_all(xbc, 'seq', split_axis=0, concat_axis=0, tiled=True)  72.6 us
    all_to_all x1, blocking collectives, per_device(): lax.all_to_all(arrange(packed), 'dom', split_axis=0, concat_axis=0, tiled...  33.7 us
    all_to_all x1, waiting for transfers between devices, per_device(): lax.all_to_all(coded.astype(jnp.int16).reshape(shards, rows, local), 'seq...  28.6 us
    dot_general x1, matrix products, per_device(): jnp.dot(normed, lax.all_gather(out_weight[0], 'seq', axis=1, tiled=True),...  16.8 us
    all_to_all x1, starting transfers between devices, per_device(): lax.all_to_all(scale.reshape(shards, rows, lheads), 'seq', split_axis=0,...  15.7 us
    convert_element_type x2, local copies, waits for them, and re-layouts, per_device(): gated = ys * jax.nn.silu(zs.astype(jnp.float32))  11 us
    all_gather x1, waiting for transfers between devices, per_device(): lax.all_gather(out_weight[0], 'seq', axis=1, tiled=True)  8.7 us
    all_to_all x1, starting transfers between devices, per_device(): lsh = lax.all_to_all(lsh, 'seq', split_axis=0, concat_axis=0, tiled=True)  7.91 us
  transfers between devices with their start and end apart: 6, of which 5 were waited for; matrix products, arithmetic and copies ran while one was open for 29% of the time, Pallas kernels for 0%

profile of v6, /device:TPU:0, one launch (start us, length us, event | category | flops | bytes accessed | tf_op | source)
XLA Modules:
  0.0 310.4 jit_solution(3656912647812934547)
XLA Ops:
  6.5 0.0 copy-start
  6.5 0.0 all-gather.3.cloned.1.call-start
  6.5 0.7 all-gather.3.cloned.1.call-update
  7.3 0.9 copy.53
  8.1 1.6 sort.17
  9.8 4.5 %concatenate.6 = bf16[256,4480]{1,0:T(8,128)(2,1)} concatenate(bf16[256,4096]{1,0:T(8,128)(2,1)} %param.9, bf16[256,128]{1,0:T(8,128)(2,1)} %param.11, bf16[256,128]{1,0:T(8,128)(2,1)} %param.12, bf16[256,64]{1,0:T(8,128)(2,1)S(1)} %copy.53, bf16[256,64]{1,0:T(8,128)(2,1)S(1)} %broadcast_in_dim.52), dimensions={1} | concatenate | bytes 4587520 | tf_op jit(solution)/shard_map/concatenate | solution.py:26
  14.3 3.9 %gather_fusion = bf16[8,32,4480]{2,1,0:T(8,128)(2,1)} fusion(bf16[8,32,4480]{2,1,0:T(8,128)(2,1)} %bitcast.95, s32[1024]{0:T(1024)S(1)} %pad_clamp_fusion), kind=kCustom, calls=%fused_computation | custom fusion | bytes 4587552 | tf_op jit(solution)/shard_map/jit(_take)/gather | solution.py:23
  18.2 1.9 broadcast_select_fusion
  20.1 33.7 %all_to_all.30 = bf16[8,32,4480]{2,1,0:T(8,128)(2,1)S(1)} all-to-all(bf16[8,32,4480]{2,1,0:T(8,128)(2,1)S(1)} %broadcast_select_fusion), channel_id=1, replica_groups=mesh['dom'=8,'seq'=16] {'dom'}, dimensions={0} | all-to-all | bytes 4587520 | tf_op jit(solution)/shard_map/all_to_all | solution.py:29
  53.8 1.4 copy-done.5
  55.2 1.6 slice.44
  56.8 0.1 copy.57
  56.9 0.6 reshape.161
  57.5 7.9 %all-to-all-start.2 = ((bf16[16,256,4]{1,2,0:T(4,128)(2,1)}), bf16[16,256,4]{1,2,0:T(4,128)(2,1)S(1)}, u32[]{:S(2)}, u32[]{:S(2)}) async-start(bf16[16,256,4]{1,2,0:T(4,128)(2,1)} %bitcast.6), calls=%async_computation.2 | async-start | bytes 65536 | tf_op jit(solution)/shard_map/all_to_all | solution.py:50
  65.4 4.1 %copy.54 = bf16[256,4096]{0,1:T(8,128)(2,1)} copy(bf16[256,4096]{1,0:T(8,128)(2,1)} %slice.44) | data formatting | bytes 4194304 | tf_op jit(solution)/shard_map/slice | solution.py:33
  69.5 3.9 %copy.55 = bf16[256,16,256]{2,0,1:T(8,128)(2,1)} copy(bf16[256,16,256]{0,2,1:T(8,128)(2,1)} %bitcast.97) | data formatting | bytes 4194304 | tf_op jit(solution)/shard_map/reshape | solution.py:42
  73.4 0.9 fusion.48
  74.3 0.2 broadcast_in_dim.56
  74.5 0.2 broadcast_in_dim.57
  74.7 3.5 %pad_maximum_fusion = bf16[16,256,512]{2,1,0:T(8,128)(2,1)} fusion(bf16[16,256,128]{2,1,0:T(8,128)(2,1)S(1)} %broadcast_in_dim.57, bf16[16,256,128]{2,1,0:T(8,128)(2,1)S(1)} %broadcast_in_dim.56, bf16[16,256,256]{2,1,0:T(8,128)(2,1)} %bitcast.100), kind=kLoop, calls=%fused_computation.17 | loop fusion | flops 12582912 | bytes 8388608 | tf_op jit(solution)/shard_map/concatenate | solution.py:40
  78.2 0.0 all-to-all-done.2
  78.2 7.3 %all-to-all-start.1 = ((bf16[16,256,512]{2,1,0:T(8,128)(2,1)}), bf16[16,256,512]{2,1,0:T(8,128)(2,1)}, u32[]{:S(2)}, u32[]{:S(2)}) async-start(bf16[16,256,512]{2,1,0:T(8,128)(2,1)} %pad_maximum_fusion), calls=%async_computation.1 | async-start | bytes 8388608 | tf_op jit(solution)/shard_map/all_to_all | solution.py:48
  85.5 0.0 copy-start.9
  85.5 0.0 copy-done
  85.5 2.0 gather_fusion.1
  87.5 0.1 dynamic-slice_bitcast_fusion
  87.6 3.3 %broadcast_select_fusion.1 = bf16[8,32,4096]{2,1,0:T(8,128)(2,1)} fusion(bf16[8,32,4096]{2,1,0:T(8,128)(2,1)} %gather_fusion.1, pred[8]{0:T(512)(128)(4,1)S(1)} %compare_and_fusion), kind=kLoop, calls=%fused_computation.36 | loop fusion | flops 1048576 | bytes 4194312 | tf_op jit(solution)/shard_map/jit(_take)/select_n | solution.py:23
  90.9 0.1 reshape.194
  91.0 2.3 reduce-window.6
  93.3 0.2 slice_reduce_fusion
  93.5 0.1 copy_bitcast_fusion
  93.6 0.2 slice_reduce_fusion.1
  93.7 0.1 bitcast_exponential_fusion
  94.0 0.6 fusion.33
  94.6 72.6 %all-to-all-done.1 = bf16[16,256,512]{2,1,0:T(8,128)(2,1)} async-done(((bf16[16,256,512]{2,1,0:T(8,128)(2,1)}), bf16[16,256,512]{2,1,0:T(8,128)(2,1)}, u32[]{:S(2)}, u32[]{:S(2)}) %all-to-all-start.1) | async-done | bytes 4194336 | tf_op jit(solution)/shard_map/all_to_all | solution.py:48
  167.2 3.8 %all-to-all-start.5 = ((bf16[8,32,4096]{2,1,0:T(8,128)(2,1)}), bf16[8,32,4096]{2,1,0:T(8,128)(2,1)S(1)}, u32[]{:S(2)}, u32[]{:S(2)}) async-start(bf16[8,32,4096]{2,1,0:T(8,128)(2,1)} %broadcast_select_fusion.1), calls=%async_computation.5 | async-start | bytes 4194304 | tf_op jit(solution)/shard_map/all_to_all | solution.py:31
  171.0 3.2 %slice.47 = bf16[16,256,256]{2,1,0:T(8,128)(2,1)} slice(bf16[16,256,512]{2,1,0:T(8,128)(2,1)} %all-to-all-done.1), slice={[0:16], [0:256], [0:256]} | slice | bytes 4194304 | tf_op jit(solution)/shard_map/slice | solution.py:53
  174.2 4.0 %copy.56 = bf16[16,256,256]{1,2,0:T(8,128)(2,1)} copy(bf16[16,256,256]{2,1,0:T(8,128)(2,1)} %slice.47) | data formatting | bytes 4194304 | tf_op jit(solution)/shard_map/slice | solution.py:53
  178.1 2.7 fusion.21
  180.8 3.1 fusion.28
  183.9 3.5 %fusion.23 = f32[16,256,4,64]{1,3,2,0:T(8,128)S(1)} fusion(f32[16,4,64,128]{3,0,2,1:T(8,128)S(1)} %fusion.28, bf16[16,256,512]{2,1,0:T(8,128)(2,1)} %all-to-all-done.1), kind=kOutput, calls=%fused_computation.31 | convolution fusion | flops 1610612736 | bytes 7340032 | tf_op jit(solution)/shard_map/cin,chpn->cihp/dot_general | solution.py:79
  187.4 0.0 copy-start.7
  187.4 2.5 fusion.37
  189.9 0.0 copy-done.7
  189.9 6.5 %abs_reduce_fusion = (f32[16,256,4]{1,2,0:T(4,128)S(1)}, f32[16,256,4,64]{1,3,2,0:T(8,128)}) fusion(bf16[16,256,4,64]{1,3,2,0:T(8,128)(2,1)S(1)} %bitcast.99, f32[4]{0:T(128)S(1)} %dynamic-slice_bitcast_fusion, f32[16,256,4,64]{1,3,2,0:T(8,128)S(1)} %fusion.23, f32[16,256,4]{1,2,0:T(4,128)S(1)} %copy.63, f32[16,4,256]{2,1,0:T(4,128)S(1)} %copy.61, ...), kind=kOutput, calls=%fused_computation.28 | convolution fusion | flops 565166080 | bytes 14942224 | tf_op jit(solution)/shard_map/chij,cjhp->cihp/dot_general | solution.py:64
  196.4 0.6 broadcast_multiply_fusion
  197.1 0.8 all-to-all-done.5
  197.9 15.7 %all-to-all-start.4 = ((f32[16,256,4]{1,2,0:T(4,128)}), f32[16,256,4]{1,2,0:T(4,128)S(1)}, u32[]{:S(2)}, u32[]{:S(2)}) async-start(f32[16,256,4]{1,2,0:T(4,128)} %get-tuple-element.9), calls=%async_computation.4 | async-start | bytes 131072 | tf_op jit(solution)/shard_map/all_to_all | solution.py:99
  213.6 4.3 %clamp_convert_fusion = s16[16,256,4,64]{1,3,2,0:T(8,128)(2,1)} fusion(f32[16,256,4,64]{1,3,2,0:T(8,128)} %get-tuple-element.16, f32[16,256,4]{1,2,0:T(4,128)S(1)} %get-tuple-element.10), kind=kLoop, calls=%fused_computation.27 | loop fusion | flops 4194304 | bytes 6356992 | tf_op jit(solution)/shard_map/convert_element_type | solution.py:93
  217.8 3.7 %all-to-all-done.4 = f32[16,256,4]{1,2,0:T(4,128)S(1)} async-done(((f32[16,256,4]{1,2,0:T(4,128)}), f32[16,256,4]{1,2,0:T(4,128)S(1)}, u32[]{:S(2)}, u32[]{:S(2)}) %all-to-all-start.4) | async-done | bytes 65568 | tf_op jit(solution)/shard_map/all_to_all | solution.py:99
  221.6 4.0 %all-to-all-start.3 = ((s16[16,256,256]{1,2,0:T(8,128)(2,1)}), s16[16,256,256]{1,2,0:T(8,128)(2,1)S(1)}, u32[]{:S(2)}, u32[]{:S(2)}) async-start(s16[16,256,256]{1,2,0:T(8,128)(2,1)} %bitcast.96), calls=%async_computation.3 | async-start | bytes 4194304 | tf_op jit(solution)/shard_map/all_to_all | solution.py:92
  225.5 2.2 convert_element_type.49
  227.7 3.7 %copy.80 = f32[32,8,16,256]{3,2,1,0:T(8,128)} copy(f32[32,8,16,256]{3,1,2,0:T(8,128)S(1)} %bitcast.89) | data formatting | bytes 8388608
  231.4 5.4 %copy.71 = f32[256,16,256]{0,2,1:T(8,128)} copy(f32[256,16,256]{2,1,0:T(8,128)} %bitcast.91) | data formatting | bytes 8388608 | tf_op jit(solution)/shard_map/convert_element_type | solution.py:105
  236.8 5.6 %copy.69 = f32[256,4096]{0,1:T(8,128)} copy(f32[256,4096]{1,0:T(8,128)} %bitcast.90) | data formatting | bytes 8388608 | tf_op jit(solution)/shard_map/convert_element_type | solution.py:105
  242.4 28.6 %all-to-all-done.3 = s16[16,256,256]{1,2,0:T(8,128)(2,1)S(1)} async-done(((s16[16,256,256]{1,2,0:T(8,128)(2,1)}), s16[16,256,256]{1,2,0:T(8,128)(2,1)S(1)}, u32[]{:S(2)}, u32[]{:S(2)}) %all-to-all-start.3) | async-done | bytes 2097184 | tf_op jit(solution)/shard_map/all_to_all | solution.py:92
  271.0 0.7 bitcast_multiply_fusion.2
  271.7 1.5 copy-done.4
  273.2 1.8 fusion.20
  275.0 0.4 copy-done.3
  275.4 0.0 copy-done.8
  275.4 2.7 fusion.18
  278.1 8.7 %all-gather.3.cloned.1.call-done = bf16[1,4096,4096]{2,1,0:T(8,128)(2,1)} async-done(((bf16[1,4096,256]{2,1,0:T(8,128)(2,1)}), bf16[1,4096,4096]{2,1,0:T(8,128)(2,1)}) %all-gather.3.cloned.1.call-update) | async-done | bytes 33554448 | tf_op jit(solution)/shard_map/all_gather | solution.py:113
  286.8 16.8 %fusion.11 = bf16[1,256,4096]{2,1,0:T(8,128)(2,1)} fusion(bf16[256,4096]{0,1:T(8,128)(2,1)} %fusion.18, bf16[1,4096,4096]{2,1,0:T(8,128)(2,1)} %all-gather.3.cloned.1.call-done), kind=kOutput, calls=%fused_computation.14 | convolution fusion | flops 8590983168 | bytes 37748736 | tf_op jit(solution)/shard_map/dot_general | solution.py:111
  (27 shorter events, 0.3 us)
Async XLA Ops:
  6.5 79.0 %copy-start = (bf16[256,4096]{1,0:T(8,128)(2,1)S(1)}, bf16[256,4096]{1,0:T(8,128)(2,1)}, u32[]{:S(2)}) copy-start(bf16[256,4096]{1,0:T(8,128)(2,1)} %param.10) | copy-start | bytes 6291460
  6.5 280.3 %all-gather.3.cloned.1.call-start = ((), (), s32[]{:S(2)}) async-start(), calls=%async_computation.6 | async-start | bytes 35651584 | tf_op jit(solution)/shard_map/all_gather | solution.py:113
  53.8 1.4 copy-start.5
  57.5 20.7 %all-to-all-start.2 = ((bf16[16,256,4]{1,2,0:T(4,128)(2,1)}), bf16[16,256,4]{1,2,0:T(4,128)(2,1)S(1)}, u32[]{:S(2)}, u32[]{:S(2)}) async-start(bf16[16,256,4]{1,2,0:T(4,128)(2,1)} %bitcast.6), calls=%async_computation.2 | async-start | bytes 65536 | tf_op jit(solution)/shard_map/all_to_all | solution.py:50
  78.2 89.0 %all-to-all-start.1 = ((bf16[16,256,512]{2,1,0:T(8,128)(2,1)}), bf16[16,256,512]{2,1,0:T(8,128)(2,1)}, u32[]{:S(2)}, u32[]{:S(2)}) async-start(bf16[16,256,512]{2,1,0:T(8,128)(2,1)} %pad_maximum_fusion), calls=%async_computation.1 | async-start | bytes 8388608 | tf_op jit(solution)/shard_map/all_to_all | solution.py:48
  85.5 2.0 copy-start.9
  167.2 30.7 %all-to-all-start.5 = ((bf16[8,32,4096]{2,1,0:T(8,128)(2,1)}), bf16[8,32,4096]{2,1,0:T(8,128)(2,1)S(1)}, u32[]{:S(2)}, u32[]{:S(2)}) async-start(bf16[8,32,4096]{2,1,0:T(8,128)(2,1)} %broadcast_select_fusion.1), calls=%async_computation.5 | async-start | bytes 4194304 | tf_op jit(solution)/shard_map/all_to_all | solution.py:31
  187.4 2.5 copy-start.7
  197.9 23.7 %copy-start.6 = (bf16[8,32,4096]{2,1,0:T(8,128)(2,1)}, bf16[8,32,4096]{2,1,0:T(8,128)(2,1)S(1)}, u32[]{:S(2)}) copy-start(bf16[8,32,4096]{2,1,0:T(8,128)(2,1)S(1)} %all-to-all-done.5) | copy-start | bytes 6291460
  197.9 23.7 %all-to-all-start.4 = ((f32[16,256,4]{1,2,0:T(4,128)}), f32[16,256,4]{1,2,0:T(4,128)S(1)}, u32[]{:S(2)}, u32[]{:S(2)}) async-start(f32[16,256,4]{1,2,0:T(4,128)} %get-tuple-element.9), calls=%async_computation.4 | async-start | bytes 131072 | tf_op jit(solution)/shard_map/all_to_all | solution.py:99
  221.6 49.4 %all-to-all-start.3 = ((s16[16,256,256]{1,2,0:T(8,128)(2,1)}), s16[16,256,256]{1,2,0:T(8,128)(2,1)S(1)}, u32[]{:S(2)}, u32[]{:S(2)}) async-start(s16[16,256,256]{1,2,0:T(8,128)(2,1)} %bitcast.96), calls=%async_computation.3 | async-start | bytes 4194304 | tf_op jit(solution)/shard_map/all_to_all | solution.py:92
  227.7 3.7 %copy-start.2 = (f32[8,32,4096]{2,1,0:T(8,128)}, f32[8,32,4096]{2,1,0:T(8,128)S(1)}, u32[]{:S(2)}) copy-start(f32[8,32,4096]{2,1,0:T(8,128)S(1)} %convert_element_type.49) | copy-start | bytes 12582916
  271.0 2.2 copy-start.4
  273.2 2.2 copy-start.3
  273.2 2.2 copy-start.8
  286.8 16.8 %copy-start.1 = (bf16[256,4096]{1,0:T(8,128)(2,1)S(1)}, bf16[256,4096]{1,0:T(8,128)(2,1)}, u32[]{:S(2)}) copy-start(bf16[256,4096]{1,0:T(8,128)(2,1)} %param.10) | copy-start | bytes 6291460
Sparse Core Ops, SparseCore 0:
  9.4 277.3 all-gather.2

commit v7 on v4

--- a/solution.py
+++ b/solution.py
@@ -1,16 +1,34 @@
 import jax
 import jax.numpy as jnp
+import numpy as np
 from jax import lax
+from jax.sharding import Mesh
 from jax.sharding import PartitionSpec as P
 
 SPAN = 256
+SEQ = ("sx", "sz")
+
+
+def code16(values, axis_name):
+    amax = jnp.max(jnp.abs(values), axis=-1, keepdims=True)
+    scale = amax / 32767.0
+    coded = jnp.clip(jnp.round(values / jnp.where(scale > 0, scale, 1.0)), -32767.0, 32767.0)
+    lead = values.shape[:2]
+    coded = lax.all_to_all(
+        coded.astype(jnp.int16).reshape(*lead, -1), axis_name, split_axis=0, concat_axis=0, tiled=True
+    )
+    scale = lax.all_to_all(
+        scale.reshape(*lead, -1), axis_name, split_axis=0, concat_axis=0, tiled=True
+    )
+    return coded.reshape(values.shape).astype(jnp.float32) * scale[..., None]
 
 
 def per_device(
     tokens_x, gate_z, in_b, in_c, log_decay, domain_ids, out_weight, norm_gain, skip_gain
 ):
     groups = lax.axis_size("dom")
-    shards = lax.axis_size("seq")
+    nx = lax.axis_size("sx")
+    nz = lax.axis_size("sz")
     rows = tokens_x.shape[0]
     seg_rows = rows // groups
     width = tokens_x.shape[1]
@@ -35,21 +53,21 @@
     cs = packed[:, width + nstate : width + 2 * nstate]
     ls = packed[:, width + 2 * nstate : width + 2 * nstate + heads]
 
-    local = width // shards
-    lheads = heads // shards
+    local = width // nz
+    lheads = heads // nz
     xbc = jnp.concatenate(
         [
-            jnp.transpose(xs.reshape(rows, shards, local), (1, 0, 2)),
-            jnp.broadcast_to(bs[None], (shards, rows, nstate)),
-            jnp.broadcast_to(cs[None], (shards, rows, nstate)),
+            jnp.transpose(xs.reshape(rows, nz, local), (1, 0, 2)),
+            jnp.broadcast_to(bs[None], (nz, rows, nstate)),
+            jnp.broadcast_to(cs[None], (nz, rows, nstate)),
         ],
         axis=2,
     )
-    xbc = lax.all_to_all(xbc, "seq", split_axis=0, concat_axis=0, tiled=True)
-    lsh = jnp.transpose(ls.reshape(rows, shards, lheads), (1, 0, 2))
-    lsh = lax.all_to_all(lsh, "seq", split_axis=0, concat_axis=0, tiled=True)
+    xbc = lax.all_to_all(xbc, "sz", split_axis=0, concat_axis=0, tiled=True)
+    lsh = jnp.transpose(ls.reshape(rows, nz, lheads), (1, 0, 2))
+    lsh = lax.all_to_all(lsh, "sz", split_axis=0, concat_axis=0, tiled=True)
 
-    blocks = shards * rows // SPAN
+    blocks = nz * rows // SPAN
     xc = xbc[:, :, :local].reshape(blocks, SPAN, lheads, hsize)
     bc = xbc[:, :, local : local + nstate].reshape(blocks, SPAN, nstate)
     cc = xbc[:, :, local + nstate :].reshape(blocks, SPAN, nstate)
@@ -68,27 +86,48 @@
     )
     block_state = jnp.einsum("cjhp,cjn->chpn", decayed, bc, preferred_element_type=jnp.float32)
 
-    idx = jnp.arange(blocks)
-    between = (idx[None, :, None] < idx[None, None, :]) & (idx[None, None, :] < idx[:, None, None])
+    kdx = jnp.arange(blocks + 1)
+    jdx = jnp.arange(blocks)
+    between = (jdx[None, :, None] < jdx[None, None, :]) & (jdx[None, None, :] < kdx[:, None, None])
     gaps = jnp.einsum(
         "kji,ih->hkj", between.astype(jnp.float32), totals, precision=lax.Precision.HIGHEST
     )
-    earlier = idx[None, :] < idx[:, None]
+    earlier = jdx[None, :] < kdx[:, None]
     carry = jnp.where(earlier[None], jnp.exp(jnp.minimum(gaps, 0.0)), 0.0)
     before = jnp.einsum("hkj,jhpn->khpn", carry, block_state, precision=lax.Precision.HIGHEST)
+    local_end = before[blocks]
+    before = before[:blocks]
+    shard_total = jnp.sum(totals, axis=0)
+
+    slab = jnp.pad(shard_total, (0, hsize - lheads))
+    ends = jnp.concatenate(
+        [local_end, jnp.broadcast_to(slab[None, :, None], (1, hsize, nstate))], axis=0
+    )
+    ends = lax.all_to_all(
+        jnp.broadcast_to(ends[None], (nx,) + ends.shape), "sx", split_axis=0, concat_axis=0, tiled=True
+    )
+    end_states = ends[:, :lheads]
+    end_totals = ends[:, lheads, :lheads, 0]
+    me = lax.axis_index("sx")
+    xdx = jnp.arange(nx)
+    inside = ((xdx[:, None] < xdx[None, :]) & (xdx[None, :] < me)).astype(jnp.float32)
+    gap_x = jnp.einsum("ji,ih->jh", inside, end_totals, precision=lax.Precision.HIGHEST)
+    weight_x = jnp.where((xdx < me)[:, None], jnp.exp(jnp.minimum(gap_x, 0.0)), 0.0)
+    incoming = jnp.einsum("jh,jhpn->hpn", weight_x, end_states, precision=lax.Precision.HIGHEST)
+    prefix = jnp.cumsum(totals, axis=0) - totals
+    before = before + jnp.exp(prefix)[:, :, None, None] * incoming[None]
+
     carried = jnp.einsum(
         "cin,chpn->cihp", cc.astype(jnp.float32), before, precision=lax.Precision.HIGHEST
     )
-    skip = lax.dynamic_slice_in_dim(skip_gain[0], lax.axis_index("seq") * lheads, lheads)
+    skip = lax.dynamic_slice_in_dim(skip_gain[0], lax.axis_index("sz") * lheads, lheads)
     ys = (
         inner
         + jnp.exp(cum)[..., None] * carried
         + skip[None, None, :, None] * xc.astype(jnp.float32)
     )
 
-    ys = lax.all_to_all(
-        ys.reshape(shards, rows, local), "seq", split_axis=0, concat_axis=0, tiled=True
-    )
+    ys = code16(ys, "sz").reshape(nz, rows, local)
     ys = jnp.transpose(ys, (1, 0, 2)).reshape(rows, width)
     gated = ys * jax.nn.silu(zs.astype(jnp.float32))
     normed = (
@@ -98,25 +137,32 @@
     ).astype(jnp.bfloat16)
     mixed = jnp.dot(
         normed,
-        lax.all_gather(out_weight[0], "seq", axis=1, tiled=True),
+        lax.all_gather(out_weight[0], SEQ, axis=1, tiled=True),
         preferred_element_type=jnp.float32,
     ).astype(jnp.bfloat16)
     return mixed.reshape(1, rows, mixed.shape[-1])
 
 
 def solution(mesh):
+    shards = mesh.shape["seq"]
+    inner = 4 if shards % 4 == 0 else shards
+    split = Mesh(
+        np.asarray(mesh.devices).reshape(mesh.shape["dom"], shards // inner, inner),
+        ("dom",) + SEQ,
+    )
+    rows = P(("dom",) + SEQ, None)
     in_specs = (
-        P(("dom", "seq"), None),
-        P(("dom", "seq"), None),
-        P(("dom", "seq"), None),
-        P(("dom", "seq"), None),
-        P(("dom", "seq"), None),
-        P("dom", "seq", None),
-        P("dom", None, "seq"),
+        rows,
+        rows,
+        rows,
+        rows,
+        rows,
+        P("dom", SEQ, None),
+        P("dom", None, SEQ),
         P("dom", None),
         P("dom", None),
     )
-    out_specs = P("dom", "seq", None)
+    out_specs = P("dom", SEQ, None)
     return jax.shard_map(
-        per_device, mesh=mesh, in_specs=in_specs, out_specs=out_specs, check_vma=False
+        per_device, mesh=split, in_specs=in_specs, out_specs=out_specs, check_vma=False
     )

time: 348 us -> 317 us (0.911); the launches traced: 342 us -> 316 us
  waiting for transfers between devices: 160 us -> 123 us
  local copies, waits for them, and re-layouts: 43.4 us -> 51.7 us
  starting transfers between devices: 34.4 us -> 26.5 us
  other arithmetic: 21.3 us -> 28 us
  matrix products: 35.5 us -> 39.6 us
    all_to_all x3 -> x5, waiting for transfers between devices: 159 us -> 113 us  [the longest x1 55.5 us: per_device(): xbc = lax.all_to_all(xbc, 'sz', split_axis=0, concat_axis=0, tiled=True)]
    convert_element_type x0 -> x3, local copies, waits for them, and re-layouts: none -> 15.3 us  [per_device(): gated = ys * jax.nn.silu(zs.astype(jnp.float32))]
    all_to_all x1, waiting for transfers between devices: 0.01 us -> 8.77 us  [per_device(): lax.all_to_all(arrange(gate_z), 'dom', split_axis=0, concat_axis=0, tiled...]
    all_to_all x3 -> x5, starting transfers between devices: 30.6 us -> 22.7 us  [the longest x1 5.32 us: per_device(): lsh = lax.all_to_all(lsh, 'sz', split_axis=0, concat_axis=0, tiled=True)]
    convert_element_type x0 -> x2, other arithmetic: none -> 6.62 us  [the longest x1 4.2 us: code16(): coded.astype(jnp.int16).reshape(*lead, -1)]
    reshape x3 -> x1, local copies, waits for them, and re-layouts: 9.91 us -> 3.94 us  [per_device(): xs.reshape(rows, nz, local)]
    dot_general x1 -> x3, matrix products: 16.7 us -> 21.1 us  [the longest x1 16.8 us: per_device(): jnp.dot(normed, lax.all_gather(out_weight[0], SEQ, axis=1, tiled=True), p...]
    unnamed x17 -> x23, local copies, waits for them, and re-layouts: 8.26 us -> 4.71 us
  transfers between devices with their start and end apart: 5 -> 7, of which waited for: 2 -> 5; matrix products, arithmetic and copies ran while one was open for 24% -> 31% of each run, Pallas kernels for 0% -> 0%
where the time goes in v7:
time: 317 us; the launch traced here: 316 us
  waiting for transfers between devices  123 us (39%)
  local copies, waits for them, and re-layouts  51.7 us (16%)
  matrix products  39.6 us (12%)
  blocking collectives  33.7 us (11%)
  other arithmetic  28 us (9%)
  starting transfers between devices  26.5 us (8%)
  between operations  13.7 us (4%)
    all_to_all x1, waiting for transfers between devices, per_device(): xbc = lax.all_to_all(xbc, 'sz', split_axis=0, concat_axis=0, tiled=True)  55.5 us
    all_to_all x1, waiting for transfers between devices, per_device(): lax.all_to_all(jnp.broadcast_to(ends[None], (nx,) + ends.shape), 'sx', sp...  49 us
    all_to_all x1, blocking collectives, per_device(): lax.all_to_all(arrange(packed), 'dom', split_axis=0, concat_axis=0, tiled...  33.7 us
    dot_general x1, matrix products, per_device(): jnp.dot(normed, lax.all_gather(out_weight[0], SEQ, axis=1, tiled=True), p...  16.8 us
    convert_element_type x3, local copies, waits for them, and re-layouts, per_device(): gated = ys * jax.nn.silu(zs.astype(jnp.float32))  15.3 us
    all_to_all x1, waiting for transfers between devices, per_device(): lax.all_to_all(arrange(gate_z), 'dom', split_axis=0, concat_axis=0, tiled...  8.77 us
    all_to_all x1, waiting for transfers between devices, code16(): lax.all_to_all(coded.astype(jnp.int16).reshape(*lead, -1), axis_name, spl...  7.35 us
    dot_general x1, matrix products, per_device(): jnp.einsum('chij,cjhp->cihp', weights, xc, preferred_element_type=jnp.flo...  6.51 us
  transfers between devices with their start and end apart: 7, of which 5 were waited for; matrix products, arithmetic and copies ran while one was open for 31% of the time, Pallas kernels for 0%

profile of v7, /device:TPU:0, one launch (start us, length us, event | category | flops | bytes accessed | tf_op | source)
XLA Modules:
  0.0 315.9 jit_solution(5942611715587620896)
XLA Ops:
  6.5 0.7 all-gather.3.cloned.1.call-update
  7.3 0.9 copy.94
  8.1 1.6 sort.17
  9.8 4.5 %concatenate.9 = bf16[256,4480]{1,0:T(8,128)(2,1)} concatenate(bf16[256,4096]{1,0:T(8,128)(2,1)} %param.9, bf16[256,128]{1,0:T(8,128)(2,1)} %param.11, bf16[256,128]{1,0:T(8,128)(2,1)} %param.12, bf16[256,64]{1,0:T(8,128)(2,1)S(1)} %copy.94, bf16[256,64]{1,0:T(8,128)(2,1)S(1)} %broadcast_in_dim.62), dimensions={1} | concatenate | bytes 4587520 | tf_op jit(solution)/shard_map/concatenate | solution.py:44
  14.3 3.9 %gather_fusion = bf16[8,32,4480]{2,1,0:T(8,128)(2,1)} fusion(bf16[8,32,4480]{2,1,0:T(8,128)(2,1)} %bitcast.104, s32[1024]{0:T(1024)S(1)} %pad_clamp_fusion), kind=kCustom, calls=%fused_computation | custom fusion | bytes 4587552 | tf_op jit(solution)/shard_map/jit(_take)/gather | solution.py:41
  18.2 1.9 broadcast_select_fusion
  20.1 33.7 %all_to_all.35 = bf16[8,32,4480]{2,1,0:T(8,128)(2,1)S(1)} all-to-all(bf16[8,32,4480]{2,1,0:T(8,128)(2,1)S(1)} %broadcast_select_fusion), channel_id=1, replica_groups=mesh['dom'=8,'sx'=4,'sz'=4] {'dom'}, dimensions={0} | all-to-all | bytes 4587520 | tf_op jit(solution)/shard_map/all_to_all | solution.py:47
  53.8 1.4 copy-done.6
  55.2 1.6 slice.60
  56.8 0.7 copy.98
  57.5 5.3 %all-to-all-start.2 = ((bf16[4,256,16]{1,2,0:T(8,128)(2,1)}), bf16[4,256,16]{1,2,0:T(8,128)(2,1)S(1)}, u32[]{:S(2)}, u32[]{:S(2)}) async-start(bf16[4,256,16]{1,2,0:T(8,128)(2,1)} %bitcast.7), calls=%async_computation.2 | async-start | bytes 65536 | tf_op jit(solution)/shard_map/all_to_all | solution.py:68
  62.8 4.1 %copy.95 = bf16[256,4096]{0,1:T(8,128)(2,1)} copy(bf16[256,4096]{1,0:T(8,128)(2,1)} %slice.60) | data formatting | bytes 4194304 | tf_op jit(solution)/shard_map/slice | solution.py:51
  66.9 3.9 %copy.96 = bf16[256,4,1024]{2,0,1:T(8,128)(2,1)} copy(bf16[256,4,1024]{0,2,1:T(8,128)(2,1)} %bitcast.109) | data formatting | bytes 4194304 | tf_op jit(solution)/shard_map/reshape | solution.py:60
  70.9 0.9 fusion.52
  71.9 3.3 %pad_maximum_fusion = bf16[4,256,1280]{2,1,0:T(8,128)(2,1)} fusion(bf16[4,256,128]{2,1,0:T(8,128)(2,1)S(1)} %broadcast_in_dim.66, bf16[4,256,128]{2,1,0:T(8,128)(2,1)S(1)} %broadcast_in_dim.65, bf16[4,256,1024]{2,1,0:T(8,128)(2,1)} %bitcast.108), kind=kLoop, calls=%fused_computation.28 | loop fusion | flops 7864320 | bytes 5242880 | tf_op jit(solution)/shard_map/concatenate | solution.py:58
  75.2 4.8 %all-to-all-start.1 = ((bf16[4,256,1280]{2,1,0:T(8,128)(2,1)}), bf16[4,256,1280]{2,1,0:T(8,128)(2,1)}, u32[]{:S(2)}, u32[]{:S(2)}) async-start(bf16[4,256,1280]{2,1,0:T(8,128)(2,1)} %pad_maximum_fusion), calls=%async_computation.1 | async-start | bytes 5242880 | tf_op jit(solution)/shard_map/all_to_all | solution.py:66
  80.0 2.0 gather_fusion.1
  82.1 2.3 reduce-window.6
  84.3 0.1 slice.67
  84.4 0.1 copy.100
  84.6 0.1 copy_bitcast_fusion
  84.7 0.2 slice_reduce_fusion.1
  84.9 0.3 fusion.31
  85.2 0.1 copy.112
  85.3 0.1 bitcast_exponential_fusion
  85.4 55.5 %all-to-all-done.1 = bf16[4,256,1280]{2,1,0:T(8,128)(2,1)} async-done(((bf16[4,256,1280]{2,1,0:T(8,128)(2,1)}), bf16[4,256,1280]{2,1,0:T(8,128)(2,1)}, u32[]{:S(2)}, u32[]{:S(2)}) %all-to-all-start.1) | async-done | bytes 2621472 | tf_op jit(solution)/shard_map/all_to_all | solution.py:66
  140.9 1.8 slice.63
  142.7 2.6 copy.97
  145.3 2.3 fusion.21
  147.6 5.0 %convolution_bitcast_fusion = f32[5,16,64,128]{3,0,2,1:T(8,128)S(1)} fusion(f32[16,5,4,1]{1,2,3,0:T(4,128)S(1)} %copy.112, f32[4,16,64,128]{3,2,1,0:T(8,128)S(1)} %fusion.21), kind=kOutput, calls=%fused_computation.30 | convolution fusion | flops 31457280 | bytes 4719872 | tf_op jit(solution)/shard_map/hkj,jhpn->khpn/dot_general | solution.py:97
  152.6 2.0 copy-done.4
  154.6 0.6 slice.71
  155.3 1.7 broadcast_in_dim.75
  157.0 4.6 %all-to-all-start.3 = ((f32[4,17,64,128]{3,2,1,0:T(8,128)}), f32[4,17,64,128]{3,2,1,0:T(8,128)}, u32[]{:S(2)}, u32[]{:S(2)}) async-start(f32[4,17,64,128]{3,2,1,0:T(8,128)} %broadcast_in_dim.75), calls=%async_computation.3 | async-start | bytes 4456448 | tf_op jit(solution)/shard_map/all_to_all | solution.py:106
  161.6 0.1 dynamic-slice_bitcast_fusion
  161.8 1.6 broadcast_select_fusion.1
  163.4 0.1 copy.105
  163.5 1.4 fusion.38
  164.9 49.0 %all-to-all-done.3 = f32[4,17,64,128]{3,2,1,0:T(8,128)} async-done(((f32[4,17,64,128]{3,2,1,0:T(8,128)}), f32[4,17,64,128]{3,2,1,0:T(8,128)}, u32[]{:S(2)}, u32[]{:S(2)}) %all-to-all-start.3) | async-done | bytes 2228256 | tf_op jit(solution)/shard_map/all_to_all | solution.py:106
  213.9 3.8 %all-to-all-start.6 = ((bf16[8,32,4096]{2,1,0:T(8,128)(2,1)}), bf16[8,32,4096]{2,1,0:T(8,128)(2,1)S(1)}, u32[]{:S(2)}, u32[]{:S(2)}) async-start(bf16[8,32,4096]{2,1,0:T(8,128)(2,1)} %broadcast_select_fusion.1), calls=%async_computation.6 | async-start | bytes 4194304 | tf_op jit(solution)/shard_map/all_to_all | solution.py:49
  217.7 0.9 slice_reduce_fusion
  218.5 0.1 fusion.34
  218.7 0.1 copy.113
  218.8 1.9 slice.73
  220.7 4.2 %fusion.23 = f32[16,1,64,128]{3,1,2,0:T(1,128)S(1)} fusion(f32[4,16,1,1]{0,2,3,1:T(1,128)S(1)} %copy.113, f32[4,16,64,128]{3,2,1,0:T(8,128)S(1)} %slice.73), kind=kOutput, calls=%fused_computation.33 | convolution fusion | flops 6291456 | bytes 2621696 | tf_op jit(solution)/shard_map/jh,jhpn->hpn/dot_general | solution.py:116
  224.9 0.7 slice_add_fusion
  225.6 3.0 fusion.25
  228.7 6.5 %abs_reduce_fusion = (f32[4,256,16]{1,2,0:T(8,128)S(1)}, f32[4,256,16,64]{1,3,2,0:T(8,128)}) fusion(bf16[4,256,16,64]{1,3,2,0:T(8,128)(2,1)S(1)} %bitcast.107, f32[16]{0:T(128)S(1)} %dynamic-slice_bitcast_fusion, f32[4,256,16,64]{1,3,2,0:T(8,128)S(1)} %fusion.25, f32[4,256,16]{1,2,0:T(8,128)S(1)} %get-tuple-element.13, ...), kind=kOutput, calls=%fused_computation.27 | convolution fusion | flops 565166080 | bytes 11796544 | tf_op jit(solution)/shard_map/chij,cjhp->cihp/dot_general | solution.py:82
  235.2 0.6 broadcast_multiply_fusion
  235.8 8.8 %all-to-all-done.6 = bf16[8,32,4096]{2,1,0:T(8,128)(2,1)S(1)} async-done(((bf16[8,32,4096]{2,1,0:T(8,128)(2,1)}), bf16[8,32,4096]{2,1,0:T(8,128)(2,1)S(1)}, u32[]{:S(2)}, u32[]{:S(2)}) %all-to-all-start.6) | async-done | bytes 2097184 | tf_op jit(solution)/shard_map/all_to_all | solution.py:49
  244.6 3.3 %all-to-all-start.5 = ((f32[4,256,16]{1,2,0:T(8,128)}), f32[4,256,16]{1,2,0:T(8,128)S(1)}, u32[]{:S(2)}, u32[]{:S(2)}) async-start(f32[4,256,16]{1,2,0:T(8,128)} %get-tuple-element.11), calls=%async_computation.5 | async-start | bytes 131072 | tf_op jit(solution)/shard_map/all_to_all | solution.py:20
  247.9 4.2 %clamp_convert_fusion = s16[4,256,16,64]{1,3,2,0:T(8,128)(2,1)} fusion(f32[4,256,16,64]{1,3,2,0:T(8,128)} %get-tuple-element.18, f32[4,256,16]{1,2,0:T(8,128)S(1)} %get-tuple-element.12), kind=kLoop, calls=%fused_computation.26 | loop fusion | flops 4194304 | bytes 6356992 | tf_op jit(solution)/shard_map/convert_element_type | solution.py:18
  252.1 1.4 all-to-all-done.5
  253.5 4.7 %all-to-all-start.4 = ((s16[4,256,1024]{1,2,0:T(8,128)(2,1)}), s16[4,256,1024]{1,2,0:T(8,128)(2,1)}, u32[]{:S(2)}, u32[]{:S(2)}) async-start(s16[4,256,1024]{1,2,0:T(8,128)(2,1)} %bitcast.105), calls=%async_computation.4 | async-start | bytes 4194304 | tf_op jit(solution)/shard_map/all_to_all | solution.py:17
  258.2 4.5 %reshape.197 = f32[256,4,1024]{2,1,0:T(4,128)} reshape(bf16[8,32,4096]{2,1,0:T(8,128)(2,1)S(1)} %all-to-all-done.6) | data formatting | bytes 6291456 | tf_op jit(solution)/shard_map/convert_element_type | solution.py:132
  262.6 5.2 %copy.110 = f32[256,4,1024]{0,2,1:T(8,128)} copy(f32[256,4,1024]{2,1,0:T(4,128)} %reshape.197) | data formatting | bytes 8388608 | tf_op jit(solution)/shard_map/convert_element_type | solution.py:132
  267.9 2.4 convert_element_type.52
  270.3 5.6 %copy.108 = f32[256,4096]{0,1:T(8,128)} copy(f32[256,4096]{1,0:T(8,128)} %bitcast.100) | data formatting | bytes 8388608 | tf_op jit(solution)/shard_map/convert_element_type | solution.py:132
  275.9 7.3 %all-to-all-done.4 = s16[4,256,1024]{1,2,0:T(8,128)(2,1)} async-done(((s16[4,256,1024]{1,2,0:T(8,128)(2,1)}), s16[4,256,1024]{1,2,0:T(8,128)(2,1)}, u32[]{:S(2)}, u32[]{:S(2)}) %all-to-all-start.4) | async-done | bytes 2097184 | tf_op jit(solution)/shard_map/all_to_all | solution.py:17
  283.2 2.4 bitcast_multiply_fusion.2
  285.7 0.4 copy-done.2
  286.1 3.5 %fusion.20 = f32[256]{0:T(256)S(1)} fusion(f32[256,4,1024]{0,2,1:T(8,128)S(1)} %copy-done.2, f32[4,256,16]{1,2,0:T(8,128)S(1)} %all-to-all-done.5, s16[4,256,1024]{1,2,0:T(8,128)(2,1)} %all-to-all-done.4), kind=kLoop, calls=%fused_computation.23 | loop fusion | flops 9436928 | bytes 6358016 | tf_op jit(solution)/shard_map/reduce_sum | solution.py:135
  289.6 2.7 fusion.18
  292.3 16.8 %fusion.11 = bf16[1,256,4096]{2,1,0:T(8,128)(2,1)} fusion(bf16[256,4096]{0,1:T(8,128)(2,1)} %fusion.18, bf16[1,4096,4096]{2,1,0:T(8,128)(2,1)} %all-gather.3.cloned.1.call-done), kind=kOutput, calls=%fused_computation.14 | convolution fusion | flops 8590983168 | bytes 37748736 | tf_op jit(solution)/shard_map/dot_general | solution.py:138
  (44 shorter events, 0.4 us)
Async XLA Ops:
  6.5 73.4 %copy-start = (bf16[256,4096]{1,0:T(8,128)(2,1)S(1)}, bf16[256,4096]{1,0:T(8,128)(2,1)}, u32[]{:S(2)}) copy-start(bf16[256,4096]{1,0:T(8,128)(2,1)} %param.10) | copy-start | bytes 6291460
  6.5 285.8 %all-gather.3.cloned.1.call-start = ((), (), s32[]{:S(2)}) async-start(), calls=%async_computation.7 | async-start | bytes 35651584 | tf_op jit(solution)/shard_map/all_gather | solution.py:140
  53.8 1.4 copy-start.6
  57.5 17.7 %all-to-all-start.2 = ((bf16[4,256,16]{1,2,0:T(8,128)(2,1)}), bf16[4,256,16]{1,2,0:T(8,128)(2,1)S(1)}, u32[]{:S(2)}, u32[]{:S(2)}) async-start(bf16[4,256,16]{1,2,0:T(8,128)(2,1)} %bitcast.7), calls=%async_computation.2 | async-start | bytes 65536 | tf_op jit(solution)/shard_map/all_to_all | solution.py:68
  75.2 65.8 %all-to-all-start.1 = ((bf16[4,256,1280]{2,1,0:T(8,128)(2,1)}), bf16[4,256,1280]{2,1,0:T(8,128)(2,1)}, u32[]{:S(2)}, u32[]{:S(2)}) async-start(bf16[4,256,1280]{2,1,0:T(8,128)(2,1)} %pad_maximum_fusion), calls=%async_computation.1 | async-start | bytes 5242880 | tf_op jit(solution)/shard_map/all_to_all | solution.py:66
  152.6 2.0 copy-start.4
  157.0 4.7 %copy-start.10 = (f32[1,64]{1,0:T(1,128)S(1)}, f32[1,64]{1,0:T(1,128)}, u32[]{:S(2)}) copy-start(f32[1,64]{1,0:T(1,128)} %param.17) | copy-start | bytes 772
  157.0 4.8 %copy-start.7 = (bf16[8,32,4096]{2,1,0:T(8,128)(2,1)S(1)}, bf16[8,32,4096]{2,1,0:T(8,128)(2,1)}, u32[]{:S(2)}) copy-start(bf16[8,32,4096]{2,1,0:T(8,128)(2,1)} %gather_fusion.1) | copy-start | bytes 6291460
  157.0 56.9 %all-to-all-start.3 = ((f32[4,17,64,128]{3,2,1,0:T(8,128)}), f32[4,17,64,128]{3,2,1,0:T(8,128)}, u32[]{:S(2)}, u32[]{:S(2)}) async-start(f32[4,17,64,128]{3,2,1,0:T(8,128)} %broadcast_in_dim.75), calls=%async_computation.3 | async-start | bytes 4456448 | tf_op jit(solution)/shard_map/all_to_all | solution.py:106
  213.9 30.7 %all-to-all-start.6 = ((bf16[8,32,4096]{2,1,0:T(8,128)(2,1)}), bf16[8,32,4096]{2,1,0:T(8,128)(2,1)S(1)}, u32[]{:S(2)}, u32[]{:S(2)}) async-start(bf16[8,32,4096]{2,1,0:T(8,128)(2,1)} %broadcast_select_fusion.1), calls=%async_computation.6 | async-start | bytes 4194304 | tf_op jit(solution)/shard_map/all_to_all | solution.py:49
  218.8 6.2 %copy-start.5 = (f32[5,16,64,128]{3,0,2,1:T(8,128)S(1)}, f32[5,16,64,128]{3,0,2,1:T(8,128)}, u32[]{:S(2)}) copy-start(f32[5,16,64,128]{3,0,2,1:T(8,128)} %copy-done.4) | copy-start | bytes 7864324
  225.6 3.1 copy-start.8
  244.6 8.9 %all-to-all-start.5 = ((f32[4,256,16]{1,2,0:T(8,128)}), f32[4,256,16]{1,2,0:T(8,128)S(1)}, u32[]{:S(2)}, u32[]{:S(2)}) async-start(f32[4,256,16]{1,2,0:T(8,128)} %get-tuple-element.11), calls=%async_computation.5 | async-start | bytes 131072 | tf_op jit(solution)/shard_map/all_to_all | solution.py:20
  253.5 29.8 %all-to-all-start.4 = ((s16[4,256,1024]{1,2,0:T(8,128)(2,1)}), s16[4,256,1024]{1,2,0:T(8,128)(2,1)}, u32[]{:S(2)}, u32[]{:S(2)}) async-start(s16[4,256,1024]{1,2,0:T(8,128)(2,1)} %bitcast.105), calls=%async_computation.4 | async-start | bytes 4194304 | tf_op jit(solution)/shard_map/all_to_all | solution.py:17
  283.2 2.8 copy-start.2
  286.1 3.5 %copy-start.3 = (f32[256,4096]{0,1:T(8,128)S(1)}, f32[256,4096]{0,1:T(8,128)}, u32[]{:S(2)}) copy-start(f32[256,4096]{0,1:T(8,128)} %copy.108) | copy-start | bytes 12582916
  286.1 3.5 %copy-start.9 = (f32[1,4096]{1,0:T(1,128)S(1)}, f32[1,4096]{1,0:T(1,128)}, u32[]{:S(2)}) copy-start(f32[1,4096]{1,0:T(1,128)} %param.16) | copy-start | bytes 49156
  292.3 16.8 %copy-start.1 = (bf16[256,4096]{1,0:T(8,128)(2,1)S(1)}, bf16[256,4096]{1,0:T(8,128)(2,1)}, u32[]{:S(2)}) copy-start(bf16[256,4096]{1,0:T(8,128)(2,1)} %param.10) | copy-start | bytes 6291460
Sparse Core Ops, SparseCore 0:
  9.4 260.2 all-gather.2

commit v8 on v7

--- a/solution.py
+++ b/solution.py
@@ -103,17 +103,14 @@
     ends = jnp.concatenate(
         [local_end, jnp.broadcast_to(slab[None, :, None], (1, hsize, nstate))], axis=0
     )
-    ends = lax.all_to_all(
-        jnp.broadcast_to(ends[None], (nx,) + ends.shape), "sx", split_axis=0, concat_axis=0, tiled=True
-    )
-    end_states = ends[:, :lheads]
-    end_totals = ends[:, lheads, :lheads, 0]
-    me = lax.axis_index("sx")
-    xdx = jnp.arange(nx)
-    inside = ((xdx[:, None] < xdx[None, :]) & (xdx[None, :] < me)).astype(jnp.float32)
-    gap_x = jnp.einsum("ji,ih->jh", inside, end_totals, precision=lax.Precision.HIGHEST)
-    weight_x = jnp.where((xdx < me)[:, None], jnp.exp(jnp.minimum(gap_x, 0.0)), 0.0)
-    incoming = jnp.einsum("jh,jhpn->hpn", weight_x, end_states, precision=lax.Precision.HIGHEST)
+    got = [
+        lax.ppermute(ends, "sx", [(i, i + d) for i in range(nx - d)]) for d in range(1, nx)
+    ]
+    incoming = jnp.zeros_like(local_end)
+    gap = jnp.zeros((lheads,), jnp.float32)
+    for piece in got:
+        incoming = incoming + jnp.exp(gap)[:, None, None] * piece[:lheads]
+        gap = gap + piece[lheads, :lheads, 0]
     prefix = jnp.cumsum(totals, axis=0) - totals
     before = before + jnp.exp(prefix)[:, :, None, None] * incoming[None]
 

time: 317 us -> 304 us (0.959)
  blocking collectives: 33.7 us -> 0 us
  starting transfers between devices: 26.5 us -> 36.9 us
  waiting for transfers between devices: 123 us -> 133 us
  other arithmetic: 28 us -> 34.2 us
  matrix products: 39.6 us -> 35.5 us
  local copies, waits for them, and re-layouts: 51.7 us -> 48.1 us
    ppermute x0 -> x3, waiting for transfers between devices: none -> 39.5 us  [per_device(): lax.ppermute(ends, 'sx', [(i, i + d) for i in range(nx - d)])]
    all_to_all x1 -> x0, blocking collectives: 33.7 us -> none  [per_device(): lax.all_to_all(arrange(packed), 'dom', split_axis=0, concat_axis=0, tiled...]
    all_to_all x1, waiting for transfers between devices: 49 us -> 27.3 us  [per_device(): lax.all_to_all(arrange(packed), 'dom', split_axis=0, concat_axis=0, tiled...]
    ppermute x0 -> x3, starting transfers between devices: none -> 11 us  [per_device(): lax.ppermute(ends, 'sx', [(i, i + d) for i in range(nx - d)])]
    all_to_all x1, waiting for transfers between devices: 8.77 us -> 0.01 us  [per_device(): lax.all_to_all(arrange(gate_z), 'dom', split_axis=0, concat_axis=0, tiled...]
    dot_general x2 -> x0, matrix products: 4.34 us -> none  [the longest x1 4.22 us: per_device(): jnp.einsum('jh,jhpn->hpn', weight_x, end_states, precision=lax.Precision....]
  transfers between devices with their start and end apart: 7 -> 10, of which waited for: 5 -> 6; matrix products, arithmetic and copies ran while one was open for 31% -> 33% of each run, Pallas kernels for 0% -> 0%
where the time goes in v8:
time: 304 us; the launch traced here: 302 us
  waiting for transfers between devices  133 us (44%)
  local copies, waits for them, and re-layouts  48.1 us (16%)
  starting transfers between devices  36.9 us (12%)
  matrix products  35.5 us (12%)
  other arithmetic  34.2 us (11%)
  between operations  13.7 us (5%)
    all_to_all x1, waiting for transfers between devices, per_device(): xbc = lax.all_to_all(xbc, 'sz', split_axis=0, concat_axis=0, tiled=True)  56 us
    ppermute x3, waiting for transfers between devices, per_device(): lax.ppermute(ends, 'sx', [(i, i + d) for i in range(nx - d)])  39.5 us
    all_to_all x1, waiting for transfers between devices, per_device(): lax.all_to_all(arrange(packed), 'dom', split_axis=0, concat_axis=0, tiled...  27.3 us
    dot_general x1, matrix products, per_device(): jnp.dot(normed, lax.all_gather(out_weight[0], SEQ, axis=1, tiled=True), p...  16.8 us
    convert_element_type x3, local copies, waits for them, and re-layouts, per_device(): gated = ys * jax.nn.silu(zs.astype(jnp.float32))  15.3 us
    ppermute x3, starting transfers between devices, per_device(): lax.ppermute(ends, 'sx', [(i, i + d) for i in range(nx - d)])  11 us
    all_to_all x1, waiting for transfers between devices, code16(): lax.all_to_all(coded.astype(jnp.int16).reshape(*lead, -1), axis_name, spl...  7.68 us
    slice x2, local copies, waits for them, and re-layouts, per_device(): xc = xbc[:, :, :local].reshape(blocks, SPAN, lheads, hsize)  7.02 us
  transfers between devices with their start and end apart: 10, of which 6 were waited for; matrix products, arithmetic and copies ran while one was open for 33% of the time, Pallas kernels for 0%

profile of v8, /device:TPU:0, one launch (start us, length us, event | category | flops | bytes accessed | tf_op | source)
XLA Modules:
  0.0 301.7 jit_solution(18166064035659469289)
XLA Ops:
  6.5 0.7 all-gather.3.cloned.1.call-update
  7.3 0.9 copy.56
  8.1 1.6 sort.17
  9.8 4.5 %concatenate.9 = bf16[256,4480]{1,0:T(8,128)(2,1)} concatenate(bf16[256,4096]{1,0:T(8,128)(2,1)} %param.9, bf16[256,128]{1,0:T(8,128)(2,1)} %param.11, bf16[256,128]{1,0:T(8,128)(2,1)} %param.12, bf16[256,64]{1,0:T(8,128)(2,1)S(1)} %copy.56, bf16[256,64]{1,0:T(8,128)(2,1)S(1)} %broadcast_in_dim.54), dimensions={1} | concatenate | bytes 4587520 | tf_op jit(solution)/shard_map/concatenate | solution.py:44
  14.3 3.9 %gather_fusion = bf16[8,32,4480]{2,1,0:T(8,128)(2,1)} fusion(bf16[8,32,4480]{2,1,0:T(8,128)(2,1)} %bitcast.95, s32[1024]{0:T(1024)S(1)} %pad_clamp_fusion), kind=kCustom, calls=%fused_computation | custom fusion | bytes 4587552 | tf_op jit(solution)/shard_map/jit(_take)/gather | solution.py:41
  18.2 3.4 %broadcast_select_fusion = bf16[8,32,4480]{2,1,0:T(8,128)(2,1)} fusion(bf16[8,32,4480]{2,1,0:T(8,128)(2,1)} %gather_fusion, pred[8]{0:T(512)(128)(4,1)S(1)} %compare_and_fusion), kind=kLoop, calls=%fused_computation.29 | loop fusion | flops 1146880 | bytes 4587528 | tf_op jit(solution)/shard_map/jit(_take)/select_n | solution.py:41
  21.6 4.6 %all-to-all-start = ((bf16[8,32,4480]{2,1,0:T(8,128)(2,1)}), bf16[8,32,4480]{2,1,0:T(8,128)(2,1)}, u32[]{:S(2)}, u32[]{:S(2)}) async-start(bf16[8,32,4480]{2,1,0:T(8,128)(2,1)} %broadcast_select_fusion), calls=%async_computation | async-start | bytes 4587520 | tf_op jit(solution)/shard_map/all_to_all | solution.py:47
  26.2 2.1 gather_fusion.1
  28.3 27.3 %all-to-all-done = bf16[8,32,4480]{2,1,0:T(8,128)(2,1)} async-done(((bf16[8,32,4480]{2,1,0:T(8,128)(2,1)}), bf16[8,32,4480]{2,1,0:T(8,128)(2,1)}, u32[]{:S(2)}, u32[]{:S(2)}) %all-to-all-start) | async-done | bytes 2293792 | tf_op jit(solution)/shard_map/all_to_all | solution.py:47
  55.5 0.8 slice.78
  56.4 1.9 slice.72
  58.3 0.7 copy.60
  59.0 5.3 %all-to-all-start.2 = ((bf16[4,256,16]{1,2,0:T(8,128)(2,1)}), bf16[4,256,16]{1,2,0:T(8,128)(2,1)S(1)}, u32[]{:S(2)}, u32[]{:S(2)}) async-start(bf16[4,256,16]{1,2,0:T(8,128)(2,1)} %bitcast.7), calls=%async_computation.2 | async-start | bytes 65536 | tf_op jit(solution)/shard_map/all_to_all | solution.py:68
  64.2 2.4 copy.57
  66.7 4.0 %copy.58 = bf16[256,4,1024]{2,0,1:T(8,128)(2,1)} copy(bf16[256,4,1024]{0,2,1:T(8,128)(2,1)} %bitcast.100) | data formatting | bytes 4194304 | tf_op jit(solution)/shard_map/reshape | solution.py:60
  70.7 0.9 fusion.49
  71.7 3.5 %pad_maximum_fusion = bf16[4,256,1280]{2,1,0:T(8,128)(2,1)} fusion(bf16[4,256,128]{2,1,0:T(8,128)(2,1)S(1)} %broadcast_in_dim.58, bf16[4,256,128]{2,1,0:T(8,128)(2,1)S(1)} %broadcast_in_dim.57, bf16[4,256,1024]{2,1,0:T(8,128)(2,1)} %bitcast.99), kind=kLoop, calls=%fused_computation.28 | loop fusion | flops 7864320 | bytes 5242880 | tf_op jit(solution)/shard_map/concatenate | solution.py:58
  75.1 4.8 %all-to-all-start.1 = ((bf16[4,256,1280]{2,1,0:T(8,128)(2,1)}), bf16[4,256,1280]{2,1,0:T(8,128)(2,1)}, u32[]{:S(2)}, u32[]{:S(2)}) async-start(bf16[4,256,1280]{2,1,0:T(8,128)(2,1)} %pad_maximum_fusion), calls=%async_computation.1 | async-start | bytes 5242880 | tf_op jit(solution)/shard_map/all_to_all | solution.py:66
  79.9 1.6 broadcast_select_fusion.1
  81.6 2.3 reduce-window.6
  83.8 0.1 slice.79
  83.9 0.1 copy.62
  84.1 0.1 copy_bitcast_fusion
  84.2 0.2 slice_reduce_fusion
  84.4 0.3 fusion.29
  84.7 0.1 copy.74
  84.8 0.1 bitcast_exponential_fusion
  84.9 56.0 %all-to-all-done.1 = bf16[4,256,1280]{2,1,0:T(8,128)(2,1)} async-done(((bf16[4,256,1280]{2,1,0:T(8,128)(2,1)}), bf16[4,256,1280]{2,1,0:T(8,128)(2,1)}, u32[]{:S(2)}, u32[]{:S(2)}) %all-to-all-start.1) | async-done | bytes 2621472 | tf_op jit(solution)/shard_map/all_to_all | solution.py:66
  140.8 3.6 %all-to-all-start.5 = ((bf16[8,32,4096]{2,1,0:T(8,128)(2,1)}), bf16[8,32,4096]{2,1,0:T(8,128)(2,1)S(1)}, u32[]{:S(2)}, u32[]{:S(2)}) async-start(bf16[8,32,4096]{2,1,0:T(8,128)(2,1)} %broadcast_select_fusion.1), calls=%async_computation.5 | async-start | bytes 4194304 | tf_op jit(solution)/shard_map/all_to_all | solution.py:49
  144.5 3.1 %slice.75 = bf16[4,256,1024]{2,1,0:T(8,128)(2,1)} slice(bf16[4,256,1280]{2,1,0:T(8,128)(2,1)} %all-to-all-done.1), slice={[0:4], [0:256], [0:1024]} | slice | bytes 4194304 | tf_op jit(solution)/shard_map/slice | solution.py:71
  147.5 3.9 %copy.59 = bf16[4,256,1024]{1,2,0:T(8,128)(2,1)} copy(bf16[4,256,1024]{2,1,0:T(8,128)(2,1)} %slice.75) | data formatting | bytes 4194304 | tf_op jit(solution)/shard_map/slice | solution.py:71
  151.5 2.4 fusion.21
  153.9 5.0 %convolution_bitcast_fusion = f32[5,16,64,128]{3,0,2,1:T(8,128)S(1)} fusion(f32[16,5,4,1]{1,2,3,0:T(4,128)S(1)} %copy.74, f32[4,16,64,128]{3,2,1,0:T(8,128)S(1)} %fusion.21), kind=kOutput, calls=%fused_computation.30 | convolution fusion | flops 31457280 | bytes 4719872 | tf_op jit(solution)/shard_map/hkj,jhpn->khpn/dot_general | solution.py:97
  158.9 2.0 copy-done.4
  160.9 0.6 slice.83
  161.5 0.1 broadcast_in_dim.61
  161.6 3.4 %collective-permute-start = (f32[17,64,128]{2,1,0:T(8,128)S(1)}, f32[17,64,128]{2,1,0:T(8,128)S(1)}, u32[]{:S(2)}, u32[]{:S(2)}) collective-permute-start(f32[17,64,128]{2,1,0:T(8,128)S(1)} %pad_maximum_fusion.1), channel_id=1, source_target_pairs={{0,4},{4,8},{8,12},{1,5},{5,9},{9,13},{2,6},{6,10},{10,14},{3,7},{... | collective-permute-start | bytes 1671176 | tf_op jit(solution)/shard_map/ppermute | solution.py:107
  165.1 5.4 %collective-permute-start.1 = (f32[17,64,128]{2,1,0:T(8,128)S(1)}, f32[17,64,128]{2,1,0:T(8,128)}, u32[]{:S(2)}, u32[]{:S(2)}) collective-permute-start(f32[17,64,128]{2,1,0:T(8,128)S(1)} %pad_maximum_fusion.1), channel_id=1, source_target_pairs={{0,8},{4,12},{1,9},{5,13},{2,10},{6,14},{3,11},{7,15},{16,24},{20,... | collective-permute-start | bytes 1671176 | tf_op jit(solution)/shard_map/ppermute | solution.py:107
  170.5 0.1 dynamic-slice_bitcast_fusion
  170.6 2.1 collective-permute-start.2
  172.7 0.1 copy.67
  172.8 1.4 fusion.35
  174.2 15.8 %collective-permute-done = f32[17,64,128]{2,1,0:T(8,128)S(1)} collective-permute-done((f32[17,64,128]{2,1,0:T(8,128)S(1)}, f32[17,64,128]{2,1,0:T(8,128)S(1)}, u32[]{:S(2)}, u32[]{:S(2)}) %collective-permute-start) | collective-permute-done | bytes 557088 | tf_op jit(solution)/shard_map/ppermute | solution.py:107
  190.0 23.7 %collective-permute-done.1 = f32[17,64,128]{2,1,0:T(8,128)} collective-permute-done((f32[17,64,128]{2,1,0:T(8,128)S(1)}, f32[17,64,128]{2,1,0:T(8,128)}, u32[]{:S(2)}, u32[]{:S(2)}) %collective-permute-start.1) | collective-permute-done | bytes 557088 | tf_op jit(solution)/shard_map/ppermute | solution.py:107
  213.7 0.8 exponential_reduce_fusion
  214.5 1.4 fusion.30
  215.9 3.1 %slice_add_fusion = f32[4,16,64,128]{3,0,2,1:T(4,128)S(1)} fusion(f32[5,16,64,128]{3,0,2,1:T(8,128)} %copy-done.4, f32[16,64,128]{2,1,0:T(8,128)S(1)} %fusion.30, f32[4,16]{0,1:T(8,128)S(1)} %copy.67), kind=kLoop, calls=%fused_computation.32 | loop fusion | flops 1048576 | bytes 4718848 | tf_op jit(solution)/shard_map/add | solution.py:115
  219.0 3.0 %fusion.23 = f32[4,256,16,64]{1,3,2,0:T(8,128)S(1)} fusion(f32[4,16,64,128]{3,0,2,1:T(4,128)S(1)} %slice_add_fusion, bf16[4,256,1280]{2,1,0:T(8,128)(2,1)} %all-to-all-done.1), kind=kOutput, calls=%fused_computation.33 | convolution fusion | flops 1610612736 | bytes 6553600 | tf_op jit(solution)/shard_map/cin,chpn->cihp/dot_general | solution.py:117
  222.1 6.7 %abs_reduce_fusion = (f32[4,256,16]{1,2,0:T(8,128)S(1)}, f32[4,256,16,64]{1,3,2,0:T(8,128)}) fusion(bf16[4,256,16,64]{1,3,2,0:T(8,128)(2,1)S(1)} %bitcast.98, f32[16]{0:T(128)S(1)} %dynamic-slice_bitcast_fusion, f32[4,256,16,64]{1,3,2,0:T(8,128)S(1)} %fusion.23, f32[4,256,16]{1,2,0:T(8,128)S(1)} %get-tuple-element.15, ...), kind=kOutput, calls=%fused_computation.27 | convolution fusion | flops 565166080 | bytes 11796544 | tf_op jit(solution)/shard_map/chij,cjhp->cihp/dot_general | solution.py:82
  228.8 0.6 broadcast_multiply_fusion
  229.4 3.3 %all-to-all-start.4 = ((f32[4,256,16]{1,2,0:T(8,128)}), f32[4,256,16]{1,2,0:T(8,128)S(1)}, u32[]{:S(2)}, u32[]{:S(2)}) async-start(f32[4,256,16]{1,2,0:T(8,128)} %get-tuple-element.13), calls=%async_computation.4 | async-start | bytes 131072 | tf_op jit(solution)/shard_map/all_to_all | solution.py:20
  232.7 4.2 %clamp_convert_fusion = s16[4,256,16,64]{1,3,2,0:T(8,128)(2,1)} fusion(f32[4,256,16,64]{1,3,2,0:T(8,128)} %get-tuple-element.20, f32[4,256,16]{1,2,0:T(8,128)S(1)} %get-tuple-element.14), kind=kLoop, calls=%fused_computation.26 | loop fusion | flops 4194304 | bytes 6356992 | tf_op jit(solution)/shard_map/convert_element_type | solution.py:18
  236.9 2.2 all-to-all-done.4
  239.1 4.4 %all-to-all-start.3 = ((s16[4,256,1024]{1,2,0:T(8,128)(2,1)}), s16[4,256,1024]{1,2,0:T(8,128)(2,1)}, u32[]{:S(2)}, u32[]{:S(2)}) async-start(s16[4,256,1024]{1,2,0:T(8,128)(2,1)} %bitcast.96), calls=%async_computation.3 | async-start | bytes 4194304 | tf_op jit(solution)/shard_map/all_to_all | solution.py:17
  243.6 4.5 %reshape.205 = f32[256,4,1024]{2,1,0:T(4,128)} reshape(bf16[8,32,4096]{2,1,0:T(8,128)(2,1)S(1)} %all-to-all-done.5) | data formatting | bytes 6291456 | tf_op jit(solution)/shard_map/convert_element_type | solution.py:129
  248.1 5.2 %copy.72 = f32[256,4,1024]{0,2,1:T(8,128)} copy(f32[256,4,1024]{2,1,0:T(4,128)} %reshape.205) | data formatting | bytes 8388608 | tf_op jit(solution)/shard_map/convert_element_type | solution.py:129
  253.3 2.4 convert_element_type.51
  255.7 5.6 %copy.70 = f32[256,4096]{0,1:T(8,128)} copy(f32[256,4096]{1,0:T(8,128)} %bitcast.94) | data formatting | bytes 8388608 | tf_op jit(solution)/shard_map/convert_element_type | solution.py:129
  261.3 7.7 %all-to-all-done.3 = s16[4,256,1024]{1,2,0:T(8,128)(2,1)} async-done(((s16[4,256,1024]{1,2,0:T(8,128)(2,1)}), s16[4,256,1024]{1,2,0:T(8,128)(2,1)}, u32[]{:S(2)}, u32[]{:S(2)}) %all-to-all-start.3) | async-done | bytes 2097184 | tf_op jit(solution)/shard_map/all_to_all | solution.py:17
  269.0 2.4 bitcast_multiply_fusion.2
  271.4 0.4 copy-done.2
  271.8 3.5 %fusion.20 = f32[256]{0:T(256)S(1)} fusion(f32[256,4,1024]{0,2,1:T(8,128)S(1)} %copy-done.2, f32[4,256,16]{1,2,0:T(8,128)S(1)} %all-to-all-done.4, s16[4,256,1024]{1,2,0:T(8,128)(2,1)} %all-to-all-done.3), kind=kLoop, calls=%fused_computation.23 | loop fusion | flops 9436928 | bytes 6358016 | tf_op jit(solution)/shard_map/reduce_sum | solution.py:132
  275.3 2.7 fusion.18
  278.1 16.8 %fusion.11 = bf16[1,256,4096]{2,1,0:T(8,128)(2,1)} fusion(bf16[256,4096]{0,1:T(8,128)(2,1)} %fusion.18, bf16[1,4096,4096]{2,1,0:T(8,128)(2,1)} %all-gather.3.cloned.1.call-done), kind=kOutput, calls=%fused_computation.14 | convolution fusion | flops 8590983168 | bytes 37748736 | tf_op jit(solution)/shard_map/dot_general | solution.py:135
  (40 shorter events, 0.3 us)
Async XLA Ops:
  6.5 19.6 %copy-start = (bf16[256,4096]{1,0:T(8,128)(2,1)S(1)}, bf16[256,4096]{1,0:T(8,128)(2,1)}, u32[]{:S(2)}) copy-start(bf16[256,4096]{1,0:T(8,128)(2,1)} %param.10) | copy-start | bytes 6291460
  6.5 271.5 %all-gather.3.cloned.1.call-start = ((), (), s32[]{:S(2)}) async-start(), calls=%async_computation.6 | async-start | bytes 35651584 | tf_op jit(solution)/shard_map/all_gather | solution.py:137
  21.6 34.0 %all-to-all-start = ((bf16[8,32,4480]{2,1,0:T(8,128)(2,1)}), bf16[8,32,4480]{2,1,0:T(8,128)(2,1)}, u32[]{:S(2)}, u32[]{:S(2)}) async-start(bf16[8,32,4480]{2,1,0:T(8,128)(2,1)} %broadcast_select_fusion), calls=%async_computation | async-start | bytes 4587520 | tf_op jit(solution)/shard_map/all_to_all | solution.py:47
  59.0 16.1 %all-to-all-start.2 = ((bf16[4,256,16]{1,2,0:T(8,128)(2,1)}), bf16[4,256,16]{1,2,0:T(8,128)(2,1)S(1)}, u32[]{:S(2)}, u32[]{:S(2)}) async-start(bf16[4,256,16]{1,2,0:T(8,128)(2,1)} %bitcast.7), calls=%async_computation.2 | async-start | bytes 65536 | tf_op jit(solution)/shard_map/all_to_all | solution.py:68
  71.6 8.3 %copy-start.6 = (bf16[8,32,4096]{2,1,0:T(8,128)(2,1)S(1)}, bf16[8,32,4096]{2,1,0:T(8,128)(2,1)}, u32[]{:S(2)}) copy-start(bf16[8,32,4096]{2,1,0:T(8,128)(2,1)} %gather_fusion.1) | copy-start | bytes 6291460
  75.1 65.7 %all-to-all-start.1 = ((bf16[4,256,1280]{2,1,0:T(8,128)(2,1)}), bf16[4,256,1280]{2,1,0:T(8,128)(2,1)}, u32[]{:S(2)}, u32[]{:S(2)}) async-start(bf16[4,256,1280]{2,1,0:T(8,128)(2,1)} %pad_maximum_fusion), calls=%async_computation.1 | async-start | bytes 5242880 | tf_op jit(solution)/shard_map/all_to_all | solution.py:66
  140.8 88.6 %all-to-all-start.5 = ((bf16[8,32,4096]{2,1,0:T(8,128)(2,1)}), bf16[8,32,4096]{2,1,0:T(8,128)(2,1)S(1)}, u32[]{:S(2)}, u32[]{:S(2)}) async-start(bf16[8,32,4096]{2,1,0:T(8,128)(2,1)} %broadcast_select_fusion.1), calls=%async_computation.5 | async-start | bytes 4194304 | tf_op jit(solution)/shard_map/all_to_all | solution.py:49
  153.9 16.6 %copy-start.8 = (f32[1,64]{1,0:T(1,128)S(1)}, f32[1,64]{1,0:T(1,128)}, u32[]{:S(2)}) copy-start(f32[1,64]{1,0:T(1,128)} %param.17) | copy-start | bytes 772
  158.9 2.0 copy-start.4
  161.6 28.3 %collective-permute-start = (f32[17,64,128]{2,1,0:T(8,128)S(1)}, f32[17,64,128]{2,1,0:T(8,128)S(1)}, u32[]{:S(2)}, u32[]{:S(2)}) collective-permute-start(f32[17,64,128]{2,1,0:T(8,128)S(1)} %pad_maximum_fusion.1), channel_id=1, source_target_pairs={{0,4},{4,8},{8,12},{1,5},{5,9},{9,13},{2,6},{6,10},{10,14},{3,7},{... | collective-permute-start | bytes 1671176 | tf_op jit(solution)/shard_map/ppermute | solution.py:107
  165.1 48.6 %collective-permute-start.1 = (f32[17,64,128]{2,1,0:T(8,128)S(1)}, f32[17,64,128]{2,1,0:T(8,128)}, u32[]{:S(2)}, u32[]{:S(2)}) collective-permute-start(f32[17,64,128]{2,1,0:T(8,128)S(1)} %pad_maximum_fusion.1), channel_id=1, source_target_pairs={{0,8},{4,12},{1,9},{5,13},{2,10},{6,14},{3,11},{7,15},{16,24},{20,... | collective-permute-start | bytes 1671176 | tf_op jit(solution)/shard_map/ppermute | solution.py:107
  170.6 43.9 %collective-permute-start.2 = (f32[17,64,128]{2,1,0:T(8,128)S(1)}, f32[17,64,128]{2,1,0:T(8,128)}, u32[]{:S(2)}, u32[]{:S(2)}) collective-permute-start(f32[17,64,128]{2,1,0:T(8,128)S(1)} %pad_maximum_fusion.1), channel_id=1, source_target_pairs={{0,12},{1,13},{2,14},{3,15},{16,28},{17,29},{18,30},{19,31},{32,44... | collective-permute-start | bytes 1671176 | tf_op jit(solution)/shard_map/ppermute | solution.py:107
  219.0 3.1 %copy-start.5 = (bf16[4,256,1024]{1,2,0:T(8,128)(2,1)S(1)}, bf16[4,256,1024]{1,2,0:T(8,128)(2,1)}, u32[]{:S(2)}) copy-start(bf16[4,256,1024]{1,2,0:T(8,128)(2,1)} %copy.59) | copy-start | bytes 6291460
  229.4 9.7 %all-to-all-start.4 = ((f32[4,256,16]{1,2,0:T(8,128)}), f32[4,256,16]{1,2,0:T(8,128)S(1)}, u32[]{:S(2)}, u32[]{:S(2)}) async-start(f32[4,256,16]{1,2,0:T(8,128)} %get-tuple-element.13), calls=%async_computation.4 | async-start | bytes 131072 | tf_op jit(solution)/shard_map/all_to_all | solution.py:20
  239.1 29.9 %all-to-all-start.3 = ((s16[4,256,1024]{1,2,0:T(8,128)(2,1)}), s16[4,256,1024]{1,2,0:T(8,128)(2,1)}, u32[]{:S(2)}, u32[]{:S(2)}) async-start(s16[4,256,1024]{1,2,0:T(8,128)(2,1)} %bitcast.96), calls=%async_computation.3 | async-start | bytes 4194304 | tf_op jit(solution)/shard_map/all_to_all | solution.py:17
  269.0 2.8 copy-start.2
  271.8 3.5 %copy-start.3 = (f32[256,4096]{0,1:T(8,128)S(1)}, f32[256,4096]{0,1:T(8,128)}, u32[]{:S(2)}) copy-start(f32[256,4096]{0,1:T(8,128)} %copy.70) | copy-start | bytes 12582916
  271.8 3.5 %copy-start.7 = (f32[1,4096]{1,0:T(1,128)S(1)}, f32[1,4096]{1,0:T(1,128)}, u32[]{:S(2)}) copy-start(f32[1,4096]{1,0:T(1,128)} %param.16) | copy-start | bytes 49156
  278.1 16.8 %copy-start.1 = (bf16[256,4096]{1,0:T(8,128)(2,1)S(1)}, bf16[256,4096]{1,0:T(8,128)(2,1)}, u32[]{:S(2)}) copy-start(bf16[256,4096]{1,0:T(8,128)(2,1)} %param.10) | copy-start | bytes 6291460
Sparse Core Ops, SparseCore 0:
  9.4 258.5 all-gather.2

commit v9 on v8

--- a/solution.py
+++ b/solution.py
@@ -99,18 +99,24 @@
     before = before[:blocks]
     shard_total = jnp.sum(totals, axis=0)
 
-    slab = jnp.pad(shard_total, (0, hsize - lheads))
-    ends = jnp.concatenate(
-        [local_end, jnp.broadcast_to(slab[None, :, None], (1, hsize, nstate))], axis=0
-    )
-    got = [
-        lax.ppermute(ends, "sx", [(i, i + d) for i in range(nx - d)]) for d in range(1, nx)
-    ]
+    amax = jnp.max(jnp.abs(local_end), axis=-1, keepdims=True)
+    scale = amax / 32767.0
+    coded = jnp.clip(
+        jnp.round(local_end / jnp.where(scale > 0, scale, 1.0)), -32767.0, 32767.0
+    ).astype(jnp.int16)
+    lanes = 128
+    side = jnp.concatenate(
+        [scale.reshape(-1), shard_total, jnp.zeros((lanes - lheads,), jnp.float32)]
+    ).reshape(-1, lanes)
     incoming = jnp.zeros_like(local_end)
     gap = jnp.zeros((lheads,), jnp.float32)
-    for piece in got:
-        incoming = incoming + jnp.exp(gap)[:, None, None] * piece[:lheads]
-        gap = gap + piece[lheads, :lheads, 0]
+    for d in range(1, nx):
+        route = [(i, i + d) for i in range(nx - d)]
+        piece = lax.ppermute(coded, "sx", route).astype(jnp.float32)
+        got = lax.ppermute(side, "sx", route).reshape(-1)
+        piece = piece * got[: lheads * hsize].reshape(lheads, hsize, 1)
+        incoming = incoming + jnp.exp(gap)[:, None, None] * piece
+        gap = gap + got[lheads * hsize : lheads * hsize + lheads]
     prefix = jnp.cumsum(totals, axis=0) - totals
     before = before + jnp.exp(prefix)[:, :, None, None] * incoming[None]
 

time: 304 us -> 302 us (level)
  waiting for transfers between devices: 133 us -> 115 us
  local copies, waits for them, and re-layouts: 48.1 us -> 56 us
  starting transfers between devices: 36.9 us -> 42.6 us
    ppermute x3 -> x6, waiting for transfers between devices: 39.5 us -> 8.23 us  [the longest x3 8.22 us: per_device(): got = lax.ppermute(side, 'sx', route).reshape(-1)]
    all_to_all x1, waiting for transfers between devices: 7.68 us -> 22.7 us  [code16(): lax.all_to_all(coded.astype(jnp.int16).reshape(*lead, -1), axis_name, spl...]
    ppermute x3 -> x6, starting transfers between devices: 11 us -> 16.5 us  [the longest x3 10.5 us: per_device(): got = lax.ppermute(side, 'sx', route).reshape(-1)]
    mul x0 -> x3, local copies, waits for them, and re-layouts: none -> 3.43 us  [per_device(): piece = piece * got[:lheads * hsize].reshape(lheads, hsize, 1)]
    slice x2 -> x5, local copies, waits for them, and re-layouts: 0.2 us -> 3.35 us  [the longest x3 3.15 us: per_device(): piece = piece * got[:lheads * hsize].reshape(lheads, hsize, 1)]
  transfers between devices with their start and end apart: 10 -> 13, of which waited for: 6 -> 5; matrix products, arithmetic and copies ran while one was open for 33% -> 36% of each run, Pallas kernels for 0% -> 0%
where the time goes in v9:
time: 302 us; the launch traced here: 298 us
  waiting for transfers between devices  115 us (38%)
  local copies, waits for them, and re-layouts  56 us (19%)
  starting transfers between devices  42.6 us (14%)
  other arithmetic  35.4 us (12%)
  matrix products  35.3 us (12%)
  between operations  13.7 us (5%)
    all_to_all x1, waiting for transfers between devices, per_device(): xbc = lax.all_to_all(xbc, 'sz', split_axis=0, concat_axis=0, tiled=True)  55.8 us
    all_to_all x1, waiting for transfers between devices, per_device(): lax.all_to_all(arrange(packed), 'dom', split_axis=0, concat_axis=0, tiled...  26 us
    all_to_all x1, waiting for transfers between devices, code16(): lax.all_to_all(coded.astype(jnp.int16).reshape(*lead, -1), axis_name, spl...  22.7 us
    dot_general x1, matrix products, per_device(): jnp.dot(normed, lax.all_gather(out_weight[0], SEQ, axis=1, tiled=True), p...  16.8 us
    convert_element_type x3, local copies, waits for them, and re-layouts, per_device(): gated = ys * jax.nn.silu(zs.astype(jnp.float32))  15.4 us
    ppermute x3, starting transfers between devices, per_device(): got = lax.ppermute(side, 'sx', route).reshape(-1)  10.5 us
    ppermute x3, waiting for transfers between devices, per_device(): got = lax.ppermute(side, 'sx', route).reshape(-1)  8.22 us
    slice x2, local copies, waits for them, and re-layouts, per_device(): xc = xbc[:, :, :local].reshape(blocks, SPAN, lheads, hsize)  7.02 us
  transfers between devices with their start and end apart: 13, of which 5 were waited for; matrix products, arithmetic and copies ran while one was open for 36% of the time, Pallas kernels for 0%

profile of v9, /device:TPU:0, one launch (start us, length us, event | category | flops | bytes accessed | tf_op | source)
XLA Modules:
  0.0 298.5 jit_solution(4279179637281817642)
XLA Ops:
  6.5 0.7 all-gather.3.cloned.1.call-update
  7.3 0.9 copy.56
  8.1 1.6 sort.17
  9.8 4.5 %concatenate.9 = bf16[256,4480]{1,0:T(8,128)(2,1)} concatenate(bf16[256,4096]{1,0:T(8,128)(2,1)} %param.9, bf16[256,128]{1,0:T(8,128)(2,1)} %param.11, bf16[256,128]{1,0:T(8,128)(2,1)} %param.12, bf16[256,64]{1,0:T(8,128)(2,1)S(1)} %copy.56, bf16[256,64]{1,0:T(8,128)(2,1)S(1)} %broadcast_in_dim.58), dimensions={1} | concatenate | bytes 4587520 | tf_op jit(solution)/shard_map/concatenate | solution.py:44
  14.3 3.9 %gather_fusion = bf16[8,32,4480]{2,1,0:T(8,128)(2,1)} fusion(bf16[8,32,4480]{2,1,0:T(8,128)(2,1)} %bitcast.98, s32[1024]{0:T(1024)S(1)} %pad_clamp_fusion), kind=kCustom, calls=%fused_computation | custom fusion | bytes 4587552 | tf_op jit(solution)/shard_map/jit(_take)/gather | solution.py:41
  18.2 3.4 %broadcast_select_fusion = bf16[8,32,4480]{2,1,0:T(8,128)(2,1)} fusion(bf16[8,32,4480]{2,1,0:T(8,128)(2,1)} %gather_fusion, pred[8]{0:T(512)(128)(4,1)S(1)} %compare_and_fusion), kind=kLoop, calls=%fused_computation.29 | loop fusion | flops 1146880 | bytes 4587528 | tf_op jit(solution)/shard_map/jit(_take)/select_n | solution.py:41
  21.6 4.7 %all-to-all-start = ((bf16[8,32,4480]{2,1,0:T(8,128)(2,1)}), bf16[8,32,4480]{2,1,0:T(8,128)(2,1)}, u32[]{:S(2)}, u32[]{:S(2)}) async-start(bf16[8,32,4480]{2,1,0:T(8,128)(2,1)} %broadcast_select_fusion), calls=%async_computation | async-start | bytes 4587520 | tf_op jit(solution)/shard_map/all_to_all | solution.py:47
  26.3 2.1 gather_fusion.1
  28.4 0.6 dynamic-slice_bitcast_fusion
  29.0 0.6 iota_compare_fusion
  29.7 26.0 %all-to-all-done = bf16[8,32,4480]{2,1,0:T(8,128)(2,1)} async-done(((bf16[8,32,4480]{2,1,0:T(8,128)(2,1)}), bf16[8,32,4480]{2,1,0:T(8,128)(2,1)}, u32[]{:S(2)}, u32[]{:S(2)}) %all-to-all-start) | async-done | bytes 2293792 | tf_op jit(solution)/shard_map/all_to_all | solution.py:47
  55.7 0.8 slice.81
  56.5 1.9 slice.75
  58.4 0.7 copy.60
  59.1 5.2 %all-to-all-start.2 = ((bf16[4,256,16]{1,2,0:T(8,128)(2,1)}), bf16[4,256,16]{1,2,0:T(8,128)(2,1)S(1)}, u32[]{:S(2)}, u32[]{:S(2)}) async-start(bf16[4,256,16]{1,2,0:T(8,128)(2,1)} %bitcast.7), calls=%async_computation.2 | async-start | bytes 65536 | tf_op jit(solution)/shard_map/all_to_all | solution.py:68
  64.4 2.4 copy.57
  66.8 4.0 %copy.58 = bf16[256,4,1024]{2,0,1:T(8,128)(2,1)} copy(bf16[256,4,1024]{0,2,1:T(8,128)(2,1)} %bitcast.103) | data formatting | bytes 4194304 | tf_op jit(solution)/shard_map/reshape | solution.py:60
  70.8 0.9 fusion.46
  71.8 3.5 %pad_maximum_fusion = bf16[4,256,1280]{2,1,0:T(8,128)(2,1)} fusion(bf16[4,256,128]{2,1,0:T(8,128)(2,1)S(1)} %broadcast_in_dim.62, bf16[4,256,128]{2,1,0:T(8,128)(2,1)S(1)} %broadcast_in_dim.61, bf16[4,256,1024]{2,1,0:T(8,128)(2,1)} %bitcast.102), kind=kLoop, calls=%fused_computation.28 | loop fusion | flops 7864320 | bytes 5242880 | tf_op jit(solution)/shard_map/concatenate | solution.py:58
  75.3 4.8 %all-to-all-start.1 = ((bf16[4,256,1280]{2,1,0:T(8,128)(2,1)}), bf16[4,256,1280]{2,1,0:T(8,128)(2,1)}, u32[]{:S(2)}, u32[]{:S(2)}) async-start(bf16[4,256,1280]{2,1,0:T(8,128)(2,1)} %pad_maximum_fusion), calls=%async_computation.1 | async-start | bytes 5242880 | tf_op jit(solution)/shard_map/all_to_all | solution.py:66
  80.1 1.7 broadcast_select_fusion.1
  81.7 2.3 reduce-window.6
  85.2 55.8 %all-to-all-done.1 = bf16[4,256,1280]{2,1,0:T(8,128)(2,1)} async-done(((bf16[4,256,1280]{2,1,0:T(8,128)(2,1)}), bf16[4,256,1280]{2,1,0:T(8,128)(2,1)}, u32[]{:S(2)}, u32[]{:S(2)}) %all-to-all-start.1) | async-done | bytes 2621472 | tf_op jit(solution)/shard_map/all_to_all | solution.py:66
  141.0 3.6 %all-to-all-start.5 = ((bf16[8,32,4096]{2,1,0:T(8,128)(2,1)}), bf16[8,32,4096]{2,1,0:T(8,128)(2,1)S(1)}, u32[]{:S(2)}, u32[]{:S(2)}) async-start(bf16[8,32,4096]{2,1,0:T(8,128)(2,1)} %broadcast_select_fusion.1), calls=%async_computation.5 | async-start | bytes 4194304 | tf_op jit(solution)/shard_map/all_to_all | solution.py:49
  144.6 3.1 %slice.78 = bf16[4,256,1024]{2,1,0:T(8,128)(2,1)} slice(bf16[4,256,1280]{2,1,0:T(8,128)(2,1)} %all-to-all-done.1), slice={[0:4], [0:256], [0:1024]} | slice | bytes 4194304 | tf_op jit(solution)/shard_map/slice | solution.py:71
  147.7 3.9 %copy.59 = bf16[4,256,1024]{1,2,0:T(8,128)(2,1)} copy(bf16[4,256,1024]{2,1,0:T(8,128)(2,1)} %slice.78) | data formatting | bytes 4194304 | tf_op jit(solution)/shard_map/slice | solution.py:71
  151.6 2.4 fusion.21
  154.0 5.0 %convolution_bitcast_fusion = f32[5,16,64,128]{3,0,2,1:T(8,128)S(1)} fusion(f32[16,5,4,1]{1,2,3,0:T(4,128)S(1)} %copy.74, f32[4,16,64,128]{3,2,1,0:T(8,128)S(1)} %fusion.21), kind=kOutput, calls=%fused_computation.30 | convolution fusion | flops 31457280 | bytes 4719872 | tf_op jit(solution)/shard_map/hkj,jhpn->khpn/dot_general | solution.py:97
  159.0 2.1 copy-done.4
  161.1 0.6 slice.86
  162.0 0.7 concatenate.11
  162.6 3.4 %collective-permute-start.1 = (f32[9,128]{1,0:T(8,128)}, f32[9,128]{1,0:T(8,128)S(1)}, u32[]{:S(2)}, u32[]{:S(2)}) collective-permute-start(f32[9,128]{1,0:T(8,128)} %bitcast.19), channel_id=1, source_target_pairs={{0,4},{4,8},{8,12},{1,5},{5,9},{9,13},{2,6},{6,10},{10,14},{3,7},{... | collective-permute-start | bytes 13832 | tf_op jit(solution)/shard_map/ppermute | solution.py:116
  166.0 5.3 %collective-permute-start.3 = (f32[9,128]{1,0:T(8,128)}, f32[9,128]{1,0:T(8,128)}, u32[]{:S(2)}, u32[]{:S(2)}) collective-permute-start(f32[9,128]{1,0:T(8,128)} %bitcast.19), channel_id=1, source_target_pairs={{0,8},{4,12},{1,9},{5,13},{2,10},{6,14},{3,11},{7,15},{16,24},{20,... | collective-permute-start | bytes 13832 | tf_op jit(solution)/shard_map/ppermute | solution.py:116
  171.5 2.0 collective-permute-start
  173.5 2.0 collective-permute-start.2
  175.5 2.0 collective-permute-start.4
  177.5 1.9 collective-permute-start.5
  179.4 1.3 fusion.33
  180.7 0.6 slice.87
  181.3 0.7 mul.148
  182.0 1.3 slice.89
  183.3 1.3 mul.152
  184.7 8.2 %collective-permute-done.5 = f32[9,128]{1,0:T(8,128)} collective-permute-done((f32[9,128]{1,0:T(8,128)}, f32[9,128]{1,0:T(8,128)}, u32[]{:S(2)}, u32[]{:S(2)}) %collective-permute-start.5) | collective-permute-done | bytes 4640 | tf_op jit(solution)/shard_map/ppermute | solution.py:116
  192.9 1.3 slice.91
  194.2 1.4 mul.157
  195.5 0.7 slice_exponential_fusion
  196.2 1.6 multiply_add_fusion
  197.9 3.0 %slice_add_fusion = f32[4,16,64,128]{3,0,2,1:T(4,128)S(1)} fusion(f32[5,16,64,128]{3,0,2,1:T(8,128)} %copy-done.4, f32[16,64,128]{2,1,0:T(8,128)S(1)} %multiply_add_fusion, f32[4,16]{0,1:T(8,128)S(1)} %copy.67), kind=kLoop, calls=%fused_computation.32 | loop fusion | flops 1048576 | bytes 4718848 | tf_op jit(solution)/shard_map/add | solution.py:121
  200.9 3.0 %fusion.23 = f32[4,256,16,64]{1,3,2,0:T(8,128)S(1)} fusion(f32[4,16,64,128]{3,0,2,1:T(4,128)S(1)} %slice_add_fusion, bf16[4,256,1280]{2,1,0:T(8,128)(2,1)} %all-to-all-done.1), kind=kOutput, calls=%fused_computation.33 | convolution fusion | flops 1610612736 | bytes 6553600 | tf_op jit(solution)/shard_map/cin,chpn->cihp/dot_general | solution.py:123
  204.0 6.5 %abs_reduce_fusion = (f32[4,256,16]{1,2,0:T(8,128)S(1)}, f32[4,256,16,64]{1,3,2,0:T(8,128)}) fusion(bf16[4,256,16,64]{1,3,2,0:T(8,128)(2,1)S(1)} %bitcast.101, f32[16]{0:T(128)S(1)} %copy-done.11, f32[4,256,16,64]{1,3,2,0:T(8,128)S(1)} %fusion.23, f32[4,256,16]{1,2,0:T(8,128)S(1)} %get-tuple-element.13, f32[4,16,256]{2,1,0:T(8,128)S(1)} %get-tuple-element.15, ...), kind=kOutput, calls=%fused_computation.27 | convolution fusion | flops 565166080 | bytes 11796544 | tf_op jit(solution)/shard_map/chij,cjhp->cihp/dot_general | solution.py:82
  210.5 0.6 broadcast_multiply_fusion
  211.2 3.3 %all-to-all-start.4 = ((f32[4,256,16]{1,2,0:T(8,128)}), f32[4,256,16]{1,2,0:T(8,128)S(1)}, u32[]{:S(2)}, u32[]{:S(2)}) async-start(f32[4,256,16]{1,2,0:T(8,128)} %get-tuple-element.11), calls=%async_computation.4 | async-start | bytes 131072 | tf_op jit(solution)/shard_map/all_to_all | solution.py:20
  214.5 4.4 %clamp_convert_fusion = s16[4,256,16,64]{1,3,2,0:T(8,128)(2,1)} fusion(f32[4,256,16,64]{1,3,2,0:T(8,128)} %get-tuple-element.22, f32[4,256,16]{1,2,0:T(8,128)S(1)} %get-tuple-element.12), kind=kLoop, calls=%fused_computation.26 | loop fusion | flops 4194304 | bytes 6356992 | tf_op jit(solution)/shard_map/convert_element_type | solution.py:18
  218.8 1.9 all-to-all-done.4
  220.8 4.5 %all-to-all-start.3 = ((s16[4,256,1024]{1,2,0:T(8,128)(2,1)}), s16[4,256,1024]{1,2,0:T(8,128)(2,1)}, u32[]{:S(2)}, u32[]{:S(2)}) async-start(s16[4,256,1024]{1,2,0:T(8,128)(2,1)} %bitcast.99), calls=%async_computation.3 | async-start | bytes 4194304 | tf_op jit(solution)/shard_map/all_to_all | solution.py:17
  225.2 4.5 %reshape.224 = f32[256,4,1024]{2,1,0:T(4,128)} reshape(bf16[8,32,4096]{2,1,0:T(8,128)(2,1)S(1)} %all-to-all-done.5) | data formatting | bytes 6291456 | tf_op jit(solution)/shard_map/convert_element_type | solution.py:135
  229.8 5.2 %copy.72 = f32[256,4,1024]{0,2,1:T(8,128)} copy(f32[256,4,1024]{2,1,0:T(4,128)} %reshape.224) | data formatting | bytes 8388608 | tf_op jit(solution)/shard_map/convert_element_type | solution.py:135
  235.0 2.4 convert_element_type.65
  237.4 5.6 %copy.70 = f32[256,4096]{0,1:T(8,128)} copy(f32[256,4096]{1,0:T(8,128)} %bitcast.97) | data formatting | bytes 8388608 | tf_op jit(solution)/shard_map/convert_element_type | solution.py:135
  243.0 22.7 %all-to-all-done.3 = s16[4,256,1024]{1,2,0:T(8,128)(2,1)} async-done(((s16[4,256,1024]{1,2,0:T(8,128)(2,1)}), s16[4,256,1024]{1,2,0:T(8,128)(2,1)}, u32[]{:S(2)}, u32[]{:S(2)}) %all-to-all-start.3) | async-done | bytes 2097184 | tf_op jit(solution)/shard_map/all_to_all | solution.py:17
  265.8 2.4 bitcast_multiply_fusion.2
  268.6 3.5 %fusion.20 = f32[256]{0:T(256)S(1)} fusion(f32[256,4,1024]{0,2,1:T(8,128)S(1)} %copy-done.2, f32[4,256,16]{1,2,0:T(8,128)S(1)} %all-to-all-done.4, s16[4,256,1024]{1,2,0:T(8,128)(2,1)} %all-to-all-done.3), kind=kLoop, calls=%fused_computation.23 | loop fusion | flops 9436928 | bytes 6358016 | tf_op jit(solution)/shard_map/reduce_sum | solution.py:138
  272.1 2.7 fusion.18
  274.9 16.8 %fusion.11 = bf16[1,256,4096]{2,1,0:T(8,128)(2,1)} fusion(bf16[256,4096]{0,1:T(8,128)(2,1)} %fusion.18, bf16[1,4096,4096]{2,1,0:T(8,128)(2,1)} %all-gather.3.cloned.1.call-done), kind=kOutput, calls=%fused_computation.14 | convolution fusion | flops 8590983168 | bytes 37748736 | tf_op jit(solution)/shard_map/dot_general | solution.py:141
  (61 shorter events, 2.2 us)
Async XLA Ops:
  6.5 19.8 %copy-start = (bf16[256,4096]{1,0:T(8,128)(2,1)S(1)}, bf16[256,4096]{1,0:T(8,128)(2,1)}, u32[]{:S(2)}) copy-start(bf16[256,4096]{1,0:T(8,128)(2,1)} %param.10) | copy-start | bytes 6291460
  6.5 268.3 %all-gather.3.cloned.1.call-start = ((), (), s32[]{:S(2)}) async-start(), calls=%async_computation.6 | async-start | bytes 35651584 | tf_op jit(solution)/shard_map/all_gather | solution.py:143
  21.6 6.8 %copy-start.10 = (f32[1,64]{1,0:T(1,128)S(1)}, f32[1,64]{1,0:T(1,128)}, u32[]{:S(2)}) copy-start(f32[1,64]{1,0:T(1,128)} %param.17) | copy-start | bytes 772
  21.6 34.1 %all-to-all-start = ((bf16[8,32,4480]{2,1,0:T(8,128)(2,1)}), bf16[8,32,4480]{2,1,0:T(8,128)(2,1)}, u32[]{:S(2)}, u32[]{:S(2)}) async-start(bf16[8,32,4480]{2,1,0:T(8,128)(2,1)} %broadcast_select_fusion), calls=%async_computation | async-start | bytes 4587520 | tf_op jit(solution)/shard_map/all_to_all | solution.py:47
  59.1 16.1 %all-to-all-start.2 = ((bf16[4,256,16]{1,2,0:T(8,128)(2,1)}), bf16[4,256,16]{1,2,0:T(8,128)(2,1)S(1)}, u32[]{:S(2)}, u32[]{:S(2)}) async-start(bf16[4,256,16]{1,2,0:T(8,128)(2,1)} %bitcast.7), calls=%async_computation.2 | async-start | bytes 65536 | tf_op jit(solution)/shard_map/all_to_all | solution.py:68
  71.8 8.3 %copy-start.6 = (bf16[8,32,4096]{2,1,0:T(8,128)(2,1)S(1)}, bf16[8,32,4096]{2,1,0:T(8,128)(2,1)}, u32[]{:S(2)}) copy-start(bf16[8,32,4096]{2,1,0:T(8,128)(2,1)} %gather_fusion.1) | copy-start | bytes 6291460
  75.3 65.7 %all-to-all-start.1 = ((bf16[4,256,1280]{2,1,0:T(8,128)(2,1)}), bf16[4,256,1280]{2,1,0:T(8,128)(2,1)}, u32[]{:S(2)}, u32[]{:S(2)}) async-start(bf16[4,256,1280]{2,1,0:T(8,128)(2,1)} %pad_maximum_fusion), calls=%async_computation.1 | async-start | bytes 5242880 | tf_op jit(solution)/shard_map/all_to_all | solution.py:66
  141.0 70.2 %all-to-all-start.5 = ((bf16[8,32,4096]{2,1,0:T(8,128)(2,1)}), bf16[8,32,4096]{2,1,0:T(8,128)(2,1)S(1)}, u32[]{:S(2)}, u32[]{:S(2)}) async-start(bf16[8,32,4096]{2,1,0:T(8,128)(2,1)} %broadcast_select_fusion.1), calls=%async_computation.5 | async-start | bytes 4194304 | tf_op jit(solution)/shard_map/all_to_all | solution.py:49
  159.0 2.1 copy-start.4
  162.6 14.9 %collective-permute-start.1 = (f32[9,128]{1,0:T(8,128)}, f32[9,128]{1,0:T(8,128)S(1)}, u32[]{:S(2)}, u32[]{:S(2)}) collective-permute-start(f32[9,128]{1,0:T(8,128)} %bitcast.19), channel_id=1, source_target_pairs={{0,4},{4,8},{8,12},{1,5},{5,9},{9,13},{2,6},{6,10},{10,14},{3,7},{... | collective-permute-start | bytes 13832 | tf_op jit(solution)/shard_map/ppermute | solution.py:116
  166.0 16.0 %collective-permute-start.3 = (f32[9,128]{1,0:T(8,128)}, f32[9,128]{1,0:T(8,128)}, u32[]{:S(2)}, u32[]{:S(2)}) collective-permute-start(f32[9,128]{1,0:T(8,128)} %bitcast.19), channel_id=1, source_target_pairs={{0,8},{4,12},{1,9},{5,13},{2,10},{6,14},{3,11},{7,15},{16,24},{20,... | collective-permute-start | bytes 13832 | tf_op jit(solution)/shard_map/ppermute | solution.py:116
  171.5 24.7 %collective-permute-start = (s16[16,64,128]{2,1,0:T(8,128)(2,1)S(1)}, s16[16,64,128]{2,1,0:T(8,128)(2,1)}, u32[]{:S(2)}, u32[]{:S(2)}) collective-permute-start(s16[16,64,128]{2,1,0:T(8,128)(2,1)S(1)} %clamp_convert_fusion.1), channel_id=1, source_target_pairs={{0,4},{4,8},{8,12},{1,5},{5,9},{9,13},{2,6},{6,10},{10,14},{3,7},{... | collective-permute-start | bytes 786440 | tf_op jit(solution)/shard_map/ppermute | solution.py:115
  173.5 22.7 %collective-permute-start.2 = (s16[16,64,128]{2,1,0:T(8,128)(2,1)S(1)}, s16[16,64,128]{2,1,0:T(8,128)(2,1)}, u32[]{:S(2)}, u32[]{:S(2)}) collective-permute-start(s16[16,64,128]{2,1,0:T(8,128)(2,1)S(1)} %clamp_convert_fusion.1), channel_id=1, source_target_pairs={{0,8},{4,12},{1,9},{5,13},{2,10},{6,14},{3,11},{7,15},{16,24},{20,... | collective-permute-start | bytes 786440 | tf_op jit(solution)/shard_map/ppermute | solution.py:115
  175.5 20.7 %collective-permute-start.4 = (s16[16,64,128]{2,1,0:T(8,128)(2,1)S(1)}, s16[16,64,128]{2,1,0:T(8,128)(2,1)}, u32[]{:S(2)}, u32[]{:S(2)}) collective-permute-start(s16[16,64,128]{2,1,0:T(8,128)(2,1)S(1)} %clamp_convert_fusion.1), channel_id=1, source_target_pairs={{0,12},{1,13},{2,14},{3,15},{16,28},{17,29},{18,30},{19,31},{32,44... | collective-permute-start | bytes 786440 | tf_op jit(solution)/shard_map/ppermute | solution.py:115
  177.5 3.2 %copy-start.9 = (f32[9,128]{1,0:T(8,128)}, f32[9,128]{1,0:T(8,128)S(1)}, u32[]{:S(2)}) copy-start(f32[9,128]{1,0:T(8,128)S(1)} %collective-permute-done.1) | copy-start | bytes 13828
  177.5 15.4 %collective-permute-start.5 = (f32[9,128]{1,0:T(8,128)}, f32[9,128]{1,0:T(8,128)}, u32[]{:S(2)}, u32[]{:S(2)}) collective-permute-start(f32[9,128]{1,0:T(8,128)} %bitcast.19), channel_id=1, source_target_pairs={{0,12},{1,13},{2,14},{3,15},{16,28},{17,29},{18,30},{19,31},{32,44... | collective-permute-start | bytes 13832 | tf_op jit(solution)/shard_map/ppermute | solution.py:116
  200.9 3.1 %copy-start.5 = (bf16[4,256,1024]{1,2,0:T(8,128)(2,1)S(1)}, bf16[4,256,1024]{1,2,0:T(8,128)(2,1)}, u32[]{:S(2)}) copy-start(bf16[4,256,1024]{1,2,0:T(8,128)(2,1)} %copy.59) | copy-start | bytes 6291460
  200.9 3.1 %copy-start.7 = (pred[256,256]{1,0:T(8,128)(4,1)S(1)}, pred[256,256]{1,0:T(8,128)(4,1)}, u32[]{:S(2)}) copy-start(pred[256,256]{1,0:T(8,128)(4,1)} %iota_compare_fusion) | copy-start | bytes 196612
  200.9 3.1 %copy-start.11 = (f32[16]{0:T(128)S(1)}, f32[16]{0:T(128)}, u32[]{:S(2)}) copy-start(f32[16]{0:T(128)} %dynamic-slice_bitcast_fusion) | copy-start | bytes 196
  211.2 9.6 %all-to-all-start.4 = ((f32[4,256,16]{1,2,0:T(8,128)}), f32[4,256,16]{1,2,0:T(8,128)S(1)}, u32[]{:S(2)}, u32[]{:S(2)}) async-start(f32[4,256,16]{1,2,0:T(8,128)} %get-tuple-element.11), calls=%async_computation.4 | async-start | bytes 131072 | tf_op jit(solution)/shard_map/all_to_all | solution.py:20
  220.8 45.0 %all-to-all-start.3 = ((s16[4,256,1024]{1,2,0:T(8,128)(2,1)}), s16[4,256,1024]{1,2,0:T(8,128)(2,1)}, u32[]{:S(2)}, u32[]{:S(2)}) async-start(s16[4,256,1024]{1,2,0:T(8,128)(2,1)} %bitcast.99), calls=%async_computation.3 | async-start | bytes 4194304 | tf_op jit(solution)/shard_map/all_to_all | solution.py:17
  265.8 2.8 copy-start.2
  268.6 3.5 %copy-start.3 = (f32[256,4096]{0,1:T(8,128)S(1)}, f32[256,4096]{0,1:T(8,128)}, u32[]{:S(2)}) copy-start(f32[256,4096]{0,1:T(8,128)} %copy.70) | copy-start | bytes 12582916
  268.6 3.5 %copy-start.8 = (f32[1,4096]{1,0:T(1,128)S(1)}, f32[1,4096]{1,0:T(1,128)}, u32[]{:S(2)}) copy-start(f32[1,4096]{1,0:T(1,128)} %param.16) | copy-start | bytes 49156
  274.9 16.8 %copy-start.1 = (bf16[256,4096]{1,0:T(8,128)(2,1)S(1)}, bf16[256,4096]{1,0:T(8,128)(2,1)}, u32[]{:S(2)}) copy-start(bf16[256,4096]{1,0:T(8,128)(2,1)} %param.10) | copy-start | bytes 6291460
Sparse Core Ops, SparseCore 0:
  9.4 257.0 all-gather.2

commit v10 on v9

--- a/solution.py
+++ b/solution.py
@@ -2,6 +2,8 @@
 import jax.numpy as jnp
 import numpy as np
 from jax import lax
+from jax.experimental import pallas as pl
+from jax.experimental.pallas import tpu as pltpu
 from jax.sharding import Mesh
 from jax.sharding import PartitionSpec as P
 
@@ -21,6 +23,28 @@
         scale.reshape(*lead, -1), axis_name, split_axis=0, concat_axis=0, tiled=True
     )
     return coded.reshape(values.shape).astype(jnp.float32) * scale[..., None]
+
+
+def project_kernel(a_ref, w_ref, o_ref):
+    o_ref[...] = jnp.dot(a_ref[...], w_ref[...], preferred_element_type=jnp.float32).astype(
+        o_ref.dtype
+    )
+
+
+def project(normed, weight, tile=512):
+    rows, depth = normed.shape
+    cols = weight.shape[1]
+    return pl.pallas_call(
+        project_kernel,
+        grid=(cols // tile,),
+        in_specs=[
+            pl.BlockSpec((rows, depth), lambda j: (0, 0)),
+            pl.BlockSpec((depth, tile), lambda j: (0, j)),
+        ],
+        out_specs=pl.BlockSpec((rows, tile), lambda j: (0, j)),
+        out_shape=jax.ShapeDtypeStruct((rows, cols), jnp.bfloat16),
+        compiler_params=pltpu.CompilerParams(vmem_limit_bytes=48 * 1024 * 1024),
+    )(normed, weight)
 
 
 def per_device(
@@ -138,11 +162,7 @@
         * lax.rsqrt(jnp.mean(gated * gated, axis=-1, keepdims=True) + 1e-05)
         * norm_gain[0][None, :]
     ).astype(jnp.bfloat16)
-    mixed = jnp.dot(
-        normed,
-        lax.all_gather(out_weight[0], SEQ, axis=1, tiled=True),
-        preferred_element_type=jnp.float32,
-    ).astype(jnp.bfloat16)
+    mixed = project(normed, lax.all_gather(out_weight[0], SEQ, axis=1, tiled=True))
     return mixed.reshape(1, rows, mixed.shape[-1])
 
 

time: 302 us -> 312 us (1.033)
  Pallas kernels: 0 us -> 16.8 us
  matrix products: 35.3 us -> 18.5 us
  waiting for transfers between devices: 115 us -> 126 us
    pallas_call x0 -> x1, Pallas kernels: none -> 16.8 us  [project(): pl.pallas_call(project_kernel, grid=(cols // tile,), in_specs=[pl.BlockSp...]
    dot_general x1 -> x0, matrix products: 16.8 us -> none  [per_device(): jnp.dot(normed, lax.all_gather(out_weight[0], SEQ, axis=1, tiled=True), p...]
    all_to_all x1, waiting for transfers between devices: 22.7 us -> 33.7 us  [code16(): lax.all_to_all(coded.astype(jnp.int16).reshape(*lead, -1), axis_name, spl...]
    reshape x0 -> x1, local copies, waits for them, and re-layouts: none -> 5.64 us  [per_device(): ys = jnp.transpose(ys, (1, 0, 2)).reshape(rows, width)]
    convert_element_type x3 -> x2, local copies, waits for them, and re-layouts: 15.4 us -> 9.75 us  [per_device(): gated = ys * jax.nn.silu(zs.astype(jnp.float32))]
  transfers between devices with their start and end apart: 13 -> 13, of which waited for: 5 -> 5; matrix products, arithmetic and copies ran while one was open for 36% -> 34% of each run, Pallas kernels for 0% -> 0%
where the time goes in v10:
time: 312 us; the launch traced here: 309 us
  waiting for transfers between devices  126 us (40%)
  local copies, waits for them, and re-layouts  56.2 us (18%)
  starting transfers between devices  42.6 us (14%)
  other arithmetic  34.6 us (11%)
  matrix products  18.5 us (6%)
  Pallas kernels  16.8 us (5%)
  between operations  13.7 us (4%)
    all_to_all x1, waiting for transfers between devices, per_device(): xbc = lax.all_to_all(xbc, 'sz', split_axis=0, concat_axis=0, tiled=True)  55.8 us
    all_to_all x1, waiting for transfers between devices, code16(): lax.all_to_all(coded.astype(jnp.int16).reshape(*lead, -1), axis_name, spl...  33.7 us
    all_to_all x1, waiting for transfers between devices, per_device(): lax.all_to_all(arrange(packed), 'dom', split_axis=0, concat_axis=0, tiled...  26 us
    pallas_call x1, Pallas kernels, project(): pl.pallas_call(project_kernel, grid=(cols // tile,), in_specs=[pl.BlockSp...  16.8 us
    ppermute x3, starting transfers between devices, per_device(): got = lax.ppermute(side, 'sx', route).reshape(-1)  10.5 us
    convert_element_type x2, local copies, waits for them, and re-layouts, per_device(): gated = ys * jax.nn.silu(zs.astype(jnp.float32))  9.75 us
    ppermute x3, waiting for transfers between devices, per_device(): got = lax.ppermute(side, 'sx', route).reshape(-1)  8.23 us
    slice x2, local copies, waits for them, and re-layouts, per_device(): xc = xbc[:, :, :local].reshape(blocks, SPAN, lheads, hsize)  7.02 us
  transfers between devices with their start and end apart: 13, of which 5 were waited for; matrix products, arithmetic and copies ran while one was open for 34% of the time, Pallas kernels for 0%

profile of v10, /device:TPU:0, one launch (start us, length us, event | category | flops | bytes accessed | tf_op | source)
XLA Modules:
  0.0 308.8 jit_solution(5859420336251724391)
XLA Ops:
  6.5 0.7 all-gather.3.cloned.1.call-update
  7.3 0.9 copy.54
  8.1 1.6 sort.17
  9.8 4.5 %concatenate.9 = bf16[256,4480]{1,0:T(8,128)(2,1)} concatenate(bf16[256,4096]{1,0:T(8,128)(2,1)} %param.9, bf16[256,128]{1,0:T(8,128)(2,1)} %param.11, bf16[256,128]{1,0:T(8,128)(2,1)} %param.12, bf16[256,64]{1,0:T(8,128)(2,1)S(1)} %copy.54, bf16[256,64]{1,0:T(8,128)(2,1)S(1)} %broadcast_in_dim.58), dimensions={1} | concatenate | bytes 4587520 | tf_op jit(solution)/shard_map/concatenate | solution.py:68
  14.3 3.9 %gather_fusion = bf16[8,32,4480]{2,1,0:T(8,128)(2,1)} fusion(bf16[8,32,4480]{2,1,0:T(8,128)(2,1)} %bitcast.102, s32[1024]{0:T(1024)S(1)} %pad_clamp_fusion), kind=kCustom, calls=%fused_computation | custom fusion | bytes 4587552 | tf_op jit(solution)/shard_map/jit(_take)/gather | solution.py:65
  18.2 3.4 %broadcast_select_fusion = bf16[8,32,4480]{2,1,0:T(8,128)(2,1)} fusion(bf16[8,32,4480]{2,1,0:T(8,128)(2,1)} %gather_fusion, pred[8]{0:T(512)(128)(4,1)S(1)} %compare_and_fusion), kind=kLoop, calls=%fused_computation.30 | loop fusion | flops 1146880 | bytes 4587528 | tf_op jit(solution)/shard_map/jit(_take)/select_n | solution.py:65
  21.6 4.6 %all-to-all-start = ((bf16[8,32,4480]{2,1,0:T(8,128)(2,1)}), bf16[8,32,4480]{2,1,0:T(8,128)(2,1)}, u32[]{:S(2)}, u32[]{:S(2)}) async-start(bf16[8,32,4480]{2,1,0:T(8,128)(2,1)} %broadcast_select_fusion), calls=%async_computation | async-start | bytes 4587520 | tf_op jit(solution)/shard_map/all_to_all | solution.py:71
  26.2 2.1 gather_fusion.1
  28.3 0.6 dynamic-slice_bitcast_fusion
  28.9 0.6 iota_compare_fusion
  29.6 26.0 %all-to-all-done = bf16[8,32,4480]{2,1,0:T(8,128)(2,1)} async-done(((bf16[8,32,4480]{2,1,0:T(8,128)(2,1)}), bf16[8,32,4480]{2,1,0:T(8,128)(2,1)}, u32[]{:S(2)}, u32[]{:S(2)}) %all-to-all-start) | async-done | bytes 2293792 | tf_op jit(solution)/shard_map/all_to_all | solution.py:71
  55.5 0.8 slice.81
  56.4 1.9 slice.75
  58.3 0.7 copy.58
  59.0 5.3 %all-to-all-start.2 = ((bf16[4,256,16]{1,2,0:T(8,128)(2,1)}), bf16[4,256,16]{1,2,0:T(8,128)(2,1)S(1)}, u32[]{:S(2)}, u32[]{:S(2)}) async-start(bf16[4,256,16]{1,2,0:T(8,128)(2,1)} %bitcast.7), calls=%async_computation.2 | async-start | bytes 65536 | tf_op jit(solution)/shard_map/all_to_all | solution.py:92
  64.2 2.4 copy.55
  66.7 3.0 copy.56
  69.7 0.9 fusion.42
  70.6 1.8 pad_maximum_fusion
  72.4 4.9 %all-to-all-start.1 = ((bf16[4,256,1280]{2,1,0:T(8,128)(2,1)}), bf16[4,256,1280]{2,1,0:T(8,128)(2,1)}, u32[]{:S(2)}, u32[]{:S(2)}) async-start(bf16[4,256,1280]{2,1,0:T(8,128)(2,1)} %pad_maximum_fusion), calls=%async_computation.1 | async-start | bytes 5242880 | tf_op jit(solution)/shard_map/all_to_all | solution.py:90
  77.3 1.7 broadcast_select_fusion.1
  79.0 2.3 reduce-window.6
  82.5 55.8 %all-to-all-done.1 = bf16[4,256,1280]{2,1,0:T(8,128)(2,1)} async-done(((bf16[4,256,1280]{2,1,0:T(8,128)(2,1)}), bf16[4,256,1280]{2,1,0:T(8,128)(2,1)}, u32[]{:S(2)}, u32[]{:S(2)}) %all-to-all-start.1) | async-done | bytes 2621472 | tf_op jit(solution)/shard_map/all_to_all | solution.py:90
  138.3 3.6 %all-to-all-start.5 = ((bf16[8,32,4096]{2,1,0:T(8,128)(2,1)}), bf16[8,32,4096]{2,1,0:T(8,128)(2,1)S(1)}, u32[]{:S(2)}, u32[]{:S(2)}) async-start(bf16[8,32,4096]{2,1,0:T(8,128)(2,1)} %broadcast_select_fusion.1), calls=%async_computation.5 | async-start | bytes 4194304 | tf_op jit(solution)/shard_map/all_to_all | solution.py:73
  141.9 3.1 slice.78
  145.0 3.9 %copy.57 = bf16[4,256,1024]{1,2,0:T(8,128)(2,1)} copy(bf16[4,256,1024]{2,1,0:T(8,128)(2,1)} %slice.78) | data formatting | bytes 4194304 | tf_op jit(solution)/shard_map/slice | solution.py:95
  148.9 2.3 fusion.17
  151.2 5.0 %convolution_bitcast_fusion = f32[5,16,64,128]{3,0,2,1:T(8,128)S(1)} fusion(f32[16,5,4,1]{1,2,3,0:T(4,128)S(1)} %copy.71, f32[4,16,64,128]{3,2,1,0:T(8,128)S(1)} %fusion.17), kind=kOutput, calls=%fused_computation.31 | convolution fusion | flops 31457280 | bytes 4719872 | tf_op jit(solution)/shard_map/hkj,jhpn->khpn/dot_general | solution.py:121
  156.2 2.1 copy-done.4
  158.3 0.6 slice.86
  159.1 0.7 concatenate.11
  159.8 3.4 %collective-permute-start.1 = (f32[9,128]{1,0:T(8,128)}, f32[9,128]{1,0:T(8,128)S(1)}, u32[]{:S(2)}, u32[]{:S(2)}) collective-permute-start(f32[9,128]{1,0:T(8,128)} %bitcast.19), channel_id=1, source_target_pairs={{0,4},{4,8},{8,12},{1,5},{5,9},{9,13},{2,6},{6,10},{10,14},{3,7},{... | collective-permute-start | bytes 13832 | tf_op jit(solution)/shard_map/ppermute | solution.py:140
  163.2 5.3 %collective-permute-start.3 = (f32[9,128]{1,0:T(8,128)}, f32[9,128]{1,0:T(8,128)}, u32[]{:S(2)}, u32[]{:S(2)}) collective-permute-start(f32[9,128]{1,0:T(8,128)} %bitcast.19), channel_id=1, source_target_pairs={{0,8},{4,12},{1,9},{5,13},{2,10},{6,14},{3,11},{7,15},{16,24},{20,... | collective-permute-start | bytes 13832 | tf_op jit(solution)/shard_map/ppermute | solution.py:140
  168.7 2.0 collective-permute-start
  170.7 2.0 collective-permute-start.2
  172.7 2.0 collective-permute-start.4
  174.6 1.9 collective-permute-start.5
  176.5 1.3 fusion.29
  177.9 0.6 slice.87
  178.5 0.7 mul.148
  179.2 1.3 slice.89
  180.5 1.3 mul.152
  181.8 8.2 %collective-permute-done.5 = f32[9,128]{1,0:T(8,128)} collective-permute-done((f32[9,128]{1,0:T(8,128)}, f32[9,128]{1,0:T(8,128)}, u32[]{:S(2)}, u32[]{:S(2)}) %collective-permute-start.5) | collective-permute-done | bytes 4640 | tf_op jit(solution)/shard_map/ppermute | solution.py:140
  190.0 1.3 slice.91
  191.3 1.4 mul.157
  192.7 0.7 slice_exponential_fusion
  193.4 1.6 multiply_add_fusion
  195.0 2.9 slice_add_fusion
  198.0 3.0 fusion.19
  201.1 6.5 %abs_reduce_fusion = (f32[4,256,16]{1,2,0:T(8,128)S(1)}, f32[4,256,16,64]{1,3,2,0:T(8,128)}) fusion(bf16[4,256,16,64]{1,3,2,0:T(8,128)(2,1)S(1)} %bitcast.105, f32[16]{0:T(128)S(1)} %copy-done.11, f32[4,256,16,64]{1,3,2,0:T(8,128)S(1)} %fusion.19, f32[4,256,16]{1,2,0:T(8,128)S(1)} %get-tuple-element.13, f32[4,16,256]{2,1,0:T(8,128)S(1)} %get-tuple-element.15, ...), kind=kOutput, calls=%fused_computation.27 | convolution fusion | flops 565166080 | bytes 11796544 | tf_op jit(solution)/shard_map/chij,cjhp->cihp/dot_general | solution.py:106
  207.6 0.6 broadcast_multiply_fusion
  208.2 3.3 %all-to-all-start.4 = ((f32[4,256,16]{1,2,0:T(8,128)}), f32[4,256,16]{1,2,0:T(8,128)S(1)}, u32[]{:S(2)}, u32[]{:S(2)}) async-start(f32[4,256,16]{1,2,0:T(8,128)} %get-tuple-element.11), calls=%async_computation.4 | async-start | bytes 131072 | tf_op jit(solution)/shard_map/all_to_all | solution.py:22
  211.5 4.4 %clamp_convert_fusion = s16[4,256,16,64]{1,3,2,0:T(8,128)(2,1)} fusion(f32[4,256,16,64]{1,3,2,0:T(8,128)} %get-tuple-element.22, f32[4,256,16]{1,2,0:T(8,128)S(1)} %get-tuple-element.12), kind=kLoop, calls=%fused_computation.26 | loop fusion | flops 4194304 | bytes 6356992 | tf_op jit(solution)/shard_map/convert_element_type | solution.py:20
  215.9 1.9 all-to-all-done.4
  217.8 4.5 %all-to-all-start.3 = ((s16[4,256,1024]{1,2,0:T(8,128)(2,1)}), s16[4,256,1024]{1,2,0:T(8,128)(2,1)}, u32[]{:S(2)}, u32[]{:S(2)}) async-start(s16[4,256,1024]{1,2,0:T(8,128)(2,1)} %bitcast.103), calls=%async_computation.3 | async-start | bytes 4194304 | tf_op jit(solution)/shard_map/all_to_all | solution.py:19
  222.3 4.5 %reshape.224 = f32[256,4,1024]{2,1,0:T(4,128)} reshape(bf16[8,32,4096]{2,1,0:T(8,128)(2,1)S(1)} %all-to-all-done.5) | data formatting | bytes 6291456 | tf_op jit(solution)/shard_map/convert_element_type | solution.py:159
  226.8 5.2 %copy.69 = f32[256,4,1024]{0,2,1:T(8,128)} copy(f32[256,4,1024]{2,1,0:T(4,128)} %reshape.224) | data formatting | bytes 8388608 | tf_op jit(solution)/shard_map/convert_element_type | solution.py:159
  232.1 33.7 %all-to-all-done.3 = s16[4,256,1024]{1,2,0:T(8,128)(2,1)} async-done(((s16[4,256,1024]{1,2,0:T(8,128)(2,1)}), s16[4,256,1024]{1,2,0:T(8,128)(2,1)}, u32[]{:S(2)}, u32[]{:S(2)}) %all-to-all-start.3) | async-done | bytes 2097184 | tf_op jit(solution)/shard_map/all_to_all | solution.py:19
  265.8 4.2 %bitcast_multiply_fusion.2 = f32[4,256,1024]{1,2,0:T(8,128)} fusion(s16[4,256,1024]{1,2,0:T(8,128)(2,1)} %all-to-all-done.3, f32[4,256,16]{1,2,0:T(8,128)S(1)} %all-to-all-done.4), kind=kLoop, calls=%fused_computation.24 | loop fusion | flops 2097152 | bytes 6356992 | tf_op jit(solution)/shard_map/mul | solution.py:25
  270.0 5.6 %copy.75 = f32[256,4096]{1,0:T(8,128)} copy(f32[256,4096]{0,1:T(8,128)} %bitcast.101) | data formatting | bytes 8388608 | tf_op jit(solution)/shard_map/reshape | solution.py:158
  275.6 4.8 %fusion.15 = f32[256]{0:T(256)S(1)} fusion(f32[256,4,1024]{0,2,1:T(8,128)} %copy.69, f32[4,256,16]{1,2,0:T(8,128)S(1)} %all-to-all-done.4, s16[4,256,1024]{1,2,0:T(8,128)(2,1)} %all-to-all-done.3), kind=kLoop, calls=%fused_computation.23 | loop fusion | flops 9436928 | bytes 6358016 | tf_op jit(solution)/shard_map/reduce_sum | solution.py:162
  280.4 3.1 fusion.16.a_ref
  283.5 1.6 copy-done.2
  285.1 16.8 %shard_map.91 = bf16[256,4096]{1,0:T(8,128)(2,1)} custom-call(bf16[256,4096]{1,0:T(8,128)(2,1)S(1)} %copy-done.2, bf16[4096,4096]{1,0:T(8,128)(2,1)} %bitcast.100), custom_call_target="tpu_custom_call" | custom-call | tf_op jit(solution)/shard_map/pallas_call | solution.py:37
  (60 shorter events, 1.8 us)
Async XLA Ops:
  6.5 19.6 %copy-start = (bf16[256,4096]{1,0:T(8,128)(2,1)S(1)}, bf16[256,4096]{1,0:T(8,128)(2,1)}, u32[]{:S(2)}) copy-start(bf16[256,4096]{1,0:T(8,128)(2,1)} %param.10) | copy-start | bytes 6291460
  6.5 277.0 %all-gather.3.cloned.1.call-start = ((), (), s32[]{:S(2)}) async-start(), calls=%async_computation.6 | async-start | bytes 35651584 | tf_op jit(solution)/shard_map/all_gather | solution.py:165
  21.6 34.0 %all-to-all-start = ((bf16[8,32,4480]{2,1,0:T(8,128)(2,1)}), bf16[8,32,4480]{2,1,0:T(8,128)(2,1)}, u32[]{:S(2)}, u32[]{:S(2)}) async-start(bf16[8,32,4480]{2,1,0:T(8,128)(2,1)} %broadcast_select_fusion), calls=%async_computation | async-start | bytes 4587520 | tf_op jit(solution)/shard_map/all_to_all | solution.py:71
  26.2 2.1 copy-start.10
  59.0 13.4 %all-to-all-start.2 = ((bf16[4,256,16]{1,2,0:T(8,128)(2,1)}), bf16[4,256,16]{1,2,0:T(8,128)(2,1)S(1)}, u32[]{:S(2)}, u32[]{:S(2)}) async-start(bf16[4,256,16]{1,2,0:T(8,128)(2,1)} %bitcast.7), calls=%async_computation.2 | async-start | bytes 65536 | tf_op jit(solution)/shard_map/all_to_all | solution.py:92
  72.4 4.9 %copy-start.6 = (bf16[8,32,4096]{2,1,0:T(8,128)(2,1)S(1)}, bf16[8,32,4096]{2,1,0:T(8,128)(2,1)}, u32[]{:S(2)}) copy-start(bf16[8,32,4096]{2,1,0:T(8,128)(2,1)} %gather_fusion.1) | copy-start | bytes 6291460
  72.4 65.9 %all-to-all-start.1 = ((bf16[4,256,1280]{2,1,0:T(8,128)(2,1)}), bf16[4,256,1280]{2,1,0:T(8,128)(2,1)}, u32[]{:S(2)}, u32[]{:S(2)}) async-start(bf16[4,256,1280]{2,1,0:T(8,128)(2,1)} %pad_maximum_fusion), calls=%async_computation.1 | async-start | bytes 5242880 | tf_op jit(solution)/shard_map/all_to_all | solution.py:90
  138.3 70.0 %all-to-all-start.5 = ((bf16[8,32,4096]{2,1,0:T(8,128)(2,1)}), bf16[8,32,4096]{2,1,0:T(8,128)(2,1)S(1)}, u32[]{:S(2)}, u32[]{:S(2)}) async-start(bf16[8,32,4096]{2,1,0:T(8,128)(2,1)} %broadcast_select_fusion.1), calls=%async_computation.5 | async-start | bytes 4194304 | tf_op jit(solution)/shard_map/all_to_all | solution.py:73
  156.2 2.1 copy-start.4
  159.8 14.9 %collective-permute-start.1 = (f32[9,128]{1,0:T(8,128)}, f32[9,128]{1,0:T(8,128)S(1)}, u32[]{:S(2)}, u32[]{:S(2)}) collective-permute-start(f32[9,128]{1,0:T(8,128)} %bitcast.19), channel_id=1, source_target_pairs={{0,4},{4,8},{8,12},{1,5},{5,9},{9,13},{2,6},{6,10},{10,14},{3,7},{... | collective-permute-start | bytes 13832 | tf_op jit(solution)/shard_map/ppermute | solution.py:140
  163.2 16.0 %collective-permute-start.3 = (f32[9,128]{1,0:T(8,128)}, f32[9,128]{1,0:T(8,128)}, u32[]{:S(2)}, u32[]{:S(2)}) collective-permute-start(f32[9,128]{1,0:T(8,128)} %bitcast.19), channel_id=1, source_target_pairs={{0,8},{4,12},{1,9},{5,13},{2,10},{6,14},{3,11},{7,15},{16,24},{20,... | collective-permute-start | bytes 13832 | tf_op jit(solution)/shard_map/ppermute | solution.py:140
  168.7 24.7 %collective-permute-start = (s16[16,64,128]{2,1,0:T(8,128)(2,1)S(1)}, s16[16,64,128]{2,1,0:T(8,128)(2,1)}, u32[]{:S(2)}, u32[]{:S(2)}) collective-permute-start(s16[16,64,128]{2,1,0:T(8,128)(2,1)S(1)} %clamp_convert_fusion.1), channel_id=1, source_target_pairs={{0,4},{4,8},{8,12},{1,5},{5,9},{9,13},{2,6},{6,10},{10,14},{3,7},{... | collective-permute-start | bytes 786440 | tf_op jit(solution)/shard_map/ppermute | solution.py:139
  170.7 22.7 %collective-permute-start.2 = (s16[16,64,128]{2,1,0:T(8,128)(2,1)S(1)}, s16[16,64,128]{2,1,0:T(8,128)(2,1)}, u32[]{:S(2)}, u32[]{:S(2)}) collective-permute-start(s16[16,64,128]{2,1,0:T(8,128)(2,1)S(1)} %clamp_convert_fusion.1), channel_id=1, source_target_pairs={{0,8},{4,12},{1,9},{5,13},{2,10},{6,14},{3,11},{7,15},{16,24},{20,... | collective-permute-start | bytes 786440 | tf_op jit(solution)/shard_map/ppermute | solution.py:139
  172.7 20.7 %collective-permute-start.4 = (s16[16,64,128]{2,1,0:T(8,128)(2,1)S(1)}, s16[16,64,128]{2,1,0:T(8,128)(2,1)}, u32[]{:S(2)}, u32[]{:S(2)}) collective-permute-start(s16[16,64,128]{2,1,0:T(8,128)(2,1)S(1)} %clamp_convert_fusion.1), channel_id=1, source_target_pairs={{0,12},{1,13},{2,14},{3,15},{16,28},{17,29},{18,30},{19,31},{32,44... | collective-permute-start | bytes 786440 | tf_op jit(solution)/shard_map/ppermute | solution.py:139
  174.6 3.2 %copy-start.9 = (f32[9,128]{1,0:T(8,128)}, f32[9,128]{1,0:T(8,128)S(1)}, u32[]{:S(2)}) copy-start(f32[9,128]{1,0:T(8,128)S(1)} %collective-permute-done.1) | copy-start | bytes 13828
  174.6 15.4 %collective-permute-start.5 = (f32[9,128]{1,0:T(8,128)}, f32[9,128]{1,0:T(8,128)}, u32[]{:S(2)}, u32[]{:S(2)}) collective-permute-start(f32[9,128]{1,0:T(8,128)} %bitcast.19), channel_id=1, source_target_pairs={{0,12},{1,13},{2,14},{3,15},{16,28},{17,29},{18,30},{19,31},{32,44... | collective-permute-start | bytes 13832 | tf_op jit(solution)/shard_map/ppermute | solution.py:140
  198.0 3.1 copy-start.5
  198.0 3.1 copy-start.7
  198.0 3.1 copy-start.11
  208.2 9.6 %all-to-all-start.4 = ((f32[4,256,16]{1,2,0:T(8,128)}), f32[4,256,16]{1,2,0:T(8,128)S(1)}, u32[]{:S(2)}, u32[]{:S(2)}) async-start(f32[4,256,16]{1,2,0:T(8,128)} %get-tuple-element.11), calls=%async_computation.4 | async-start | bytes 131072 | tf_op jit(solution)/shard_map/all_to_all | solution.py:22
  217.8 47.9 %all-to-all-start.3 = ((s16[4,256,1024]{1,2,0:T(8,128)(2,1)}), s16[4,256,1024]{1,2,0:T(8,128)(2,1)}, u32[]{:S(2)}, u32[]{:S(2)}) async-start(s16[4,256,1024]{1,2,0:T(8,128)(2,1)} %bitcast.103), calls=%async_computation.3 | async-start | bytes 4194304 | tf_op jit(solution)/shard_map/all_to_all | solution.py:19
  275.6 4.8 %copy-start.3 = (f32[256,4096]{1,0:T(8,128)S(1)}, f32[256,4096]{1,0:T(8,128)}, u32[]{:S(2)}) copy-start(f32[256,4096]{1,0:T(8,128)} %copy.75) | copy-start | bytes 12582916
  275.6 4.8 %copy-start.8 = (f32[1,4096]{1,0:T(1,128)S(1)}, f32[1,4096]{1,0:T(1,128)}, u32[]{:S(2)}) copy-start(f32[1,4096]{1,0:T(1,128)} %param.16) | copy-start | bytes 49156
  283.5 1.6 copy-start.2
  285.1 16.8 %copy-start.1 = (bf16[256,4096]{1,0:T(8,128)(2,1)S(1)}, bf16[256,4096]{1,0:T(8,128)(2,1)}, u32[]{:S(2)}) copy-start(bf16[256,4096]{1,0:T(8,128)(2,1)} %param.10) | copy-start | bytes 6291460
Sparse Core Ops, SparseCore 0:
  9.4 257.0 all-gather.2

commit v11 on v9

--- a/solution.py
+++ b/solution.py
@@ -40,37 +40,28 @@
     def arrange(value_rows):
         return jnp.take(value_rows.reshape(groups, seg_rows, value_rows.shape[-1]), order, axis=0)
 
-    pad = (-log_decay.shape[1]) % 128
-    packed = jnp.concatenate(
-        [tokens_x, in_b, in_c, log_decay, jnp.zeros((rows, pad), log_decay.dtype)], axis=1
+    local = width // nz
+    lheads = heads // nz
+    lanes = 128
+    xpart = jnp.transpose(arrange(tokens_x).reshape(groups, seg_rows, nz, local), (0, 2, 1, 3))
+    lpart = jnp.transpose(arrange(log_decay).reshape(groups, seg_rows, nz, lheads), (0, 2, 1, 3))
+    lpart = jnp.pad(lpart, ((0, 0), (0, 0), (0, 0), (0, lanes - lheads)))
+    side = jnp.broadcast_to(
+        arrange(jnp.concatenate([in_b, in_c], axis=1))[:, None], (groups, nz, seg_rows, 2 * nstate)
     )
-    packed = lax.all_to_all(arrange(packed), "dom", split_axis=0, concat_axis=0, tiled=True)
-    packed = packed.reshape(rows, packed.shape[-1])
+    routed = jnp.concatenate([xpart, side, lpart], axis=3)
+    routed = routed.reshape(groups * nz, seg_rows, routed.shape[-1])
+    routed = lax.all_to_all(routed, ("dom", "sz"), split_axis=0, concat_axis=0, tiled=True)
+    routed = jnp.transpose(routed.reshape(groups, nz, seg_rows, routed.shape[-1]), (1, 0, 2, 3))
+    routed = routed.reshape(nz * rows, routed.shape[-1])
     zs = lax.all_to_all(arrange(gate_z), "dom", split_axis=0, concat_axis=0, tiled=True)
     zs = zs.reshape(rows, width)
-    xs = packed[:, :width]
-    bs = packed[:, width : width + nstate]
-    cs = packed[:, width + nstate : width + 2 * nstate]
-    ls = packed[:, width + 2 * nstate : width + 2 * nstate + heads]
-
-    local = width // nz
-    lheads = heads // nz
-    xbc = jnp.concatenate(
-        [
-            jnp.transpose(xs.reshape(rows, nz, local), (1, 0, 2)),
-            jnp.broadcast_to(bs[None], (nz, rows, nstate)),
-            jnp.broadcast_to(cs[None], (nz, rows, nstate)),
-        ],
-        axis=2,
-    )
-    xbc = lax.all_to_all(xbc, "sz", split_axis=0, concat_axis=0, tiled=True)
-    lsh = jnp.transpose(ls.reshape(rows, nz, lheads), (1, 0, 2))
-    lsh = lax.all_to_all(lsh, "sz", split_axis=0, concat_axis=0, tiled=True)
 
     blocks = nz * rows // SPAN
-    xc = xbc[:, :, :local].reshape(blocks, SPAN, lheads, hsize)
-    bc = xbc[:, :, local : local + nstate].reshape(blocks, SPAN, nstate)
-    cc = xbc[:, :, local + nstate :].reshape(blocks, SPAN, nstate)
+    xc = routed[:, :local].reshape(blocks, SPAN, lheads, hsize)
+    bc = routed[:, local : local + nstate].reshape(blocks, SPAN, nstate)
+    cc = routed[:, local + nstate : local + 2 * nstate].reshape(blocks, SPAN, nstate)
+    lsh = routed[:, local + 2 * nstate : local + 2 * nstate + lheads]
     cum = jnp.cumsum(lsh.astype(jnp.float32).reshape(blocks, SPAN, lheads), axis=1)
     scores = jnp.einsum("cin,cjn->cij", cc, bc, preferred_element_type=jnp.float32)
     cum_heads = jnp.transpose(cum, (0, 2, 1))
@@ -104,7 +95,6 @@
     coded = jnp.clip(
         jnp.round(local_end / jnp.where(scale > 0, scale, 1.0)), -32767.0, 32767.0
     ).astype(jnp.int16)
-    lanes = 128
     side = jnp.concatenate(
         [scale.reshape(-1), shard_total, jnp.zeros((lanes - lheads,), jnp.float32)]
     ).reshape(-1, lanes)

time: 302 us -> 295 us (0.977)
  starting transfers between devices: 42.6 us -> 37.8 us
  local copies, waits for them, and re-layouts: 56 us -> 59.2 us
    all_to_all x3 -> x1, waiting for transfers between devices: 81.8 us -> 38.8 us  [per_device(): lax.all_to_all(routed, ('dom', 'sz'), split_axis=0, concat_axis=0, tiled=...]
    all_gather x1, waiting for transfers between devices: 0.01 us -> 31.7 us  [per_device(): lax.all_gather(out_weight[0], SEQ, axis=1, tiled=True)]
    reshape x1 -> x3, local copies, waits for them, and re-layouts: 3.99 us -> 15.6 us  [the longest x2 12.2 us: per_device(): xc = routed[:, :local].reshape(blocks, SPAN, lheads, hsize)]
    ppermute x3, waiting for transfers between devices: 0.01 us -> 11.1 us  [per_device(): piece = lax.ppermute(coded, 'sx', route).astype(jnp.float32)]
    slice x9 -> x5, local copies, waits for them, and re-layouts: 14 us -> 2.95 us  [the longest x1 1.65 us: per_device(): xc = routed[:, :local].reshape(blocks, SPAN, lheads, hsize)]
    all_to_all x1, waiting for transfers between devices: 22.7 us -> 31.2 us  [code16(): lax.all_to_all(coded.astype(jnp.int16).reshape(*lead, -1), axis_name, spl...]
    ppermute x3, waiting for transfers between devices: 8.22 us -> 0.01 us  [per_device(): got = lax.ppermute(side, 'sx', route).reshape(-1)]
    all_to_all x3 -> x1, starting transfers between devices: 14.8 us -> 8.76 us  [per_device(): lax.all_to_all(routed, ('dom', 'sz'), split_axis=0, concat_axis=0, tiled=...]
  transfers between devices with their start and end apart: 13 -> 11, of which waited for: 5 -> 6; matrix products, arithmetic and copies ran while one was open for 36% -> 36% of each run, Pallas kernels for 0% -> 0%
where the time goes in v11:
time: 295 us; the launch traced here: 293 us
  waiting for transfers between devices  116 us (39%)
  local copies, waits for them, and re-layouts  59.2 us (20%)
  starting transfers between devices  37.8 us (13%)
  matrix products  34.3 us (12%)
  other arithmetic  32.7 us (11%)
  between operations  13.8 us (5%)
    all_to_all x1, waiting for transfers between devices, per_device(): lax.all_to_all(routed, ('dom', 'sz'), split_axis=0, concat_axis=0, tiled=...  38.8 us
    all_gather x1, waiting for transfers between devices, per_device(): lax.all_gather(out_weight[0], SEQ, axis=1, tiled=True)  31.7 us
    all_to_all x1, waiting for transfers between devices, code16(): lax.all_to_all(coded.astype(jnp.int16).reshape(*lead, -1), axis_name, spl...  31.2 us
    dot_general x1, matrix products, per_device(): jnp.dot(normed, lax.all_gather(out_weight[0], SEQ, axis=1, tiled=True), p...  16.8 us
    convert_element_type x3, local copies, waits for them, and re-layouts, per_device(): gated = ys * jax.nn.silu(zs.astype(jnp.float32))  15.4 us
    reshape x2, local copies, waits for them, and re-layouts, per_device(): xc = routed[:, :local].reshape(blocks, SPAN, lheads, hsize)  12.2 us
    ppermute x3, starting transfers between devices, per_device(): got = lax.ppermute(side, 'sx', route).reshape(-1)  11.9 us
    ppermute x3, waiting for transfers between devices, per_device(): piece = lax.ppermute(coded, 'sx', route).astype(jnp.float32)  11.1 us
  transfers between devices with their start and end apart: 11, of which 6 were waited for; matrix products, arithmetic and copies ran while one was open for 36% of the time, Pallas kernels for 0%

profile of v11, /device:TPU:0, one launch (start us, length us, event | category | flops | bytes accessed | tf_op | source)
XLA Modules:
  0.0 293.3 jit_solution(4907690432914071354)
XLA Ops:
  6.5 0.7 all-gather.3.cloned.1.call-update
  7.3 1.6 sort.17
  8.9 2.0 gather_fusion.2
  10.9 3.7 %gather_fusion.3 = bf16[8,32,4096]{2,1,0:T(8,128)(2,1)} fusion(bf16[8,32,4096]{2,1,0:T(8,128)(2,1)} %bitcast.117, s32[1024]{0:T(1024)S(1)} %pad_clamp_fusion), kind=kCustom, calls=%fused_computation.1.clone | custom fusion | bytes 4194336 | tf_op jit(solution)/shard_map/jit(_take)/gather | solution.py:41
  14.7 4.1 %broadcast_select_fusion = (bf16[8,32,4096]{2,1,0:T(8,128)(2,1)}, bf16[8,32,4096]{2,1,0:T(8,128)(2,1)}) fusion(bf16[8,32,4096]{2,1,0:T(8,128)(2,1)} %gather_fusion.3, pred[8]{0:T(512)(128)(4,1)S(1)} %compare_and_fusion, bf16[8,32,4096]{2,1,0:T(8,128)(2,1)S(1)} %copy-done.7), kind=kLoop, calls=%fused_computation.40 | loop fusion | flops 2097152 | bytes 8388616 | tf_op jit(solution)/shard_map/jit(_take)/select_n | solution.py:41
  18.7 3.4 %reshape.236 = bf16[8,32,4,1024]{3,2,1,0:T(4,128)(2,1)S(1)} reshape(bf16[8,32,4096]{2,1,0:T(8,128)(2,1)} %get-tuple-element.23) | data formatting | bytes 4194304 | tf_op jit(solution)/shard_map/reshape | solution.py:46
  22.2 0.6 gather_fusion
  22.9 0.6 gather_fusion.1
  24.3 1.6 fusion.22
  25.9 2.0 copy.62
  27.8 8.8 %all-to-all-start = ((bf16[32,32,1408]{2,1,0:T(8,128)(2,1)}), bf16[32,32,1408]{2,1,0:T(8,128)(2,1)}, u32[]{:S(2)}, u32[]{:S(2)}) async-start(bf16[32,32,1408]{2,1,0:T(8,128)(2,1)} %bitcast.108), calls=%async_computation | async-start | bytes 5767168 | tf_op jit(solution)/shard_map/all_to_all | solution.py:54
  36.7 0.6 dynamic-slice_bitcast_fusion
  37.2 0.7 iota_compare_fusion.1
  37.9 38.8 %all-to-all-done = bf16[32,32,1408]{2,1,0:T(8,128)(2,1)} async-done(((bf16[32,32,1408]{2,1,0:T(8,128)(2,1)}), bf16[32,32,1408]{2,1,0:T(8,128)(2,1)}, u32[]{:S(2)}, u32[]{:S(2)}) %all-to-all-start) | async-done | bytes 2883616 | tf_op jit(solution)/shard_map/all_to_all | solution.py:54
  76.7 5.3 %all-to-all-start.3 = ((bf16[8,32,4096]{2,1,0:T(8,128)(2,1)}), bf16[8,32,4096]{2,1,0:T(8,128)(2,1)S(1)}, u32[]{:S(2)}, u32[]{:S(2)}) async-start(bf16[8,32,4096]{2,1,0:T(8,128)(2,1)} %get-tuple-element.22), calls=%async_computation.3 | async-start | bytes 4194304 | tf_op jit(solution)/shard_map/all_to_all | solution.py:57
  82.0 2.1 copy.63
  84.1 1.5 copy-done.4
  85.7 1.7 slice.67
  87.6 2.3 reduce-window.6
  90.1 6.4 %reshape.306 = bf16[4,256,16,64]{3,2,1,0:T(8,128)(2,1)} reshape(bf16[1024,1024]{1,0:T(8,128)(2,1)} %slice.67) | data formatting | bytes 4194304 | tf_op jit(solution)/shard_map/reshape | solution.py:61
  96.5 5.8 %copy.71 = bf16[4,256,16,64]{1,3,2,0:T(8,128)(2,1)} copy(bf16[4,256,16,64]{3,2,1,0:T(8,128)(2,1)} %reshape.306) | data formatting | bytes 4194304 | tf_op jit(solution)/shard_map/reshape | solution.py:61
  102.4 0.2 slice_reduce_fusion
  102.6 0.3 fusion.31
  103.1 1.1 fusion.41
  104.2 2.4 fusion.23
  106.6 5.0 %convolution_bitcast_fusion = f32[5,16,64,128]{3,0,2,1:T(8,128)S(1)} fusion(f32[16,5,4,1]{1,2,3,0:T(4,128)S(1)} %copy.82, f32[4,16,64,128]{3,2,1,0:T(8,128)S(1)} %fusion.23), kind=kOutput, calls=%fused_computation.33 | convolution fusion | flops 31457280 | bytes 4719872 | tf_op jit(solution)/shard_map/hkj,jhpn->khpn/dot_general | solution.py:88
  111.6 2.1 copy-done.5
  113.6 0.6 slice.75
  114.5 0.7 concatenate.11
  115.1 4.1 %collective-permute-start.1 = (f32[9,128]{1,0:T(8,128)}, f32[9,128]{1,0:T(8,128)}, u32[]{:S(2)}, u32[]{:S(2)}) collective-permute-start(f32[9,128]{1,0:T(8,128)} %bitcast.24), channel_id=1, source_target_pairs={{0,4},{4,8},{8,12},{1,5},{5,9},{9,13},{2,6},{6,10},{10,14},{3,7},{... | collective-permute-start | bytes 13832 | tf_op jit(solution)/shard_map/ppermute | solution.py:106
  119.2 5.9 %collective-permute-start.3 = (f32[9,128]{1,0:T(8,128)}, f32[9,128]{1,0:T(8,128)}, u32[]{:S(2)}, u32[]{:S(2)}) collective-permute-start(f32[9,128]{1,0:T(8,128)} %bitcast.24), channel_id=1, source_target_pairs={{0,8},{4,12},{1,9},{5,13},{2,10},{6,14},{3,11},{7,15},{16,24},{20,... | collective-permute-start | bytes 13832 | tf_op jit(solution)/shard_map/ppermute | solution.py:106
  125.1 1.9 collective-permute-start.5
  127.2 1.3 collective-permute-start
  128.5 1.3 collective-permute-start.2
  129.8 1.3 fusion.42
  131.2 1.5 collective-permute-start.4
  132.8 1.3 slice.76
  134.1 0.7 mul.148
  134.8 1.3 slice.78
  136.1 1.3 mul.152
  137.4 1.3 slice.80
  138.7 1.3 mul.157
  140.0 0.7 slice_exponential_fusion
  140.8 11.0 %collective-permute-done.2 = s16[16,64,128]{2,1,0:T(8,128)(2,1)S(1)} collective-permute-done((s16[16,64,128]{2,1,0:T(8,128)(2,1)S(1)}, s16[16,64,128]{2,1,0:T(8,128)(2,1)S(1)}, u32[]{:S(2)}, u32[]{:S(2)}) %collective-permute-start.2) | collective-permute-done | bytes 262176 | tf_op jit(solution)/shard_map/ppermute | solution.py:105
  151.8 1.2 multiply_add_fusion
  153.1 3.0 %slice_add_fusion = f32[4,16,64,128]{3,0,2,1:T(4,128)S(1)} fusion(f32[5,16,64,128]{3,0,2,1:T(8,128)} %copy-done.5, f32[16,64,128]{2,1,0:T(8,128)S(1)} %multiply_add_fusion, f32[4,16]{0,1:T(8,128)S(1)} %copy.75), kind=kLoop, calls=%fused_computation.35 | loop fusion | flops 1048576 | bytes 4718848 | tf_op jit(solution)/shard_map/add | solution.py:111
  156.2 1.9 fusion.25
  158.1 6.7 %abs_reduce_fusion = (f32[4,256,16]{1,2,0:T(8,128)S(1)}, f32[4,256,16,64]{1,3,2,0:T(8,128)}) fusion(bf16[4,256,16,64]{1,3,2,0:T(8,128)(2,1)S(1)} %copy-done.6, f32[16]{0:T(128)S(1)} %copy-done.15, f32[4,256,16,64]{1,3,2,0:T(8,128)S(1)} %fusion.25, f32[4,256,16]{1,2,0:T(8,128)S(1)} %get-tuple-element.14, f32[4,16,256]{2,1,0:T(8,128)S(1)} %get-tuple-element.16, ...), kind=kOutput, calls=%fused_computation.31 | convolution fusion | flops 565166080 | bytes 11796544 | tf_op jit(solution)/shard_map/chij,cjhp->cihp/dot_general | solution.py:73
  164.7 0.6 broadcast_multiply_fusion
  165.4 3.3 %all-to-all-start.2 = ((f32[4,256,16]{1,2,0:T(8,128)}), f32[4,256,16]{1,2,0:T(8,128)S(1)}, u32[]{:S(2)}, u32[]{:S(2)}) async-start(f32[4,256,16]{1,2,0:T(8,128)} %get-tuple-element.12), calls=%async_computation.2 | async-start | bytes 131072 | tf_op jit(solution)/shard_map/all_to_all | solution.py:20
  168.7 4.4 %clamp_convert_fusion = s16[4,256,16,64]{1,3,2,0:T(8,128)(2,1)} fusion(f32[4,256,16,64]{1,3,2,0:T(8,128)} %get-tuple-element.25, f32[4,256,16]{1,2,0:T(8,128)S(1)} %get-tuple-element.13), kind=kLoop, calls=%fused_computation.30 | loop fusion | flops 4194304 | bytes 6356992 | tf_op jit(solution)/shard_map/convert_element_type | solution.py:18
  173.1 2.0 all-to-all-done.2
  175.1 4.5 %all-to-all-start.1 = ((s16[4,256,1024]{1,2,0:T(8,128)(2,1)}), s16[4,256,1024]{1,2,0:T(8,128)(2,1)}, u32[]{:S(2)}, u32[]{:S(2)}) async-start(s16[4,256,1024]{1,2,0:T(8,128)(2,1)} %bitcast.109), calls=%async_computation.1 | async-start | bytes 4194304 | tf_op jit(solution)/shard_map/all_to_all | solution.py:17
  179.6 4.5 %reshape.257 = f32[256,4,1024]{2,1,0:T(4,128)} reshape(bf16[8,32,4096]{2,1,0:T(8,128)(2,1)S(1)} %all-to-all-done.3) | data formatting | bytes 6291456 | tf_op jit(solution)/shard_map/convert_element_type | solution.py:125
  184.1 5.2 %copy.80 = f32[256,4,1024]{0,2,1:T(8,128)} copy(f32[256,4,1024]{2,1,0:T(4,128)} %reshape.257) | data formatting | bytes 8388608 | tf_op jit(solution)/shard_map/convert_element_type | solution.py:125
  189.3 2.4 convert_element_type.67
  191.8 5.6 %copy.78 = f32[256,4096]{0,1:T(8,128)} copy(f32[256,4096]{1,0:T(8,128)} %bitcast.104) | data formatting | bytes 8388608 | tf_op jit(solution)/shard_map/convert_element_type | solution.py:125
  197.4 31.2 %all-to-all-done.1 = s16[4,256,1024]{1,2,0:T(8,128)(2,1)} async-done(((s16[4,256,1024]{1,2,0:T(8,128)(2,1)}), s16[4,256,1024]{1,2,0:T(8,128)(2,1)}, u32[]{:S(2)}, u32[]{:S(2)}) %all-to-all-start.1) | async-done | bytes 2097184 | tf_op jit(solution)/shard_map/all_to_all | solution.py:17
  228.5 2.5 bitcast_multiply_fusion.2
  231.0 0.6 copy-done.2
  231.6 3.6 %fusion.21 = f32[256]{0:T(256)S(1)} fusion(f32[256,4,1024]{0,2,1:T(8,128)S(1)} %copy-done.2, f32[4,256,16]{1,2,0:T(8,128)S(1)} %all-to-all-done.2, s16[4,256,1024]{1,2,0:T(8,128)(2,1)} %all-to-all-done.1), kind=kLoop, calls=%fused_computation.27 | loop fusion | flops 9436928 | bytes 6358016 | tf_op jit(solution)/shard_map/reduce_sum | solution.py:128
  235.3 2.7 fusion.19
  238.0 31.7 %all-gather.3.cloned.1.call-done = bf16[1,4096,4096]{2,1,0:T(8,128)(2,1)} async-done(((bf16[1,4096,256]{2,1,0:T(8,128)(2,1)}), bf16[1,4096,4096]{2,1,0:T(8,128)(2,1)}) %all-gather.3.cloned.1.call-update) | async-done | bytes 33554448 | tf_op jit(solution)/shard_map/all_gather | solution.py:133
  269.7 16.8 %fusion.12 = bf16[1,256,4096]{2,1,0:T(8,128)(2,1)} fusion(bf16[256,4096]{0,1:T(8,128)(2,1)} %fusion.19, bf16[1,4096,4096]{2,1,0:T(8,128)(2,1)} %all-gather.3.cloned.1.call-done), kind=kOutput, calls=%fused_computation.18 | convolution fusion | flops 8590983168 | bytes 37748736 | tf_op jit(solution)/shard_map/dot_general | solution.py:131
  (71 shorter events, 2.5 us)
Async XLA Ops:
  6.5 2.4 copy-start
  6.5 263.2 %all-gather.3.cloned.1.call-start = ((), (), s32[]{:S(2)}) async-start(), calls=%async_computation.4 | async-start | bytes 35651584 | tf_op jit(solution)/shard_map/all_gather | solution.py:133
  10.9 3.8 %copy-start.7 = (bf16[8,32,4096]{2,1,0:T(8,128)(2,1)S(1)}, bf16[8,32,4096]{2,1,0:T(8,128)(2,1)}, u32[]{:S(2)}) copy-start(bf16[8,32,4096]{2,1,0:T(8,128)(2,1)} %gather_fusion.2) | copy-start | bytes 6291460
  18.7 3.5 %copy-start.10 = (bf16[256,128]{1,0:T(8,128)(2,1)S(1)}, bf16[256,128]{1,0:T(8,128)(2,1)}, u32[]{:S(2)}) copy-start(bf16[256,128]{1,0:T(8,128)(2,1)} %param.14) | copy-start | bytes 196612
  18.7 3.5 %copy-start.11 = (bf16[256,128]{1,0:T(8,128)(2,1)S(1)}, bf16[256,128]{1,0:T(8,128)(2,1)}, u32[]{:S(2)}) copy-start(bf16[256,128]{1,0:T(8,128)(2,1)} %param.13) | copy-start | bytes 196612
  18.7 4.1 %copy-start.12 = (bf16[256,64]{0,1:T(8,128)(2,1)S(1)}, bf16[256,64]{0,1:T(8,128)(2,1)}, u32[]{:S(2)}) copy-start(bf16[256,64]{0,1:T(8,128)(2,1)} %param.15) | copy-start | bytes 98308
  27.8 8.8 %copy-start.14 = (f32[1,64]{1,0:T(1,128)S(1)}, f32[1,64]{1,0:T(1,128)}, u32[]{:S(2)}) copy-start(f32[1,64]{1,0:T(1,128)} %param.19) | copy-start | bytes 772
  27.8 48.8 %all-to-all-start = ((bf16[32,32,1408]{2,1,0:T(8,128)(2,1)}), bf16[32,32,1408]{2,1,0:T(8,128)(2,1)}, u32[]{:S(2)}, u32[]{:S(2)}) async-start(bf16[32,32,1408]{2,1,0:T(8,128)(2,1)} %bitcast.108), calls=%async_computation | async-start | bytes 5767168 | tf_op jit(solution)/shard_map/all_to_all | solution.py:54
  76.7 88.7 %all-to-all-start.3 = ((bf16[8,32,4096]{2,1,0:T(8,128)(2,1)}), bf16[8,32,4096]{2,1,0:T(8,128)(2,1)S(1)}, u32[]{:S(2)}, u32[]{:S(2)}) async-start(bf16[8,32,4096]{2,1,0:T(8,128)(2,1)} %get-tuple-element.22), calls=%async_computation.3 | async-start | bytes 4194304 | tf_op jit(solution)/shard_map/all_to_all | solution.py:57
  84.1 1.6 copy-start.4
  111.6 2.1 copy-start.5
  115.1 16.0 %collective-permute-start.1 = (f32[9,128]{1,0:T(8,128)}, f32[9,128]{1,0:T(8,128)}, u32[]{:S(2)}, u32[]{:S(2)}) collective-permute-start(f32[9,128]{1,0:T(8,128)} %bitcast.24), channel_id=1, source_target_pairs={{0,4},{4,8},{8,12},{1,5},{5,9},{9,13},{2,6},{6,10},{10,14},{3,7},{... | collective-permute-start | bytes 13832 | tf_op jit(solution)/shard_map/ppermute | solution.py:106
  119.2 15.6 %collective-permute-start.3 = (f32[9,128]{1,0:T(8,128)}, f32[9,128]{1,0:T(8,128)}, u32[]{:S(2)}, u32[]{:S(2)}) collective-permute-start(f32[9,128]{1,0:T(8,128)} %bitcast.24), channel_id=1, source_target_pairs={{0,8},{4,12},{1,9},{5,13},{2,10},{6,14},{3,11},{7,15},{16,24},{20,... | collective-permute-start | bytes 13832 | tf_op jit(solution)/shard_map/ppermute | solution.py:106
  125.1 12.3 %collective-permute-start.5 = (f32[9,128]{1,0:T(8,128)}, f32[9,128]{1,0:T(8,128)}, u32[]{:S(2)}, u32[]{:S(2)}) collective-permute-start(f32[9,128]{1,0:T(8,128)} %bitcast.24), channel_id=1, source_target_pairs={{0,12},{1,13},{2,14},{3,15},{16,28},{17,29},{18,30},{19,31},{32,44... | collective-permute-start | bytes 13832 | tf_op jit(solution)/shard_map/ppermute | solution.py:106
  127.2 13.6 %collective-permute-start = (s16[16,64,128]{2,1,0:T(8,128)(2,1)S(1)}, s16[16,64,128]{2,1,0:T(8,128)(2,1)S(1)}, u32[]{:S(2)}, u32[]{:S(2)}) collective-permute-start(s16[16,64,128]{2,1,0:T(8,128)(2,1)S(1)} %clamp_convert_fusion.1), channel_id=1, source_target_pairs={{0,4},{4,8},{8,12},{1,5},{5,9},{9,13},{2,6},{6,10},{10,14},{3,7},{... | collective-permute-start | bytes 786440 | tf_op jit(solution)/shard_map/ppermute | solution.py:105
  128.5 23.3 %collective-permute-start.2 = (s16[16,64,128]{2,1,0:T(8,128)(2,1)S(1)}, s16[16,64,128]{2,1,0:T(8,128)(2,1)S(1)}, u32[]{:S(2)}, u32[]{:S(2)}) collective-permute-start(s16[16,64,128]{2,1,0:T(8,128)(2,1)S(1)} %clamp_convert_fusion.1), channel_id=1, source_target_pairs={{0,8},{4,12},{1,9},{5,13},{2,10},{6,14},{3,11},{7,15},{16,24},{20,... | collective-permute-start | bytes 786440 | tf_op jit(solution)/shard_map/ppermute | solution.py:105
  131.2 20.7 %collective-permute-start.4 = (s16[16,64,128]{2,1,0:T(8,128)(2,1)S(1)}, s16[16,64,128]{2,1,0:T(8,128)(2,1)S(1)}, u32[]{:S(2)}, u32[]{:S(2)}) collective-permute-start(s16[16,64,128]{2,1,0:T(8,128)(2,1)S(1)} %clamp_convert_fusion.1), channel_id=1, source_target_pairs={{0,12},{1,13},{2,14},{3,15},{16,28},{17,29},{18,30},{19,31},{32,44... | collective-permute-start | bytes 786440 | tf_op jit(solution)/shard_map/ppermute | solution.py:105
  156.1 1.9 copy-start.6
  156.1 1.9 copy-start.8
  156.1 1.9 copy-start.9
  156.1 1.9 copy-start.15
  165.4 9.7 %all-to-all-start.2 = ((f32[4,256,16]{1,2,0:T(8,128)}), f32[4,256,16]{1,2,0:T(8,128)S(1)}, u32[]{:S(2)}, u32[]{:S(2)}) async-start(f32[4,256,16]{1,2,0:T(8,128)} %get-tuple-element.12), calls=%async_computation.2 | async-start | bytes 131072 | tf_op jit(solution)/shard_map/all_to_all | solution.py:20
  175.1 53.4 %all-to-all-start.1 = ((s16[4,256,1024]{1,2,0:T(8,128)(2,1)}), s16[4,256,1024]{1,2,0:T(8,128)(2,1)}, u32[]{:S(2)}, u32[]{:S(2)}) async-start(s16[4,256,1024]{1,2,0:T(8,128)(2,1)} %bitcast.109), calls=%async_computation.1 | async-start | bytes 4194304 | tf_op jit(solution)/shard_map/all_to_all | solution.py:17
  228.5 3.1 %copy-start.2 = (f32[256,4,1024]{0,2,1:T(8,128)S(1)}, f32[256,4,1024]{0,2,1:T(8,128)}, u32[]{:S(2)}) copy-start(f32[256,4,1024]{0,2,1:T(8,128)} %copy.80) | copy-start | bytes 12582916
  231.6 3.6 %copy-start.3 = (f32[256,4096]{0,1:T(8,128)S(1)}, f32[256,4096]{0,1:T(8,128)}, u32[]{:S(2)}) copy-start(f32[256,4096]{0,1:T(8,128)} %copy.78) | copy-start | bytes 12582916
  231.6 3.6 %copy-start.13 = (f32[1,4096]{1,0:T(1,128)S(1)}, f32[1,4096]{1,0:T(1,128)}, u32[]{:S(2)}) copy-start(f32[1,4096]{1,0:T(1,128)} %param.18) | copy-start | bytes 49156
  269.7 16.8 %copy-start.1 = (bf16[256,4096]{1,0:T(8,128)(2,1)S(1)}, bf16[256,4096]{1,0:T(8,128)(2,1)}, u32[]{:S(2)}) copy-start(bf16[256,4096]{1,0:T(8,128)(2,1)} %param.11) | copy-start | bytes 6291460
Sparse Core Ops, SparseCore 0:
  9.4 260.2 all-gather.2

commit v12 on v11

--- a/solution.py
+++ b/solution.py
@@ -44,24 +44,26 @@
     lheads = heads // nz
     lanes = 128
     xpart = jnp.transpose(arrange(tokens_x).reshape(groups, seg_rows, nz, local), (0, 2, 1, 3))
-    lpart = jnp.transpose(arrange(log_decay).reshape(groups, seg_rows, nz, lheads), (0, 2, 1, 3))
-    lpart = jnp.pad(lpart, ((0, 0), (0, 0), (0, 0), (0, lanes - lheads)))
     side = jnp.broadcast_to(
         arrange(jnp.concatenate([in_b, in_c], axis=1))[:, None], (groups, nz, seg_rows, 2 * nstate)
     )
-    routed = jnp.concatenate([xpart, side, lpart], axis=3)
+    routed = jnp.concatenate([xpart, side], axis=3)
     routed = routed.reshape(groups * nz, seg_rows, routed.shape[-1])
     routed = lax.all_to_all(routed, ("dom", "sz"), split_axis=0, concat_axis=0, tiled=True)
     routed = jnp.transpose(routed.reshape(groups, nz, seg_rows, routed.shape[-1]), (1, 0, 2, 3))
     routed = routed.reshape(nz * rows, routed.shape[-1])
-    zs = lax.all_to_all(arrange(gate_z), "dom", split_axis=0, concat_axis=0, tiled=True)
-    zs = zs.reshape(rows, width)
+    pad = (-log_decay.shape[1]) % lanes
+    zl = jnp.concatenate([gate_z, log_decay, jnp.zeros((rows, pad), log_decay.dtype)], axis=1)
+    zl = lax.all_to_all(arrange(zl), "dom", split_axis=0, concat_axis=0, tiled=True)
+    zl = zl.reshape(rows, zl.shape[-1])
+    zs = zl[:, :width]
+    lsh = jnp.transpose(zl[:, width : width + heads].reshape(rows, nz, lheads), (1, 0, 2))
+    lsh = lax.all_to_all(lsh, "sz", split_axis=0, concat_axis=0, tiled=True)
 
     blocks = nz * rows // SPAN
     xc = routed[:, :local].reshape(blocks, SPAN, lheads, hsize)
     bc = routed[:, local : local + nstate].reshape(blocks, SPAN, nstate)
     cc = routed[:, local + nstate : local + 2 * nstate].reshape(blocks, SPAN, nstate)
-    lsh = routed[:, local + 2 * nstate : local + 2 * nstate + lheads]
     cum = jnp.cumsum(lsh.astype(jnp.float32).reshape(blocks, SPAN, lheads), axis=1)
     scores = jnp.einsum("cin,cjn->cij", cc, bc, preferred_element_type=jnp.float32)
     cum_heads = jnp.transpose(cum, (0, 2, 1))

time: 295 us -> 292 us (0.990)
  blocking collectives: 0 us -> 46 us
  waiting for transfers between devices: 116 us -> 89.4 us
  local copies, waits for them, and re-layouts: 59.2 us -> 45.2 us
  starting transfers between devices: 37.8 us -> 33.2 us
  other arithmetic: 32.7 us -> 28.4 us
    all_to_all x0 -> x1, blocking collectives: none -> 46 us  [code16(): lax.all_to_all(coded.astype(jnp.int16).reshape(*lead, -1), axis_name, spl...]
    convert_element_type x3 -> x0, local copies, waits for them, and re-layouts: 15.4 us -> none  [per_device(): gated = ys * jax.nn.silu(zs.astype(jnp.float32))]
    ppermute x3, waiting for transfers between devices: 11.1 us -> 0.01 us  [per_device(): piece = lax.ppermute(coded, 'sx', route).astype(jnp.float32)]
    all_to_all x2, waiting for transfers between devices: 31.2 us -> 20.5 us  [the longest x1 18.2 us: per_device(): lax.all_to_all(arrange(zl), 'dom', split_axis=0, concat_axis=0, tiled=True)]
    ppermute x3, waiting for transfers between devices: 0.01 us -> 9.29 us  [per_device(): got = lax.ppermute(side, 'sx', route).reshape(-1)]
    all_gather x1, waiting for transfers between devices: 31.7 us -> 24 us  [per_device(): lax.all_gather(out_weight[0], SEQ, axis=1, tiled=True)]
    all_to_all x1, waiting for transfers between devices: 38.8 us -> 31.4 us  [per_device(): lax.all_to_all(routed, ('dom', 'sz'), split_axis=0, concat_axis=0, tiled=...]
    convert_element_type x2 -> x0, other arithmetic: 5.17 us -> none  [the longest x1 2.74 us: per_device(): normed = (gated * lax.rsqrt(jnp.mean(gated * gated, axis=-1, keepdims=Tru...]
  transfers between devices with their start and end apart: 11 -> 11, of which waited for: 6 -> 6; matrix products, arithmetic and copies ran while one was open for 36% -> 30% of each run, Pallas kernels for 0% -> 0%
where the time goes in v12:
time: 292 us; the launch traced here: 290 us
  waiting for transfers between devices  89.4 us (31%)
  blocking collectives  46 us (16%)
  local copies, waits for them, and re-layouts  45.2 us (15%)
  matrix products  34.5 us (12%)
  starting transfers between devices  33.2 us (11%)
  other arithmetic  28.4 us (10%)
  between operations  13.8 us (5%)
    all_to_all x1, blocking collectives, code16(): lax.all_to_all(coded.astype(jnp.int16).reshape(*lead, -1), axis_name, spl...  46 us
    all_to_all x1, waiting for transfers between devices, per_device(): lax.all_to_all(routed, ('dom', 'sz'), split_axis=0, concat_axis=0, tiled=...  31.4 us
    all_gather x1, waiting for transfers between devices, per_device(): lax.all_gather(out_weight[0], SEQ, axis=1, tiled=True)  24 us
    dot_general x1, matrix products, per_device(): jnp.dot(normed, lax.all_gather(out_weight[0], SEQ, axis=1, tiled=True), p...  18.8 us
    all_to_all x1, waiting for transfers between devices, per_device(): lax.all_to_all(arrange(zl), 'dom', split_axis=0, concat_axis=0, tiled=True)  18.2 us
    gather x4, local copies, waits for them, and re-layouts, arrange(): jnp.take(value_rows.reshape(groups, seg_rows, value_rows.shape[-1]), orde...  10.9 us
    ppermute x3, starting transfers between devices, per_device(): got = lax.ppermute(side, 'sx', route).reshape(-1)  10.3 us
    ppermute x3, waiting for transfers between devices, per_device(): got = lax.ppermute(side, 'sx', route).reshape(-1)  9.29 us
  transfers between devices with their start and end apart: 11, of which 6 were waited for; matrix products, arithmetic and copies ran while one was open for 30% of the time, Pallas kernels for 0%

profile of v12, /device:TPU:0, one launch (start us, length us, event | category | flops | bytes accessed | tf_op | source)
XLA Modules:
  0.0 290.5 jit_solution(5701310564195889606)
XLA Ops:
  6.5 0.7 all-gather.3.cloned.1.call-update
  7.3 0.9 copy.35
  8.1 1.6 sort.17
  9.8 4.5 %concatenate.14 = bf16[256,4224]{1,0:T(8,128)(2,1)} concatenate(bf16[256,4096]{1,0:T(8,128)(2,1)} %param.10, bf16[256,64]{1,0:T(8,128)(2,1)S(1)} %copy.35, bf16[256,64]{1,0:T(8,128)(2,1)S(1)} %broadcast_in_dim.104), dimensions={1} | concatenate | bytes 4325376 | tf_op jit(solution)/shard_map/concatenate | solution.py:56
  14.3 3.8 %gather_fusion.2 = bf16[8,32,4224]{2,1,0:T(8,128)(2,1)} fusion(bf16[8,32,4224]{2,1,0:T(8,128)(2,1)} %bitcast.94, s32[1024]{0:T(1024)S(1)} %pad_clamp_fusion), kind=kCustom, calls=%fused_computation.2 | custom fusion | bytes 4325408 | tf_op jit(solution)/shard_map/jit(_take)/gather | solution.py:41
  18.1 3.3 %broadcast_select_fusion = bf16[8,32,4224]{2,1,0:T(8,128)(2,1)} fusion(bf16[8,32,4224]{2,1,0:T(8,128)(2,1)} %gather_fusion.2, pred[8]{0:T(512)(128)(4,1)S(1)} %compare_and_fusion), kind=kLoop, calls=%fused_computation.31 | loop fusion | flops 1081344 | bytes 4325384 | tf_op jit(solution)/shard_map/jit(_take)/select_n | solution.py:41
  21.4 4.6 %all-to-all-start.1 = ((bf16[8,32,4224]{2,1,0:T(8,128)(2,1)}), bf16[8,32,4224]{2,1,0:T(8,128)(2,1)}, u32[]{:S(2)}, u32[]{:S(2)}) async-start(bf16[8,32,4224]{2,1,0:T(8,128)(2,1)} %broadcast_select_fusion), calls=%async_computation.1 | async-start | bytes 4325376 | tf_op jit(solution)/shard_map/all_to_all | solution.py:57
  26.0 2.0 gather_fusion
  28.0 4.5 %gather.15 = bf16[8,32,4,1024]{3,2,1,0:T(4,128)(2,1)} reshape(bf16[8,32,4096]{2,1,0:T(8,128)(2,1)} %gather_fusion) | data formatting | bytes 4194304 | tf_op jit(solution)/shard_map/jit(_take)/gather | solution.py:41
  32.5 0.6 gather_fusion.1
  33.2 2.6 select_bitcast_fusion
  35.8 18.2 %all-to-all-done.1 = bf16[8,32,4224]{2,1,0:T(8,128)(2,1)} async-done(((bf16[8,32,4224]{2,1,0:T(8,128)(2,1)}), bf16[8,32,4224]{2,1,0:T(8,128)(2,1)}, u32[]{:S(2)}, u32[]{:S(2)}) %all-to-all-start.1) | async-done | bytes 2162720 | tf_op jit(solution)/shard_map/all_to_all | solution.py:57
  53.9 0.8 slice.72
  54.8 0.7 copy.36
  55.5 5.3 %all-to-all-start.2 = ((bf16[4,256,16]{1,2,0:T(8,128)(2,1)}), bf16[4,256,16]{1,2,0:T(8,128)(2,1)S(1)}, u32[]{:S(2)}, u32[]{:S(2)}) async-start(bf16[4,256,16]{1,2,0:T(8,128)(2,1)} %bitcast.13), calls=%async_computation.2 | async-start | bytes 65536 | tf_op jit(solution)/shard_map/all_to_all | solution.py:61
  60.8 0.1 broadcast_in_dim.101
  60.9 1.2 pad_maximum_fusion
  62.2 2.0 copy.32
  64.2 2.3 all-to-all-done.2
  66.5 5.0 %all-to-all-start = ((bf16[32,32,1280]{2,1,0:T(8,128)(2,1)}), bf16[32,32,1280]{2,1,0:T(8,128)(2,1)}, u32[]{:S(2)}, u32[]{:S(2)}) async-start(bf16[32,32,1280]{2,1,0:T(8,128)(2,1)} %bitcast.91), calls=%async_computation | async-start | bytes 5242880 | tf_op jit(solution)/shard_map/all_to_all | solution.py:52
  71.5 0.6 dynamic-slice_bitcast_fusion
  72.1 0.6 iota_compare_fusion
  72.7 2.3 reduce-window.6
  75.3 0.2 slice_reduce_fusion
  75.6 0.3 fusion.30
  76.2 31.4 %all-to-all-done = bf16[32,32,1280]{2,1,0:T(8,128)(2,1)} async-done(((bf16[32,32,1280]{2,1,0:T(8,128)(2,1)}), bf16[32,32,1280]{2,1,0:T(8,128)(2,1)}, u32[]{:S(2)}, u32[]{:S(2)}) %all-to-all-start) | async-done | bytes 2621472 | tf_op jit(solution)/shard_map/all_to_all | solution.py:52
  107.6 1.9 copy.33
  109.6 1.4 copy-done.3
  111.0 0.3 slice.69
  111.3 4.0 %reshape.273 = bf16[4,256,16,64]{3,2,1,0:T(8,128)(2,1)} reshape(bf16[1024,1024]{1,0:T(8,128)(2,1)S(1)} %slice.69) | data formatting | bytes 4194304 | tf_op jit(solution)/shard_map/reshape | solution.py:64
  115.3 4.8 %copy.41 = bf16[4,256,16,64]{1,3,2,0:T(8,128)(2,1)S(1)} copy(bf16[4,256,16,64]{3,2,1,0:T(8,128)(2,1)} %reshape.273) | data formatting | bytes 4194304 | tf_op jit(solution)/shard_map/reshape | solution.py:64
  120.2 1.1 fusion.41
  121.3 0.7 fusion.20
  122.0 5.0 %convolution_bitcast_fusion = f32[5,16,64,128]{3,0,2,1:T(8,128)S(1)} fusion(f32[16,5,4,1]{1,2,3,0:T(4,128)S(1)} %copy.49, f32[4,16,64,128]{3,2,1,0:T(8,128)S(1)} %fusion.20), kind=kOutput, calls=%fused_computation.32 | convolution fusion | flops 31457280 | bytes 4719872 | tf_op jit(solution)/shard_map/hkj,jhpn->khpn/dot_general | solution.py:90
  127.0 2.0 copy-done.2
  129.0 0.6 slice.77
  129.6 0.2 abs_reduce_fusion.1
  129.9 0.7 concatenate.15
  130.5 3.3 %collective-permute-start.1 = (f32[9,128]{1,0:T(8,128)}, f32[9,128]{1,0:T(8,128)S(1)}, u32[]{:S(2)}, u32[]{:S(2)}) collective-permute-start(f32[9,128]{1,0:T(8,128)} %bitcast.25), channel_id=1, source_target_pairs={{0,4},{4,8},{8,12},{1,5},{5,9},{9,13},{2,6},{6,10},{10,14},{3,7},{... | collective-permute-start | bytes 13832 | tf_op jit(solution)/shard_map/ppermute | solution.py:108
  133.9 5.2 %collective-permute-start.3 = (f32[9,128]{1,0:T(8,128)}, f32[9,128]{1,0:T(8,128)}, u32[]{:S(2)}, u32[]{:S(2)}) collective-permute-start(f32[9,128]{1,0:T(8,128)} %bitcast.25), channel_id=1, source_target_pairs={{0,8},{4,12},{1,9},{5,13},{2,10},{6,14},{3,11},{7,15},{16,24},{20,... | collective-permute-start | bytes 13832 | tf_op jit(solution)/shard_map/ppermute | solution.py:108
  139.0 0.2 clamp_convert_fusion.1
  139.2 1.3 collective-permute-start
  140.6 1.3 collective-permute-start.2
  141.9 2.0 collective-permute-start.4
  143.9 1.9 collective-permute-start.5
  145.8 1.3 fusion.42
  147.1 0.7 slice.80
  147.9 9.3 %collective-permute-done.5 = f32[9,128]{1,0:T(8,128)} collective-permute-done((f32[9,128]{1,0:T(8,128)}, f32[9,128]{1,0:T(8,128)}, u32[]{:S(2)}, u32[]{:S(2)}) %collective-permute-start.5) | collective-permute-done | bytes 4640 | tf_op jit(solution)/shard_map/ppermute | solution.py:108
  157.2 0.7 slice.82
  157.9 0.7 slice_exponential_fusion
  158.6 1.5 multiply_add_fusion
  160.1 3.1 %slice_add_fusion = f32[4,16,64,128]{3,0,2,1:T(4,128)S(1)} fusion(f32[5,16,64,128]{3,0,2,1:T(8,128)} %copy-done.2, f32[16,64,128]{2,1,0:T(8,128)S(1)} %multiply_add_fusion, f32[4,16]{0,1:T(8,128)S(1)} %copy.45), kind=kLoop, calls=%fused_computation.34 | loop fusion | flops 1048576 | bytes 4718848 | tf_op jit(solution)/shard_map/add | solution.py:113
  163.2 1.9 fusion.22
  165.1 6.6 %abs_reduce_fusion = (f32[4,256,16]{1,2,0:T(8,128)S(1)}, f32[4,256,16,64]{1,3,2,0:T(8,128)}) fusion(bf16[4,256,16,64]{1,3,2,0:T(8,128)(2,1)S(1)} %copy.41, f32[16]{0:T(128)S(1)} %copy-done.11, f32[4,256,16,64]{1,3,2,0:T(8,128)S(1)} %fusion.22, f32[4,256,16]{1,2,0:T(8,128)S(1)} %get-tuple-element.13, f32[4,16,256]{2,1,0:T(8,128)S(1)} %get-tuple-element.15, ...), kind=kOutput, calls=%fused_computation.29 | convolution fusion | flops 565166080 | bytes 11796544 | tf_op jit(solution)/shard_map/chij,cjhp->cihp/dot_general | solution.py:75
  171.7 0.6 broadcast_multiply_fusion
  172.3 3.3 %all-to-all-start.4 = ((f32[4,256,16]{1,2,0:T(8,128)}), f32[4,256,16]{1,2,0:T(8,128)S(1)}, u32[]{:S(2)}, u32[]{:S(2)}) async-start(f32[4,256,16]{1,2,0:T(8,128)} %get-tuple-element.11), calls=%async_computation.4 | async-start | bytes 131072 | tf_op jit(solution)/shard_map/all_to_all | solution.py:20
  175.6 2.9 clamp_convert_fusion
  178.5 3.5 %all-to-all-done.4 = f32[4,256,16]{1,2,0:T(8,128)S(1)} async-done(((f32[4,256,16]{1,2,0:T(8,128)}), f32[4,256,16]{1,2,0:T(8,128)S(1)}, u32[]{:S(2)}, u32[]{:S(2)}) %all-to-all-start.4) | async-done | bytes 65568 | tf_op jit(solution)/shard_map/all_to_all | solution.py:20
  182.0 46.0 %all_to_all.25 = s16[4,256,1024]{1,2,0:T(8,128)(2,1)S(1)} all-to-all(s16[4,256,1024]{1,2,0:T(8,128)(2,1)S(1)} %bitcast.95), channel_id=1, replica_groups=mesh['dom'=8,'sx'=4,'sz'=4] {'sz'}, dimensions={0} | all-to-all | bytes 4194304 | tf_op jit(solution)/shard_map/all_to_all | solution.py:17
  228.0 2.6 bitcast_multiply_fusion
  230.6 5.7 %copy.53 = f32[256,4096]{1,0:T(8,128)} copy(f32[256,4096]{0,1:T(8,128)} %bitcast.90) | data formatting | bytes 8388608 | tf_op jit(solution)/shard_map/reshape | solution.py:126
  236.4 4.4 %multiply_reduce_fusion = f32[256]{0:T(256)S(1)} fusion(f32[256,4096]{1,0:T(8,128)} %copy.53, bf16[256,4224]{1,0:T(8,128)(2,1)} %bitcast.11), kind=kLoop, calls=%fused_computation.27 | loop fusion | flops 8388352 | bytes 6292480 | tf_op jit(solution)/shard_map/reduce_sum | solution.py:130
  240.8 24.0 %all-gather.3.cloned.1.call-done = bf16[1,4096,4096]{2,1,0:T(8,128)(2,1)} async-done(((bf16[1,4096,256]{2,1,0:T(8,128)(2,1)}), bf16[1,4096,4096]{2,1,0:T(8,128)(2,1)}) %all-gather.3.cloned.1.call-update) | async-done | bytes 33554448 | tf_op jit(solution)/shard_map/all_gather | solution.py:135
  264.8 18.8 %fusion.11 = bf16[1,256,4096]{2,1,0:T(8,128)(2,1)} fusion(bf16[1,4096,4096]{2,1,0:T(8,128)(2,1)} %all-gather.3.cloned.1.call-done, f32[4096]{0:T(1024)S(1)} %bitcast.104, f32[256]{0:T(256)S(1)} %add_rsqrt_fusion, f32[256,4096]{1,0:T(8,128)} %copy.53, bf16[256,4224]{1,0:T(8,128)(2,1)} %bitcast.11), kind=kOutput, calls=%fused_computation.17 | convolution fusion | flops 8600420352 | bytes 41960448 | tf_op jit(solution)/shard_map/dot_general | solution.py:133
  (57 shorter events, 1.2 us)
Async XLA Ops:
  6.5 19.4 %copy-start = (bf16[256,4096]{1,0:T(8,128)(2,1)S(1)}, bf16[256,4096]{1,0:T(8,128)(2,1)}, u32[]{:S(2)}) copy-start(bf16[256,4096]{1,0:T(8,128)(2,1)} %param.9) | copy-start | bytes 6291460
  6.5 258.3 %all-gather.3.cloned.1.call-start = ((), (), s32[]{:S(2)}) async-start(), calls=%async_computation.5 | async-start | bytes 35651584 | tf_op jit(solution)/shard_map/all_gather | solution.py:135
  21.4 32.6 %all-to-all-start.1 = ((bf16[8,32,4224]{2,1,0:T(8,128)(2,1)}), bf16[8,32,4224]{2,1,0:T(8,128)(2,1)}, u32[]{:S(2)}, u32[]{:S(2)}) async-start(bf16[8,32,4224]{2,1,0:T(8,128)(2,1)} %broadcast_select_fusion), calls=%async_computation.1 | async-start | bytes 4325376 | tf_op jit(solution)/shard_map/all_to_all | solution.py:57
  26.0 6.6 %copy-start.6 = (bf16[256,128]{1,0:T(8,128)(2,1)S(1)}, bf16[256,128]{1,0:T(8,128)(2,1)}, u32[]{:S(2)}) copy-start(bf16[256,128]{1,0:T(8,128)(2,1)} %param.12) | copy-start | bytes 196612
  26.0 6.5 %copy-start.7 = (bf16[256,128]{1,0:T(8,128)(2,1)S(1)}, bf16[256,128]{1,0:T(8,128)(2,1)}, u32[]{:S(2)}) copy-start(bf16[256,128]{1,0:T(8,128)(2,1)} %param.11) | copy-start | bytes 196612
  55.5 11.0 %all-to-all-start.2 = ((bf16[4,256,16]{1,2,0:T(8,128)(2,1)}), bf16[4,256,16]{1,2,0:T(8,128)(2,1)S(1)}, u32[]{:S(2)}, u32[]{:S(2)}) async-start(bf16[4,256,16]{1,2,0:T(8,128)(2,1)} %bitcast.13), calls=%async_computation.2 | async-start | bytes 65536 | tf_op jit(solution)/shard_map/all_to_all | solution.py:61
  62.1 9.4 %copy-start.10 = (f32[1,64]{1,0:T(1,128)S(1)}, f32[1,64]{1,0:T(1,128)}, u32[]{:S(2)}) copy-start(f32[1,64]{1,0:T(1,128)} %param.17) | copy-start | bytes 772
  66.5 41.1 %all-to-all-start = ((bf16[32,32,1280]{2,1,0:T(8,128)(2,1)}), bf16[32,32,1280]{2,1,0:T(8,128)(2,1)}, u32[]{:S(2)}, u32[]{:S(2)}) async-start(bf16[32,32,1280]{2,1,0:T(8,128)(2,1)} %bitcast.91), calls=%async_computation | async-start | bytes 5242880 | tf_op jit(solution)/shard_map/all_to_all | solution.py:52
  109.5 1.5 copy-start.3
  127.0 2.1 copy-start.2
  130.5 13.4 %collective-permute-start.1 = (f32[9,128]{1,0:T(8,128)}, f32[9,128]{1,0:T(8,128)S(1)}, u32[]{:S(2)}, u32[]{:S(2)}) collective-permute-start(f32[9,128]{1,0:T(8,128)} %bitcast.25), channel_id=1, source_target_pairs={{0,4},{4,8},{8,12},{1,5},{5,9},{9,13},{2,6},{6,10},{10,14},{3,7},{... | collective-permute-start | bytes 13832 | tf_op jit(solution)/shard_map/ppermute | solution.py:108
  133.9 13.3 %collective-permute-start.3 = (f32[9,128]{1,0:T(8,128)}, f32[9,128]{1,0:T(8,128)}, u32[]{:S(2)}, u32[]{:S(2)}) collective-permute-start(f32[9,128]{1,0:T(8,128)} %bitcast.25), channel_id=1, source_target_pairs={{0,8},{4,12},{1,9},{5,13},{2,10},{6,14},{3,11},{7,15},{16,24},{20,... | collective-permute-start | bytes 13832 | tf_op jit(solution)/shard_map/ppermute | solution.py:108
  139.2 19.4 %collective-permute-start = (s16[16,64,128]{2,1,0:T(8,128)(2,1)S(1)}, s16[16,64,128]{2,1,0:T(8,128)(2,1)S(1)}, u32[]{:S(2)}, u32[]{:S(2)}) collective-permute-start(s16[16,64,128]{2,1,0:T(8,128)(2,1)S(1)} %clamp_convert_fusion.1), channel_id=1, source_target_pairs={{0,4},{4,8},{8,12},{1,5},{5,9},{9,13},{2,6},{6,10},{10,14},{3,7},{... | collective-permute-start | bytes 786440 | tf_op jit(solution)/shard_map/ppermute | solution.py:107
  140.6 18.0 %collective-permute-start.2 = (s16[16,64,128]{2,1,0:T(8,128)(2,1)S(1)}, s16[16,64,128]{2,1,0:T(8,128)(2,1)S(1)}, u32[]{:S(2)}, u32[]{:S(2)}) collective-permute-start(s16[16,64,128]{2,1,0:T(8,128)(2,1)S(1)} %clamp_convert_fusion.1), channel_id=1, source_target_pairs={{0,8},{4,12},{1,9},{5,13},{2,10},{6,14},{3,11},{7,15},{16,24},{20,... | collective-permute-start | bytes 786440 | tf_op jit(solution)/shard_map/ppermute | solution.py:107
  141.9 16.7 %collective-permute-start.4 = (s16[16,64,128]{2,1,0:T(8,128)(2,1)S(1)}, s16[16,64,128]{2,1,0:T(8,128)(2,1)}, u32[]{:S(2)}, u32[]{:S(2)}) collective-permute-start(s16[16,64,128]{2,1,0:T(8,128)(2,1)S(1)} %clamp_convert_fusion.1), channel_id=1, source_target_pairs={{0,12},{1,13},{2,14},{3,15},{16,28},{17,29},{18,30},{19,31},{32,44... | collective-permute-start | bytes 786440 | tf_op jit(solution)/shard_map/ppermute | solution.py:107
  143.9 3.1 %copy-start.8 = (f32[9,128]{1,0:T(8,128)}, f32[9,128]{1,0:T(8,128)S(1)}, u32[]{:S(2)}) copy-start(f32[9,128]{1,0:T(8,128)S(1)} %collective-permute-done.1) | copy-start | bytes 13828
  143.9 13.3 %collective-permute-start.5 = (f32[9,128]{1,0:T(8,128)}, f32[9,128]{1,0:T(8,128)}, u32[]{:S(2)}, u32[]{:S(2)}) collective-permute-start(f32[9,128]{1,0:T(8,128)} %bitcast.25), channel_id=1, source_target_pairs={{0,12},{1,13},{2,14},{3,15},{16,28},{17,29},{18,30},{19,31},{32,44... | collective-permute-start | bytes 13832 | tf_op jit(solution)/shard_map/ppermute | solution.py:108
  163.2 1.9 copy-start.4
  163.2 1.9 copy-start.5
  163.2 1.9 copy-start.11
  172.3 9.7 %all-to-all-start.4 = ((f32[4,256,16]{1,2,0:T(8,128)}), f32[4,256,16]{1,2,0:T(8,128)S(1)}, u32[]{:S(2)}, u32[]{:S(2)}) async-start(f32[4,256,16]{1,2,0:T(8,128)} %get-tuple-element.11), calls=%async_computation.4 | async-start | bytes 131072 | tf_op jit(solution)/shard_map/all_to_all | solution.py:20
  236.4 28.4 %copy-start.9 = (f32[1,4096]{1,0:T(1,128)S(1)}, f32[1,4096]{1,0:T(1,128)}, u32[]{:S(2)}) copy-start(f32[1,4096]{1,0:T(1,128)} %param.16) | copy-start | bytes 49156
  264.8 18.8 %copy-start.1 = (bf16[256,4096]{1,0:T(8,128)(2,1)S(1)}, bf16[256,4096]{1,0:T(8,128)(2,1)}, u32[]{:S(2)}) copy-start(bf16[256,4096]{1,0:T(8,128)(2,1)} %param.9) | copy-start | bytes 6291460
Sparse Core Ops, SparseCore 0:
  9.4 255.2 all-gather.2

commit v13 on v12

--- a/solution.py
+++ b/solution.py
@@ -130,6 +130,7 @@
         * lax.rsqrt(jnp.mean(gated * gated, axis=-1, keepdims=True) + 1e-05)
         * norm_gain[0][None, :]
     ).astype(jnp.bfloat16)
+    normed = lax.optimization_barrier(normed)
     mixed = jnp.dot(
         normed,
         lax.all_gather(out_weight[0], SEQ, axis=1, tiled=True),

time: 292 us -> 290 us (level)
  waiting for transfers between devices: 89.4 us -> 84.1 us
  other arithmetic: 28.4 us -> 33.3 us
    all_gather x1, waiting for transfers between devices: 24 us -> 18.7 us  [per_device(): lax.all_gather(out_weight[0], SEQ, axis=1, tiled=True)]
    convert_element_type x0 -> x1, other arithmetic: none -> 4.67 us  [per_device(): normed = (gated * lax.rsqrt(jnp.mean(gated * gated, axis=-1, keepdims=Tru...]
  transfers between devices with their start and end apart: 11 -> 11, of which waited for: 6 -> 6; matrix products, arithmetic and copies ran while one was open for 30% -> 31% of each run, Pallas kernels for 0% -> 0%
where the time goes in v13:
time: 290 us; the launch traced here: 288 us
  waiting for transfers between devices  84.1 us (29%)
  blocking collectives  46.3 us (16%)
  local copies, waits for them, and re-layouts  45.3 us (16%)
  other arithmetic  33.3 us (11%)
  starting transfers between devices  33.2 us (11%)
  matrix products  32.4 us (11%)
  between operations  13.8 us (5%)
    all_to_all x1, blocking collectives, code16(): lax.all_to_all(coded.astype(jnp.int16).reshape(*lead, -1), axis_name, spl...  46.3 us
    all_to_all x1, waiting for transfers between devices, per_device(): lax.all_to_all(routed, ('dom', 'sz'), split_axis=0, concat_axis=0, tiled=...  31.3 us
    all_gather x1, waiting for transfers between devices, per_device(): lax.all_gather(out_weight[0], SEQ, axis=1, tiled=True)  18.7 us
    all_to_all x1, waiting for transfers between devices, per_device(): lax.all_to_all(arrange(zl), 'dom', split_axis=0, concat_axis=0, tiled=True)  18.2 us
    dot_general x1, matrix products, per_device(): jnp.dot(normed, lax.all_gather(out_weight[0], SEQ, axis=1, tiled=True), p...  16.7 us
    gather x4, local copies, waits for them, and re-layouts, arrange(): jnp.take(value_rows.reshape(groups, seg_rows, value_rows.shape[-1]), orde...  10.8 us
    ppermute x3, starting transfers between devices, per_device(): got = lax.ppermute(side, 'sx', route).reshape(-1)  10.4 us
    ppermute x3, waiting for transfers between devices, per_device(): got = lax.ppermute(side, 'sx', route).reshape(-1)  9.29 us
  transfers between devices with their start and end apart: 11, of which 6 were waited for; matrix products, arithmetic and copies ran while one was open for 31% of the time, Pallas kernels for 0%

profile of v13, /device:TPU:0, one launch (start us, length us, event | category | flops | bytes accessed | tf_op | source)
XLA Modules:
  0.0 288.4 jit_solution(17202571141753803287)
XLA Ops:
  6.5 0.7 all-gather.3.cloned.1.call-update
  7.3 0.9 copy.35
  8.1 1.6 sort.17
  9.8 4.5 %concatenate.14 = bf16[256,4224]{1,0:T(8,128)(2,1)} concatenate(bf16[256,4096]{1,0:T(8,128)(2,1)} %param.10, bf16[256,64]{1,0:T(8,128)(2,1)S(1)} %copy.35, bf16[256,64]{1,0:T(8,128)(2,1)S(1)} %broadcast_in_dim.104), dimensions={1} | concatenate | bytes 4325376 | tf_op jit(solution)/shard_map/concatenate | solution.py:56
  14.3 3.8 %gather_fusion.2 = bf16[8,32,4224]{2,1,0:T(8,128)(2,1)} fusion(bf16[8,32,4224]{2,1,0:T(8,128)(2,1)} %bitcast.95, s32[1024]{0:T(1024)S(1)} %pad_clamp_fusion), kind=kCustom, calls=%fused_computation.2 | custom fusion | bytes 4325408 | tf_op jit(solution)/shard_map/jit(_take)/gather | solution.py:41
  18.1 3.3 %broadcast_select_fusion = bf16[8,32,4224]{2,1,0:T(8,128)(2,1)} fusion(bf16[8,32,4224]{2,1,0:T(8,128)(2,1)} %gather_fusion.2, pred[8]{0:T(512)(128)(4,1)S(1)} %compare_and_fusion), kind=kLoop, calls=%fused_computation.31 | loop fusion | flops 1081344 | bytes 4325384 | tf_op jit(solution)/shard_map/jit(_take)/select_n | solution.py:41
  21.4 4.6 %all-to-all-start.1 = ((bf16[8,32,4224]{2,1,0:T(8,128)(2,1)}), bf16[8,32,4224]{2,1,0:T(8,128)(2,1)}, u32[]{:S(2)}, u32[]{:S(2)}) async-start(bf16[8,32,4224]{2,1,0:T(8,128)(2,1)} %broadcast_select_fusion), calls=%async_computation.1 | async-start | bytes 4325376 | tf_op jit(solution)/shard_map/all_to_all | solution.py:57
  26.0 2.0 gather_fusion
  28.0 4.5 %gather.15 = bf16[8,32,4,1024]{3,2,1,0:T(4,128)(2,1)} reshape(bf16[8,32,4096]{2,1,0:T(8,128)(2,1)} %gather_fusion) | data formatting | bytes 4194304 | tf_op jit(solution)/shard_map/jit(_take)/gather | solution.py:41
  32.5 0.6 gather_fusion.1
  33.2 2.6 select_bitcast_fusion
  35.7 18.2 %all-to-all-done.1 = bf16[8,32,4224]{2,1,0:T(8,128)(2,1)} async-done(((bf16[8,32,4224]{2,1,0:T(8,128)(2,1)}), bf16[8,32,4224]{2,1,0:T(8,128)(2,1)}, u32[]{:S(2)}, u32[]{:S(2)}) %all-to-all-start.1) | async-done | bytes 2162720 | tf_op jit(solution)/shard_map/all_to_all | solution.py:57
  53.9 0.8 slice.72
  54.8 0.7 copy.36
  55.5 5.3 %all-to-all-start.2 = ((bf16[4,256,16]{1,2,0:T(8,128)(2,1)}), bf16[4,256,16]{1,2,0:T(8,128)(2,1)S(1)}, u32[]{:S(2)}, u32[]{:S(2)}) async-start(bf16[4,256,16]{1,2,0:T(8,128)(2,1)} %bitcast.13), calls=%async_computation.2 | async-start | bytes 65536 | tf_op jit(solution)/shard_map/all_to_all | solution.py:61
  60.9 1.2 pad_maximum_fusion
  62.1 2.0 copy.32
  64.1 2.3 all-to-all-done.2
  66.5 5.0 %all-to-all-start = ((bf16[32,32,1280]{2,1,0:T(8,128)(2,1)}), bf16[32,32,1280]{2,1,0:T(8,128)(2,1)}, u32[]{:S(2)}, u32[]{:S(2)}) async-start(bf16[32,32,1280]{2,1,0:T(8,128)(2,1)} %bitcast.92), calls=%async_computation | async-start | bytes 5242880 | tf_op jit(solution)/shard_map/all_to_all | solution.py:52
  71.5 0.6 dynamic-slice_bitcast_fusion
  72.2 0.7 iota_compare_fusion
  72.8 2.3 reduce-window.6
  75.4 0.2 slice_reduce_fusion
  75.7 0.3 fusion.28
  76.3 31.3 %all-to-all-done = bf16[32,32,1280]{2,1,0:T(8,128)(2,1)} async-done(((bf16[32,32,1280]{2,1,0:T(8,128)(2,1)}), bf16[32,32,1280]{2,1,0:T(8,128)(2,1)}, u32[]{:S(2)}, u32[]{:S(2)}) %all-to-all-start) | async-done | bytes 2621472 | tf_op jit(solution)/shard_map/all_to_all | solution.py:52
  107.6 1.9 copy.33
  109.5 1.4 copy-done.4
  111.0 0.3 slice.69
  111.3 4.0 %reshape.273 = bf16[4,256,16,64]{3,2,1,0:T(8,128)(2,1)} reshape(bf16[1024,1024]{1,0:T(8,128)(2,1)S(1)} %slice.69) | data formatting | bytes 4194304 | tf_op jit(solution)/shard_map/reshape | solution.py:64
  115.3 4.8 %copy.41 = bf16[4,256,16,64]{1,3,2,0:T(8,128)(2,1)S(1)} copy(bf16[4,256,16,64]{3,2,1,0:T(8,128)(2,1)} %reshape.273) | data formatting | bytes 4194304 | tf_op jit(solution)/shard_map/reshape | solution.py:64
  120.2 1.1 fusion.38
  121.2 0.7 fusion.20
  122.0 5.0 %convolution_bitcast_fusion = f32[5,16,64,128]{3,0,2,1:T(8,128)S(1)} fusion(f32[16,5,4,1]{1,2,3,0:T(4,128)S(1)} %copy.49, f32[4,16,64,128]{3,2,1,0:T(8,128)S(1)} %fusion.20), kind=kOutput, calls=%fused_computation.32 | convolution fusion | flops 31457280 | bytes 4719872 | tf_op jit(solution)/shard_map/hkj,jhpn->khpn/dot_general | solution.py:90
  127.0 2.0 copy-done.3
  129.0 0.6 slice.77
  129.6 0.2 abs_reduce_fusion.1
  129.9 0.7 concatenate.15
  130.5 3.3 %collective-permute-start.1 = (f32[9,128]{1,0:T(8,128)}, f32[9,128]{1,0:T(8,128)S(1)}, u32[]{:S(2)}, u32[]{:S(2)}) collective-permute-start(f32[9,128]{1,0:T(8,128)} %bitcast.25), channel_id=1, source_target_pairs={{0,4},{4,8},{8,12},{1,5},{5,9},{9,13},{2,6},{6,10},{10,14},{3,7},{... | collective-permute-start | bytes 13832 | tf_op jit(solution)/shard_map/ppermute | solution.py:108
  133.8 5.2 %collective-permute-start.3 = (f32[9,128]{1,0:T(8,128)}, f32[9,128]{1,0:T(8,128)}, u32[]{:S(2)}, u32[]{:S(2)}) collective-permute-start(f32[9,128]{1,0:T(8,128)} %bitcast.25), channel_id=1, source_target_pairs={{0,8},{4,12},{1,9},{5,13},{2,10},{6,14},{3,11},{7,15},{16,24},{20,... | collective-permute-start | bytes 13832 | tf_op jit(solution)/shard_map/ppermute | solution.py:108
  139.0 0.2 clamp_convert_fusion.1
  139.2 1.3 collective-permute-start
  140.6 1.3 collective-permute-start.2
  141.9 2.0 collective-permute-start.4
  143.9 1.9 collective-permute-start.5
  145.8 1.3 fusion.39
  147.1 0.7 slice.80
  147.9 9.3 %collective-permute-done.5 = f32[9,128]{1,0:T(8,128)} collective-permute-done((f32[9,128]{1,0:T(8,128)}, f32[9,128]{1,0:T(8,128)}, u32[]{:S(2)}, u32[]{:S(2)}) %collective-permute-start.5) | collective-permute-done | bytes 4640 | tf_op jit(solution)/shard_map/ppermute | solution.py:108
  157.2 0.7 slice.82
  157.9 0.7 slice_exponential_fusion
  158.6 1.5 multiply_add_fusion
  160.1 3.1 %slice_add_fusion = f32[4,16,64,128]{3,0,2,1:T(4,128)S(1)} fusion(f32[5,16,64,128]{3,0,2,1:T(8,128)} %copy-done.3, f32[16,64,128]{2,1,0:T(8,128)S(1)} %multiply_add_fusion, f32[4,16]{0,1:T(8,128)S(1)} %copy.45), kind=kLoop, calls=%fused_computation.34 | loop fusion | flops 1048576 | bytes 4718848 | tf_op jit(solution)/shard_map/add | solution.py:113
  163.2 1.9 fusion.22
  165.2 6.6 %abs_reduce_fusion = (f32[4,256,16]{1,2,0:T(8,128)S(1)}, f32[4,256,16,64]{1,3,2,0:T(8,128)}) fusion(bf16[4,256,16,64]{1,3,2,0:T(8,128)(2,1)S(1)} %copy.41, f32[16]{0:T(128)S(1)} %copy-done.12, f32[4,256,16,64]{1,3,2,0:T(8,128)S(1)} %fusion.22, f32[4,256,16]{1,2,0:T(8,128)S(1)} %get-tuple-element.13, f32[4,16,256]{2,1,0:T(8,128)S(1)} %get-tuple-element.15, ...), kind=kOutput, calls=%fused_computation.29 | convolution fusion | flops 565166080 | bytes 11796544 | tf_op jit(solution)/shard_map/chij,cjhp->cihp/dot_general | solution.py:75
  171.7 0.6 broadcast_multiply_fusion
  172.4 3.3 %all-to-all-start.4 = ((f32[4,256,16]{1,2,0:T(8,128)}), f32[4,256,16]{1,2,0:T(8,128)S(1)}, u32[]{:S(2)}, u32[]{:S(2)}) async-start(f32[4,256,16]{1,2,0:T(8,128)} %get-tuple-element.11), calls=%async_computation.4 | async-start | bytes 131072 | tf_op jit(solution)/shard_map/all_to_all | solution.py:20
  175.7 2.9 clamp_convert_fusion
  178.5 3.5 %all-to-all-done.4 = f32[4,256,16]{1,2,0:T(8,128)S(1)} async-done(((f32[4,256,16]{1,2,0:T(8,128)}), f32[4,256,16]{1,2,0:T(8,128)S(1)}, u32[]{:S(2)}, u32[]{:S(2)}) %all-to-all-start.4) | async-done | bytes 65568 | tf_op jit(solution)/shard_map/all_to_all | solution.py:20
  182.0 46.3 %all_to_all.25 = s16[4,256,1024]{1,2,0:T(8,128)(2,1)S(1)} all-to-all(s16[4,256,1024]{1,2,0:T(8,128)(2,1)S(1)} %bitcast.96), channel_id=1, replica_groups=mesh['dom'=8,'sx'=4,'sz'=4] {'sz'}, dimensions={0} | all-to-all | bytes 4194304 | tf_op jit(solution)/shard_map/all_to_all | solution.py:17
  228.4 2.7 bitcast_multiply_fusion
  231.1 5.7 %copy.53 = f32[256,4096]{1,0:T(8,128)} copy(f32[256,4096]{0,1:T(8,128)} %bitcast.91) | data formatting | bytes 8388608 | tf_op jit(solution)/shard_map/reshape | solution.py:126
  236.8 4.5 %multiply_reduce_fusion = f32[256]{0:T(256)S(1)} fusion(f32[256,4096]{1,0:T(8,128)} %copy.53, bf16[256,4224]{1,0:T(8,128)(2,1)} %bitcast.11), kind=kLoop, calls=%fused_computation.27 | loop fusion | flops 8388352 | bytes 6292480 | tf_op jit(solution)/shard_map/reduce_sum | solution.py:130
  241.4 4.7 %multiply_convert_fusion.2 = bf16[256,4096]{1,0:T(8,128)(2,1)} fusion(f32[4096]{0:T(1024)S(1)} %bitcast.104, f32[256]{0:T(256)S(1)} %add_rsqrt_fusion, f32[256,4096]{1,0:T(8,128)S(1)} %copy-done.2, bf16[256,4224]{1,0:T(8,128)(2,1)} %bitcast.11), kind=kLoop, calls=%fused_computation.26 | loop fusion | flops 9437184 | bytes 8406016 | tf_op jit(solution)/shard_map/convert_element_type | solution.py:132
  246.1 18.7 %all-gather.3.cloned.1.call-done = bf16[1,4096,4096]{2,1,0:T(8,128)(2,1)} async-done(((bf16[1,4096,256]{2,1,0:T(8,128)(2,1)}), bf16[1,4096,4096]{2,1,0:T(8,128)(2,1)}) %all-gather.3.cloned.1.call-update) | async-done | bytes 33554448 | tf_op jit(solution)/shard_map/all_gather | solution.py:136
  264.8 16.7 %fusion.11 = bf16[1,256,4096]{2,1,0:T(8,128)(2,1)} fusion(bf16[256,4096]{1,0:T(8,128)(2,1)} %multiply_convert_fusion.2, bf16[1,4096,4096]{2,1,0:T(8,128)(2,1)} %all-gather.3.cloned.1.call-done), kind=kOutput, calls=%fused_computation.17 | convolution fusion | flops 8590983168 | bytes 37748736 | tf_op jit(solution)/shard_map/dot_general | solution.py:134
  (60 shorter events, 1.3 us)
Async XLA Ops:
  6.5 19.4 %copy-start = (bf16[256,4096]{1,0:T(8,128)(2,1)S(1)}, bf16[256,4096]{1,0:T(8,128)(2,1)}, u32[]{:S(2)}) copy-start(bf16[256,4096]{1,0:T(8,128)(2,1)} %param.9) | copy-start | bytes 6291460
  6.5 258.2 %all-gather.3.cloned.1.call-start = ((), (), s32[]{:S(2)}) async-start(), calls=%async_computation.5 | async-start | bytes 35651584 | tf_op jit(solution)/shard_map/all_gather | solution.py:136
  21.4 32.6 %all-to-all-start.1 = ((bf16[8,32,4224]{2,1,0:T(8,128)(2,1)}), bf16[8,32,4224]{2,1,0:T(8,128)(2,1)}, u32[]{:S(2)}, u32[]{:S(2)}) async-start(bf16[8,32,4224]{2,1,0:T(8,128)(2,1)} %broadcast_select_fusion), calls=%async_computation.1 | async-start | bytes 4325376 | tf_op jit(solution)/shard_map/all_to_all | solution.py:57
  25.9 6.5 %copy-start.7 = (bf16[256,128]{1,0:T(8,128)(2,1)S(1)}, bf16[256,128]{1,0:T(8,128)(2,1)}, u32[]{:S(2)}) copy-start(bf16[256,128]{1,0:T(8,128)(2,1)} %param.12) | copy-start | bytes 196612
  26.0 6.5 %copy-start.8 = (bf16[256,128]{1,0:T(8,128)(2,1)S(1)}, bf16[256,128]{1,0:T(8,128)(2,1)}, u32[]{:S(2)}) copy-start(bf16[256,128]{1,0:T(8,128)(2,1)} %param.11) | copy-start | bytes 196612
  55.5 11.0 %all-to-all-start.2 = ((bf16[4,256,16]{1,2,0:T(8,128)(2,1)}), bf16[4,256,16]{1,2,0:T(8,128)(2,1)S(1)}, u32[]{:S(2)}, u32[]{:S(2)}) async-start(bf16[4,256,16]{1,2,0:T(8,128)(2,1)} %bitcast.13), calls=%async_computation.2 | async-start | bytes 65536 | tf_op jit(solution)/shard_map/all_to_all | solution.py:61
  62.1 9.4 %copy-start.11 = (f32[1,64]{1,0:T(1,128)S(1)}, f32[1,64]{1,0:T(1,128)}, u32[]{:S(2)}) copy-start(f32[1,64]{1,0:T(1,128)} %param.17) | copy-start | bytes 772
  66.5 41.1 %all-to-all-start = ((bf16[32,32,1280]{2,1,0:T(8,128)(2,1)}), bf16[32,32,1280]{2,1,0:T(8,128)(2,1)}, u32[]{:S(2)}, u32[]{:S(2)}) async-start(bf16[32,32,1280]{2,1,0:T(8,128)(2,1)} %bitcast.92), calls=%async_computation | async-start | bytes 5242880 | tf_op jit(solution)/shard_map/all_to_all | solution.py:52
  109.5 1.5 copy-start.4
  127.0 2.0 copy-start.3
  130.5 13.4 %collective-permute-start.1 = (f32[9,128]{1,0:T(8,128)}, f32[9,128]{1,0:T(8,128)S(1)}, u32[]{:S(2)}, u32[]{:S(2)}) collective-permute-start(f32[9,128]{1,0:T(8,128)} %bitcast.25), channel_id=1, source_target_pairs={{0,4},{4,8},{8,12},{1,5},{5,9},{9,13},{2,6},{6,10},{10,14},{3,7},{... | collective-permute-start | bytes 13832 | tf_op jit(solution)/shard_map/ppermute | solution.py:108
  133.8 13.3 %collective-permute-start.3 = (f32[9,128]{1,0:T(8,128)}, f32[9,128]{1,0:T(8,128)}, u32[]{:S(2)}, u32[]{:S(2)}) collective-permute-start(f32[9,128]{1,0:T(8,128)} %bitcast.25), channel_id=1, source_target_pairs={{0,8},{4,12},{1,9},{5,13},{2,10},{6,14},{3,11},{7,15},{16,24},{20,... | collective-permute-start | bytes 13832 | tf_op jit(solution)/shard_map/ppermute | solution.py:108
  139.2 19.4 %collective-permute-start = (s16[16,64,128]{2,1,0:T(8,128)(2,1)S(1)}, s16[16,64,128]{2,1,0:T(8,128)(2,1)S(1)}, u32[]{:S(2)}, u32[]{:S(2)}) collective-permute-start(s16[16,64,128]{2,1,0:T(8,128)(2,1)S(1)} %clamp_convert_fusion.1), channel_id=1, source_target_pairs={{0,4},{4,8},{8,12},{1,5},{5,9},{9,13},{2,6},{6,10},{10,14},{3,7},{... | collective-permute-start | bytes 786440 | tf_op jit(solution)/shard_map/ppermute | solution.py:107
  140.6 18.1 %collective-permute-start.2 = (s16[16,64,128]{2,1,0:T(8,128)(2,1)S(1)}, s16[16,64,128]{2,1,0:T(8,128)(2,1)S(1)}, u32[]{:S(2)}, u32[]{:S(2)}) collective-permute-start(s16[16,64,128]{2,1,0:T(8,128)(2,1)S(1)} %clamp_convert_fusion.1), channel_id=1, source_target_pairs={{0,8},{4,12},{1,9},{5,13},{2,10},{6,14},{3,11},{7,15},{16,24},{20,... | collective-permute-start | bytes 786440 | tf_op jit(solution)/shard_map/ppermute | solution.py:107
  141.9 16.7 %collective-permute-start.4 = (s16[16,64,128]{2,1,0:T(8,128)(2,1)S(1)}, s16[16,64,128]{2,1,0:T(8,128)(2,1)}, u32[]{:S(2)}, u32[]{:S(2)}) collective-permute-start(s16[16,64,128]{2,1,0:T(8,128)(2,1)S(1)} %clamp_convert_fusion.1), channel_id=1, source_target_pairs={{0,12},{1,13},{2,14},{3,15},{16,28},{17,29},{18,30},{19,31},{32,44... | collective-permute-start | bytes 786440 | tf_op jit(solution)/shard_map/ppermute | solution.py:107
  143.9 3.1 %copy-start.10 = (f32[9,128]{1,0:T(8,128)}, f32[9,128]{1,0:T(8,128)S(1)}, u32[]{:S(2)}) copy-start(f32[9,128]{1,0:T(8,128)S(1)} %collective-permute-done.1) | copy-start | bytes 13828
  143.9 13.3 %collective-permute-start.5 = (f32[9,128]{1,0:T(8,128)}, f32[9,128]{1,0:T(8,128)}, u32[]{:S(2)}, u32[]{:S(2)}) collective-permute-start(f32[9,128]{1,0:T(8,128)} %bitcast.25), channel_id=1, source_target_pairs={{0,12},{1,13},{2,14},{3,15},{16,28},{17,29},{18,30},{19,31},{32,44... | collective-permute-start | bytes 13832 | tf_op jit(solution)/shard_map/ppermute | solution.py:108
  163.2 1.9 copy-start.5
  163.2 1.9 copy-start.6
  163.2 1.9 copy-start.12
  172.4 9.7 %all-to-all-start.4 = ((f32[4,256,16]{1,2,0:T(8,128)}), f32[4,256,16]{1,2,0:T(8,128)S(1)}, u32[]{:S(2)}, u32[]{:S(2)}) async-start(f32[4,256,16]{1,2,0:T(8,128)} %get-tuple-element.11), calls=%async_computation.4 | async-start | bytes 131072 | tf_op jit(solution)/shard_map/all_to_all | solution.py:20
  236.8 4.5 %copy-start.2 = (f32[256,4096]{1,0:T(8,128)S(1)}, f32[256,4096]{1,0:T(8,128)}, u32[]{:S(2)}) copy-start(f32[256,4096]{1,0:T(8,128)} %copy.53) | copy-start | bytes 12582916
  236.8 4.5 %copy-start.9 = (f32[1,4096]{1,0:T(1,128)S(1)}, f32[1,4096]{1,0:T(1,128)}, u32[]{:S(2)}) copy-start(f32[1,4096]{1,0:T(1,128)} %param.16) | copy-start | bytes 49156
  264.8 16.8 %copy-start.1 = (bf16[256,4096]{1,0:T(8,128)(2,1)S(1)}, bf16[256,4096]{1,0:T(8,128)(2,1)}, u32[]{:S(2)}) copy-start(bf16[256,4096]{1,0:T(8,128)(2,1)} %param.9) | copy-start | bytes 6291460
Sparse Core Ops, SparseCore 0:
  9.4 255.2 all-gather.2
